TPU v7x, 512 devices: a whole 4x4x16 slice. The times are simulated.
512 devices in a mesh: row: 64 (over x, z), col: 8 (over y, core).
Axes of the slice: x: 4, y: 4, z: 16, core: 2. Of those that a mesh axis runs over, the one named last changes fastest.
Arguments:
- current: bfloat16 [2, 256, 32, 4, 128], P(None, 'row', 'col'), may hold values from -6 to 6
- probe: bfloat16 [2, 256, 32, 4, 128], P(None, 'row', 'col'), may hold values from -6 to 6
- near_list: int32 [256, 32, 2], P('row', 'col'), may hold values from 0 to 9, as said below
- near_blocks: bfloat16 [2, 256, 32, 2, 128, 128], P(None, 'row', 'col'), may hold values from -0.25 to 0.25
- radiation: bfloat16 [2, 128, 128], replicated, may hold values from -0.375 to 0.375
- reception: bfloat16 [2, 128, 128], replicated, may hold values from -0.375 to 0.375
- interp: float32 [256, 128], replicated, may hold values from -0.5 to 0.5
- phase: float32 [16, 256], replicated, may hold values from -3.140625 to 3.140625
- leaf_table: float32 [2, 15, 15, 128], replicated, may hold values from -0.36 to 0.36
- coarse_table: bfloat16 [2, 127, 15, 256], replicated, may hold values from -0.023925781 to 0.023925781
Outputs:
- forward_out: float32 [2, 256, 32, 4, 128], P(None, 'row', 'col')
- adjoint_out: float32 [2, 256, 32, 4, 128], P(None, 'row', 'col')
Inputs may be any that keep to these rules, and one draw needn't show every extreme that they name: `near_list`: the 2 slots of a box hold distinct codes; only slots after the first may be empty (code 9).
All inputs are finite; a program needn't handle non-finite values.
Results may differ from a plain program's by a relative error of at most 0.0027.
Values may be sent and summed in bfloat16 or wider, within the bound.
No kernel may reach another device: no remote copies, remote signals or barrier semaphores. Data moves between devices by JAX's collectives and lax.ppermute only.
A program may use at most 128 MiB of HBM per device.

v0:
```python
import jax
import jax.numpy as jnp
from jax import lax
from jax.sharding import PartitionSpec as P

HIGH = lax.Precision.HIGHEST


def with_halo(cells, sides, width):
    for axis, dim in sides:
        count = lax.axis_size(axis)
        ends = count - 1
        head = lax.slice_in_dim(cells, 0, width, axis=dim)
        tail = lax.slice_in_dim(cells, cells.shape[dim] - width, cells.shape[dim], axis=dim)
        cells = jnp.concatenate(
            [
                lax.ppermute(tail, axis, [(i, (i + 1) % count) for i in range(ends)]),
                cells,
                lax.ppermute(head, axis, [((i + 1) % count, i) for i in range(ends)]),
            ],
            axis=dim,
        )
    return cells


def from_behind(block, axis, distance):
    devices = range(lax.axis_size(axis))
    route = [(i - distance, i) for i in devices if i - distance in devices]
    return lax.ppermute(block, axis, route)


def complex_mul(left_re, left_im, right_re, right_im):
    return (left_re * right_re - left_im * right_im, left_re * right_im + left_im * right_re)


def conj_flip(table, axes):
    flipped = jnp.flip(table, axes)
    return jnp.stack([flipped[0], -flipped[1]])


def product(form, left, right):
    return jnp.einsum(form, left, right, preferred_element_type=jnp.float32)


def near_field(current, probe, near_list, near_blocks):
    box_side = current.shape[1]
    one_hot = (near_list[..., None] == jnp.arange(9)).astype(jnp.bfloat16)
    blocks_re = near_blocks[0]
    blocks_im = near_blocks[1]
    padded = with_halo(current, (("row", 1), ("col", 2)), 1)
    shifted = jnp.stack(
        [
            padded[
                :,
                offset_code // 3 : offset_code // 3 + box_side,
                offset_code % 3 : offset_code % 3 + box_side,
            ]
            for offset_code in range(9)
        ]
    )
    picked = product("rcko,oxrcmp->xkrcmp", one_hot, shifted).astype(jnp.bfloat16)
    fwd_re = product("rckpq,krcmq->rcmp", blocks_re, picked[0]) - product(
        "rckpq,krcmq->rcmp", blocks_im, picked[1]
    )
    fwd_im = product("rckpq,krcmq->rcmp", blocks_re, picked[1]) + product(
        "rckpq,krcmq->rcmp", blocks_im, picked[0]
    )
    near_fwd = jnp.stack([fwd_re, fwd_im])
    back_re = product("rckpq,rcmp->krcmq", blocks_re, probe[0]) + product(
        "rckpq,rcmp->krcmq", blocks_im, probe[1]
    )
    back_im = product("rckpq,rcmp->krcmq", blocks_re, probe[1]) - product(
        "rckpq,rcmp->krcmq", blocks_im, probe[0]
    )
    contrib = jnp.stack([back_re, back_im])
    placed_all = jnp.einsum(
        "rcko,xkrcmp->oxrcmp", one_hot.astype(jnp.float32), contrib, precision=HIGH
    )
    placed = jnp.zeros((2, box_side + 2, box_side + 2) + contrib.shape[4:], jnp.float32)
    for offset_code in range(9):
        placed = placed.at[
            :,
            offset_code // 3 : offset_code // 3 + box_side,
            offset_code % 3 : offset_code % 3 + box_side,
        ].add(placed_all[offset_code])
    for step_dir, send_row, keep_row in ((1, box_side + 1, 1), (-1, 0, box_side)):
        arrived = from_behind(placed[:, send_row], "row", step_dir)
        placed = placed.at[:, keep_row].add(arrived)
    for step_dir, send_col, keep_col in ((1, box_side + 1, 1), (-1, 0, box_side)):
        arrived = from_behind(placed[:, 1 : box_side + 1, send_col], "col", step_dir)
        placed = placed.at[:, 1 : box_side + 1, keep_col].add(arrived)
    return (near_fwd, placed[:, 1 : box_side + 1, 1 : box_side + 1])


def gather_ordered(block, axis):
    count = lax.axis_size(axis)
    index = lax.axis_index(axis)
    held = block[None]
    step = 1
    while step < count:
        other = lax.ppermute(held, axis, [(i, i ^ step) for i in range(count)])
        lower = (index & step) == 0
        held = jnp.where(
            lower, jnp.concatenate([held, other], 0), jnp.concatenate([other, held], 0)
        )
        step *= 2
    return held


def scatter_sum(parts, axis):
    count = lax.axis_size(axis)
    index = lax.axis_index(axis)
    held = parts
    step = count // 2
    while step >= 1:
        half = held.shape[0] // 2
        upper = (index & step) != 0
        send = jnp.where(upper, held[:half], held[half:])
        keep = jnp.where(upper, held[half:], held[:half])
        held = keep + lax.ppermute(send, axis, [(i, i ^ step) for i in range(count)])
        step //= 2
    return held[0]


def coarse_exchange(top_b, coarse_tab):
    row_count = lax.axis_size("row")
    col_count = lax.axis_size("col")
    row_idx = lax.axis_index("row")
    col_idx = lax.axis_index("col")
    sources = gather_ordered(top_b, "row").astype(jnp.float32)
    zero = jnp.zeros((), jnp.int32)
    fwd_tab = coarse_tab[0]
    fwd = lax.dynamic_slice(
        fwd_tab,
        (zero, row_idx, col_count - 1 - col_idx, zero),
        (2, row_count, col_count, fwd_tab.shape[-1]),
    )
    fwd = jnp.flip(fwd, 1)
    adj = lax.dynamic_slice(
        fwd_tab,
        (zero, row_count - 1 - row_idx, col_idx, zero),
        (2, row_count, col_count, fwd_tab.shape[-1]),
    )
    adj = jnp.flip(adj, 2)
    adj = jnp.stack([adj[0], -adj[1]])
    coeff = jnp.stack([fwd, adj]).astype(jnp.float32)
    src_rows = jnp.arange(row_count)
    dst_cols = jnp.arange(col_count)
    distant = (jnp.abs(row_idx - src_rows)[:, None] > 1) | (jnp.abs(dst_cols - col_idx)[None, :] > 1)
    weight = distant.astype(jnp.float32)[None, :, :, None]
    coef_re = coeff[:, 0] * weight
    coef_im = coeff[:, 1] * weight
    val_re = jnp.moveaxis(sources[:, :, 0], 0, 1)[:, :, None]
    val_im = jnp.moveaxis(sources[:, :, 1], 0, 1)[:, :, None]
    c_re = coef_re[:, :, :, None]
    c_im = coef_im[:, :, :, None]
    got_re = (c_re * val_re - c_im * val_im).sum(1)
    got_im = (c_re * val_im + c_im * val_re).sum(1)
    parts = jnp.moveaxis(jnp.stack([got_re, got_im], 1), 2, 0)
    return scatter_sum(parts, "col")


def far_field(vectors, rad_tab, rcv_tab, leaf_tab, coarse_tab, interp, phase):
    box_side = vectors.shape[2]
    span = 3 * box_side
    reach = 2 * box_side - 1
    out_re = product("srcmp,sqp->srcmq", vectors[:, 0], rad_tab[:, 0]) - product(
        "srcmp,sqp->srcmq", vectors[:, 1], rad_tab[:, 1]
    )
    out_im = product("srcmp,sqp->srcmq", vectors[:, 0], rad_tab[:, 1]) + product(
        "srcmp,sqp->srcmq", vectors[:, 1], rad_tab[:, 0]
    )
    leaf_out = jnp.stack([out_re, out_im], 1)
    window = with_halo(leaf_out, (("row", 2), ("col", 3)), box_side)
    offsets = jnp.arange(2 * reach + 1) - reach
    near_offset = jnp.abs(offsets) <= 1
    keep = 1.0 - (near_offset[:, None] & near_offset[None, :]).astype(jnp.float32)
    masked = leaf_tab * keep[None, None, :, :, None]
    rows_in = []
    for row_pos in range(box_side):
        cols_in = []
        for col_pos in range(box_side):
            row_first = box_side - 1 - row_pos
            col_first = box_side - 1 - col_pos
            coeffs = masked[:, :, row_first : row_first + span, col_first : col_first + span]
            part_re, part_im = complex_mul(
                coeffs[:, 0, :, :, None], coeffs[:, 1, :, :, None], window[:, 0], window[:, 1]
            )
            cols_in.append(jnp.stack([part_re.sum((1, 2)), part_im.sum((1, 2))], 1))
        rows_in.append(jnp.stack(cols_in, 2))
    leaf_in = jnp.stack(rows_in, 2)
    interpolated = jnp.einsum("kq,sxrcmq->sxrcmk", interp, leaf_out, precision=HIGH)
    angles = phase.reshape(box_side, box_side, -1)
    cos_ph = jnp.cos(angles)[:, :, None, :]
    sin_ph = jnp.sin(angles)[:, :, None, :]
    top_re = (cos_ph * interpolated[:, 0] - sin_ph * interpolated[:, 1]).sum((1, 2))
    top_im = (cos_ph * interpolated[:, 1] + sin_ph * interpolated[:, 0]).sum((1, 2))
    top_b = jnp.stack([top_re, top_im], 1).astype(jnp.bfloat16)
    coarse_in = coarse_exchange(top_b, coarse_tab)
    in_re = coarse_in[:, 0][:, None, None]
    in_im = coarse_in[:, 1][:, None, None]
    back_re = cos_ph * in_re + sin_ph * in_im
    back_im = cos_ph * in_im - sin_ph * in_re
    spread = jnp.einsum(
        "kq,sxrcmk->sxrcmq", interp, jnp.stack([back_re, back_im], 1), precision=HIGH
    )
    incoming = (leaf_in + spread).astype(jnp.bfloat16)
    res_re = product("srcmq,spq->srcmp", incoming[:, 0], rcv_tab[:, 0]) - product(
        "srcmq,spq->srcmp", incoming[:, 1], rcv_tab[:, 1]
    )
    res_im = product("srcmq,spq->srcmp", incoming[:, 0], rcv_tab[:, 1]) + product(
        "srcmq,spq->srcmp", incoming[:, 1], rcv_tab[:, 0]
    )
    return jnp.stack([res_re, res_im], 1)


def per_device(
    current,
    probe,
    near_list,
    near_blocks,
    radiation,
    reception,
    interp,
    phase,
    leaf_table,
    coarse_table,
):
    near_fwd, near_adj = near_field(current, probe, near_list, near_blocks)
    fwd_set = (radiation, reception, leaf_table, coarse_table)
    adj_set = (
        jnp.stack([reception[0].T, -reception[1].T]),
        jnp.stack([radiation[0].T, -radiation[1].T]),
        conj_flip(leaf_table, (1, 2)),
        None,
    )
    far_both = far_field(
        jnp.stack([current, probe]),
        jnp.stack([fwd_set[0], adj_set[0]]),
        jnp.stack([fwd_set[1], adj_set[1]]),
        jnp.stack([fwd_set[2], adj_set[2]]),
        coarse_table[None],
        interp,
        phase,
    )
    far_fwd = far_both[0]
    far_adj = far_both[1]
    return (near_fwd + far_fwd, near_adj + far_adj)


def solution(mesh):
    placed = (
        P(None, "row", "col", None, None),
        P(None, "row", "col", None, None),
        P("row", "col", None),
        P(None, "row", "col", None, None, None),
        P(),
        P(),
        P(),
        P(),
        P(),
        P(),
    )
    return jax.shard_map(
        per_device,
        mesh=mesh,
        in_specs=placed,
        out_specs=(P(None, "row", "col", None, None), P(None, "row", "col", None, None)),
        check_vma=False,
    )
```

profile of v0, /device:TPU:1, one launch (start us, length us, event | category | flops | bytes accessed | tf_op | source)
XLA Modules:
  0.0 219.9 jit_solution(7066208127666837738)
XLA Ops:
  7.7 5.7 %collective-permute-start.4 = (f32[2,2,4,4,4,128]{5,4,3,2,0,1:T(4,128)}, f32[2,2,4,4,4,128]{5,4,3,2,0,1:T(4,128)}, u32[]{:S(2)}, u32[]{:S(2)}) collective-permute-start(f32[2,2,4,4,4,128]{5,4,3,2,0,1:T(4,128)} %pad_maximum_fusion.2), channel_id=1, source_target_pairs={{0,8},{8,16},{16,24},{24,32},{32,40},{40,48},{48,56},{56,64},{64,7... | collective-permute-start | bytes 393224 | tf_op jit(solution)/shard_map/ppermute | solution.py:17
  14.7 3.0 %collective-permute-start.8 = (bf16[1,2,2,4,256]{4,3,0,1,2:T(4,128)(2,1)}, bf16[1,2,2,4,256]{4,3,0,1,2:T(4,128)(2,1)}, u32[]{:S(2)}, u32[]{:S(2)}) collective-permute-start(bf16[1,2,2,4,256]{4,3,0,1,2:T(4,128)(2,1)} %pad_maximum_fusion.12), channel_id=1, source_target_pairs={{0,8},{8,0},{16,24},{24,16},{32,40},{40,32},{48,56},{56,48},{64,72... | collective-permute-start | bytes 24584 | tf_op jit(solution)/shard_map/ppermute | solution.py:101
  26.1 3.0 %collective-permute-start.17 = (f32[2,6,4,128]{3,2,0,1:T(4,128)}, f32[2,6,4,128]{3,2,0,1:T(4,128)}, u32[]{:S(2)}, u32[]{:S(2)}) collective-permute-start(f32[2,6,4,128]{3,2,0,1:T(4,128)} %slice_bitcast_fusion.25), channel_id=1, source_target_pairs={{0,8},{8,16},{16,24},{24,32},{32,40},{40,48},{48,56},{56,64},{64,7... | collective-permute-start | bytes 73736 | tf_op jit(solution)/shard_map/ppermute | solution.py:29
  29.7 5.9 %collective-permute-start = (bf16[2,1,4,4,128]{4,3,2,1,0:T(4,128)(2,1)}, bf16[2,1,4,4,128]{4,3,2,1,0:T(4,128)(2,1)}, u32[]{:S(2)}, u32[]{:S(2)}) collective-permute-start(bf16[2,1,4,4,128]{4,3,2,1,0:T(4,128)(2,1)} %get-tuple-element.293), channel_id=1, source_target_pairs={{0,8},{8,16},{16,24},{24,32},{32,40},{40,48},{48,56},{56,64},{64,7... | collective-permute-start | bytes 24584 | tf_op jit(solution)/shard_map/ppermute | solution.py:17
  37.7 3.5 %fusion.131 = (f32[2,1,12,12,128]{4,1,3,2,0:T(1,128)}, f32[2,1,12,12,128]{4,1,3,2,0:T(1,128)}, f32[2,1,12,12,128]{4,1,3,2,0:T(1,128)}, f32[2,1,12,12,128]{4,1,3,...) fusion(f32[2,2,15,15,128]{4,1,3,2,0:T(2,128)S(1)} %maximum_mult, ...), kind=kLoop, calls=%fused_computation.324 | loop fusion | bytes 5603328 | tf_op jit(solution)/shard_map/slice | solution.py:187
  41.2 2.4 %fusion.132 = (f32[2,1,12,12,128]{4,1,3,2,0:T(1,128)}, f32[2,1,12,12,128]{4,1,3,2,0:T(1,128)}, f32[2,1,12,12,128]{4,1,3,2,0:T(1,128)}, f32[2,1,12,12,128]{4,1,3,...) fusion(f32[2,2,15,15,128]{4,1,3,2,0:T(2,128)S(1)} %maximum_mult, ...), kind=kLoop, calls=%fused_computation.325 | loop fusion | bytes 3833856 | tf_op jit(solution)/shard_map/slice | solution.py:187
  44.3 2.9 %constant_dynamic-slice_fusion = (bf16[1,64,8,256]{3,0,2,1:T(2,128)(2,1)}, bf16[1,64,8,256]{3,0,2,1:T(2,128)(2,1)S(1)}) fusion(bf16[2,127,15,256]{3,0,2,1:T(2,128)(2,1)} %param.45, s32[]{:T(128)S(6)} %select_n.101, s32[]{:T(128)S(6)} %select_n.102, s32[]{:T(128)S(6)} %add.263), kind=kLoop, calls=%fused_computation.303 | loop fusion | bytes 1048588 | tf_op jit(solution)/shard_map/slice | solution.py:145
  53.6 2.9 %fusion.130 = (f32[2,1,64,8,256]{4,1,3,2,0:T(1,128)}, f32[2,1,64,8,256]{4,1,3,2,0:T(1,128)}) fusion(f32[2,2,64,8,256]{4,1,3,2,0:T(2,128)S(1)} %maximum_convert_fusion), kind=kLoop, calls=%fused_computation.323 | loop fusion | bytes 4194304 | tf_op jit(solution)/shard_map/slice | solution.py:151
  109.9 2.4 %collective-permute-done.1 = bf16[2,1,4,4,128]{4,3,2,1,0:T(4,128)(2,1)S(1)} collective-permute-done((bf16[2,1,4,4,128]{4,3,2,1,0:T(4,128)(2,1)S(1)}, bf16[2,1,4,4,128]{4,3,2,1,0:T(4,128)(2,1)S(1)}, u32[]{:S(2)}, u32[]{:S(2)}) %collective-permute-start.1) | collective-permute-done | bytes 8224 | tf_op jit(solution)/shard_map/ppermute | solution.py:19
  113.1 6.1 %collective-permute-start.3 = (bf16[2,6,1,4,128]{4,3,2,1,0:T(4,128)(2,1)S(1)}, bf16[2,6,1,4,128]{4,3,2,1,0:T(4,128)(2,1)S(1)}, u32[]{:S(2)}, u32[]{:S(2)}) collective-permute-start(bf16[2,6,1,4,128]{4,3,2,1,0:T(4,128)(2,1)S(1)} %get-tuple-element.285), channel_id=1, source_target_pairs={{1,0},{2,1},{3,2},{4,3},{5,4},{6,5},{7,6},{9,8},{10,9},{11,10},{12... | collective-permute-start | bytes 36872 | tf_op jit(solution)/shard_map/ppermute | solution.py:19
  123.9 4.3 %collective-permute-start.9 = (bf16[2,2,2,4,256]{4,3,0,1,2:T(4,128)(2,1)}, bf16[2,2,2,4,256]{4,3,0,1,2:T(4,128)(2,1)}, u32[]{:S(2)}, u32[]{:S(2)}) collective-permute-start(bf16[2,2,2,4,256]{4,3,0,1,2:T(4,128)(2,1)} %maximum_select_fusion.5), channel_id=1, source_target_pairs={{0,16},{8,24},{16,0},{24,8},{32,48},{40,56},{48,32},{56,40},{64,80... | collective-permute-start | bytes 49160 | tf_op jit(solution)/shard_map/ppermute | solution.py:101
  132.4 3.9 %stack.386 = bf16[9,2,4,4,4,128]{5,0,4,1,3,2:T(8,128)(2,1)} concatenate(bf16[1,2,4,4,4,128]{5,0,4,1,3,2:T(2,128)(2,1)} %copy.732, bf16[1,2,4,4,4,128]{5,0,4,1,3,2:T(2,128)(2,1)} %copy.733, bf16[1,2,4,4,4,128]{5,0,4,1,3,2:T(2,128)(2,1)} %copy.734, bf16[1,2,4,4,4,128]{5,0,4,1,3,2:T(2,128)(2,1)} %copy.735, bf16[1,2,4,4,4,128]{5,0,4,1,3,2:T(2,128)(2,1)} %copy.736, ...), dimensions={0} | concatenate | bytes 589824 | tf_op jit(solution)/shard_map/stack | solution.py:51
  142.1 8.6 %collective-permute-start.10 = (bf16[4,2,2,4,256]{4,3,0,1,2:T(4,128)(2,1)S(1)}, bf16[4,2,2,4,256]{4,3,0,1,2:T(4,128)(2,1)S(1)}, u32[]{:S(2)}, u32[]{:S(2)}) collective-permute-start(bf16[4,2,2,4,256]{4,3,0,1,2:T(4,128)(2,1)S(1)} %maximum_select_fusion.4), channel_id=1, source_target_pairs={{0,32},{8,40},{16,48},{24,56},{32,0},{40,8},{48,16},{56,24},{64,96... | collective-permute-start | bytes 98312 | tf_op jit(solution)/shard_map/ppermute | solution.py:101
  150.8 3.0 %collective-permute-start.19 = (f32[2,4,4,128]{3,2,1,0:T(4,128)S(1)}, f32[2,4,4,128]{3,2,1,0:T(4,128)S(1)}, u32[]{:S(2)}, u32[]{:S(2)}) collective-permute-start(f32[2,4,4,128]{3,2,1,0:T(4,128)S(1)} %slice_bitcast_fusion.28), channel_id=1, source_target_pairs={{0,1},{1,2},{2,3},{3,4},{4,5},{5,6},{6,7},{8,9},{9,10},{10,11},{11... | collective-permute-start | bytes 49160 | tf_op jit(solution)/shard_map/ppermute | solution.py:29
  153.8 11.9 %collective-permute-start.11 = (bf16[8,2,2,4,256]{4,3,0,1,2:T(4,128)(2,1)S(1)}, bf16[8,2,2,4,256]{4,3,0,1,2:T(4,128)(2,1)S(1)}, u32[]{:S(2)}, u32[]{:S(2)}) collective-permute-start(bf16[8,2,2,4,256]{4,3,0,1,2:T(4,128)(2,1)S(1)} %maximum_select_fusion.3), channel_id=1, source_target_pairs={{0,64},{8,72},{16,80},{24,88},{32,96},{40,104},{48,112},{56,120},{... | collective-permute-start | bytes 196616 | tf_op jit(solution)/shard_map/ppermute | solution.py:101
  168.2 6.3 %collective-permute-start.12 = (bf16[16,2,2,4,256]{4,3,0,1,2:T(4,128)(2,1)S(1)}, bf16[16,2,2,4,256]{4,3,0,1,2:T(4,128)(2,1)S(1)}, u32[]{:S(2)}, u32[]{:S(2)}) collective-permute-start(bf16[16,2,2,4,256]{4,3,0,1,2:T(4,128)(2,1)S(1)} %maximum_select_fusion.2), channel_id=1, source_target_pairs={{0,128},{8,136},{16,144},{24,152},{32,160},{40,168},{48,176},{56,1... | collective-permute-start | bytes 393224 | tf_op jit(solution)/shard_map/ppermute | solution.py:101
  174.6 7.9 %collective-permute-start.20 = (f32[2,4,4,128]{3,2,1,0:T(4,128)S(1)}, f32[2,4,4,128]{3,2,1,0:T(4,128)S(1)}, u32[]{:S(2)}, u32[]{:S(2)}) collective-permute-start(f32[2,4,4,128]{3,2,1,0:T(4,128)S(1)} %slice_bitcast_fusion.26), channel_id=1, source_target_pairs={{1,0},{2,1},{3,2},{4,3},{5,4},{6,5},{7,6},{9,8},{10,9},{11,10},{12... | collective-permute-start | bytes 49160 | tf_op jit(solution)/shard_map/ppermute | solution.py:29
  182.7 3.2 %collective-permute-start.13 = (bf16[32,2,2,4,256]{4,3,0,1,2:T(4,128)(2,1)S(1)}, bf16[32,2,2,4,256]{4,3,0,1,2:T(4,128)(2,1)S(1)}, u32[]{:S(2)}, u32[]{:S(2)}) collective-permute-start(bf16[32,2,2,4,256]{4,3,0,1,2:T(4,128)(2,1)S(1)} %maximum_select_fusion.1), channel_id=1, source_target_pairs={{0,256},{8,264},{16,272},{24,280},{32,288},{40,296},{48,304},{56,3... | collective-permute-start | bytes 786440 | tf_op jit(solution)/shard_map/ppermute | solution.py:101
  187.1 5.2 %collective-permute-start.7 = (f32[2,2,12,4,4,128]{5,4,3,2,0,1:T(4,128)S(1)}, f32[2,2,12,4,4,128]{5,4,3,2,0,1:T(4,128)S(1)}, u32[]{:S(2)}, u32[]{:S(2)}) collective-permute-start(f32[2,2,12,4,4,128]{5,4,3,2,0,1:T(4,128)S(1)} %pad_maximum_fusion.1), channel_id=1, source_target_pairs={{1,0},{2,1},{3,2},{4,3},{5,4},{6,5},{7,6},{9,8},{10,9},{11,10},{12... | collective-permute-start | bytes 1179656 | tf_op jit(solution)/shard_map/ppermute | solution.py:19
  192.2 3.1 %collective-permute-start.6 = (f32[2,2,12,4,4,128]{5,4,3,2,0,1:T(4,128)S(1)}, f32[2,2,12,4,4,128]{5,4,3,2,0,1:T(4,128)S(1)}, u32[]{:S(2)}, u32[]{:S(2)}) collective-permute-start(f32[2,2,12,4,4,128]{5,4,3,2,0,1:T(4,128)S(1)} %pad_maximum_fusion.1), channel_id=1, source_target_pairs={{0,1},{1,2},{2,3},{3,4},{4,5},{5,6},{6,7},{8,9},{9,10},{10,11},{11... | collective-permute-start | bytes 1179656 | tf_op jit(solution)/shard_map/ppermute | solution.py:17
  203.2 2.4 %subtract_reduce_fusion.10 = (f32[2,4,128]{2,1,0:T(4,128)S(1)}, f32[2,4,128]{2,1,0:T(4,128)S(1)}, f32[2,4,128]{2,1,0:T(4,128)S(1)}, f32[2,4,128]{2,1,0:T(4,128)S...) fusion(f32[2,12,12,128]{3,2,1,0:T(8,128)S(1)} %copy-done.20, ...), kind=kLoop, calls=%fused_computation.71 | loop fusion | flops 7065600 | bytes 2998272 | tf_op jit(solution)/shard_map/reduce_sum | solution.py:189
  205.9 2.4 %subtract_reduce_fusion.16 = (f32[2,4,128]{2,1,0:T(4,128)S(1)}, f32[2,4,128]{2,1,0:T(4,128)S(1)}, f32[2,4,128]{2,1,0:T(4,128)S(1)}, f32[2,4,128]{2,1,0:T(4,128)S...) fusion(f32[2,12,12,128]{3,2,1,0:T(8,128)S(1)} %copy-done.8, ...), kind=kLoop, calls=%fused_computation.83 | loop fusion | flops 7065600 | bytes 2998272 | tf_op jit(solution)/shard_map/reduce_sum | solution.py:189
  210.5 2.6 %collective-permute-done.15 = f32[2,2,2,4,256]{4,0,3,1,2:T(2,128)S(1)} collective-permute-done((f32[2,2,2,4,256]{4,0,3,1,2:T(2,128)S(1)}, f32[2,2,2,4,256]{4,0,3,1,2:T(2,128)S(1)}, u32[]{:S(2)}, u32[]{:S(2)}) %collective-permute-start.15) | collective-permute-done | bytes 32800 | tf_op jit(solution)/shard_map/ppermute | solution.py:120
  213.2 3.9 %collective-permute-start.16 = (f32[1,2,2,4,256]{4,0,3,1,2:T(1,128)S(1)}, f32[1,2,2,4,256]{4,0,3,1,2:T(1,128)S(1)}, u32[]{:S(2)}, u32[]{:S(2)}) collective-permute-start(f32[1,2,2,4,256]{4,0,3,1,2:T(1,128)S(1)} %broadcast_select_fusion.1), channel_id=1, source_target_pairs={{0,1},{1,0},{2,3},{3,2},{4,5},{5,4},{6,7},{7,6},{8,9},{9,8},{10,11... | collective-permute-start | bytes 49160 | tf_op jit(solution)/shard_map/ppermute | solution.py:120
  (437 shorter events, 111.1 us)
Async XLA Ops:
  0.6 17.1 %copy-start.92 = (bf16[2,4,4,4,128]{4,3,2,1,0:T(4,128)(2,1)S(1)}, bf16[2,4,4,4,128]{4,3,2,1,0:T(4,128)(2,1)}, u32[]{:S(2)}) copy-start(bf16[2,4,4,4,128]{4,3,2,1,0:T(4,128)(2,1)} %param.37) | copy-start | bytes 98308
  6.4 179.5 %collective-permute-start.5 = (f32[2,2,4,4,4,128]{5,4,3,2,0,1:T(4,128)}, f32[2,2,4,4,4,128]{5,4,3,2,0,1:T(4,128)}, u32[]{:S(2)}, u32[]{:S(2)}) collective-permute-start(f32[2,2,4,4,4,128]{5,4,3,2,0,1:T(4,128)} %pad_maximum_fusion.2), channel_id=1, source_target_pairs={{8,0},{16,8},{24,16},{32,24},{40,32},{48,40},{56,48},{64,56},{72,6... | collective-permute-start | bytes 393224 | tf_op jit(solution)/shard_map/ppermute | solution.py:19
  7.7 178.2 %collective-permute-start.4 = (f32[2,2,4,4,4,128]{5,4,3,2,0,1:T(4,128)}, f32[2,2,4,4,4,128]{5,4,3,2,0,1:T(4,128)}, u32[]{:S(2)}, u32[]{:S(2)}) collective-permute-start(f32[2,2,4,4,4,128]{5,4,3,2,0,1:T(4,128)} %pad_maximum_fusion.2), channel_id=1, source_target_pairs={{0,8},{8,16},{16,24},{24,32},{32,40},{40,48},{48,56},{56,64},{64,7... | collective-permute-start | bytes 393224 | tf_op jit(solution)/shard_map/ppermute | solution.py:17
  14.7 104.4 %collective-permute-start.8 = (bf16[1,2,2,4,256]{4,3,0,1,2:T(4,128)(2,1)}, bf16[1,2,2,4,256]{4,3,0,1,2:T(4,128)(2,1)}, u32[]{:S(2)}, u32[]{:S(2)}) collective-permute-start(bf16[1,2,2,4,256]{4,3,0,1,2:T(4,128)(2,1)} %pad_maximum_fusion.12), channel_id=1, source_target_pairs={{0,8},{8,0},{16,24},{24,16},{32,40},{40,32},{48,56},{56,48},{64,72... | collective-permute-start | bytes 24584 | tf_op jit(solution)/shard_map/ppermute | solution.py:101
  26.1 113.0 %collective-permute-start.17 = (f32[2,6,4,128]{3,2,0,1:T(4,128)}, f32[2,6,4,128]{3,2,0,1:T(4,128)}, u32[]{:S(2)}, u32[]{:S(2)}) collective-permute-start(f32[2,6,4,128]{3,2,0,1:T(4,128)} %slice_bitcast_fusion.25), channel_id=1, source_target_pairs={{0,8},{8,16},{16,24},{24,32},{32,40},{40,48},{48,56},{56,64},{64,7... | collective-permute-start | bytes 73736 | tf_op jit(solution)/shard_map/ppermute | solution.py:29
  29.7 78.2 %collective-permute-start = (bf16[2,1,4,4,128]{4,3,2,1,0:T(4,128)(2,1)}, bf16[2,1,4,4,128]{4,3,2,1,0:T(4,128)(2,1)}, u32[]{:S(2)}, u32[]{:S(2)}) collective-permute-start(bf16[2,1,4,4,128]{4,3,2,1,0:T(4,128)(2,1)} %get-tuple-element.293), channel_id=1, source_target_pairs={{0,8},{8,16},{16,24},{24,32},{32,40},{40,48},{48,56},{56,64},{64,7... | collective-permute-start | bytes 24584 | tf_op jit(solution)/shard_map/ppermute | solution.py:17
  100.1 21.0 %copy-start.102 = (bf16[2,4,256]{2,1,0:T(4,128)(2,1)S(1)}, bf16[2,4,256]{2,1,0:T(4,128)(2,1)}, u32[]{:S(2)}) copy-start(bf16[2,4,256]{2,1,0:T(4,128)(2,1)} %copy-done.101) | copy-start | bytes 12292
  100.1 21.0 %copy-start.104 = (bf16[2,4,256]{2,1,0:T(4,128)(2,1)S(1)}, bf16[2,4,256]{2,1,0:T(4,128)(2,1)}, u32[]{:S(2)}) copy-start(bf16[2,4,256]{2,1,0:T(4,128)(2,1)} %copy-done.103) | copy-start | bytes 12292
  107.9 4.4 %collective-permute-start.1 = (bf16[2,1,4,4,128]{4,3,2,1,0:T(4,128)(2,1)S(1)}, bf16[2,1,4,4,128]{4,3,2,1,0:T(4,128)(2,1)S(1)}, u32[]{:S(2)}, u32[]{:S(2)}) collective-permute-start(bf16[2,1,4,4,128]{4,3,2,1,0:T(4,128)(2,1)S(1)} %copy-done.107), channel_id=1, source_target_pairs={{8,0},{16,8},{24,16},{32,24},{40,32},{48,40},{56,48},{64,56},{72,6... | collective-permute-start | bytes 24584 | tf_op jit(solution)/shard_map/ppermute | solution.py:19
  113.1 10.8 %collective-permute-start.3 = (bf16[2,6,1,4,128]{4,3,2,1,0:T(4,128)(2,1)S(1)}, bf16[2,6,1,4,128]{4,3,2,1,0:T(4,128)(2,1)S(1)}, u32[]{:S(2)}, u32[]{:S(2)}) collective-permute-start(bf16[2,6,1,4,128]{4,3,2,1,0:T(4,128)(2,1)S(1)} %get-tuple-element.285), channel_id=1, source_target_pairs={{1,0},{2,1},{3,2},{4,3},{5,4},{6,5},{7,6},{9,8},{10,9},{11,10},{12... | collective-permute-start | bytes 36872 | tf_op jit(solution)/shard_map/ppermute | solution.py:19
  119.1 9.1 %collective-permute-start.2 = (bf16[2,6,1,4,128]{4,3,2,1,0:T(4,128)(2,1)S(1)}, bf16[2,6,1,4,128]{4,3,2,1,0:T(4,128)(2,1)S(1)}, u32[]{:S(2)}, u32[]{:S(2)}) collective-permute-start(bf16[2,6,1,4,128]{4,3,2,1,0:T(4,128)(2,1)S(1)} %get-tuple-element.286), channel_id=1, source_target_pairs={{0,1},{1,2},{2,3},{3,4},{4,5},{5,6},{6,7},{8,9},{9,10},{10,11},{11... | collective-permute-start | bytes 36872 | tf_op jit(solution)/shard_map/ppermute | solution.py:17
  123.9 17.3 %collective-permute-start.9 = (bf16[2,2,2,4,256]{4,3,0,1,2:T(4,128)(2,1)}, bf16[2,2,2,4,256]{4,3,0,1,2:T(4,128)(2,1)}, u32[]{:S(2)}, u32[]{:S(2)}) collective-permute-start(bf16[2,2,2,4,256]{4,3,0,1,2:T(4,128)(2,1)} %maximum_select_fusion.5), channel_id=1, source_target_pairs={{0,16},{8,24},{16,0},{24,8},{32,48},{40,56},{48,32},{56,40},{64,80... | collective-permute-start | bytes 49160 | tf_op jit(solution)/shard_map/ppermute | solution.py:101
  139.9 10.8 %collective-permute-start.18 = (f32[2,6,4,128]{3,2,0,1:T(4,128)S(1)}, f32[2,6,4,128]{3,2,0,1:T(4,128)S(1)}, u32[]{:S(2)}, u32[]{:S(2)}) collective-permute-start(f32[2,6,4,128]{3,2,0,1:T(4,128)S(1)} %slice_bitcast_fusion.23), channel_id=1, source_target_pairs={{8,0},{16,8},{24,16},{32,24},{40,32},{48,40},{56,48},{64,56},{72,6... | collective-permute-start | bytes 73736 | tf_op jit(solution)/shard_map/ppermute | solution.py:29
  142.1 11.6 %collective-permute-start.10 = (bf16[4,2,2,4,256]{4,3,0,1,2:T(4,128)(2,1)S(1)}, bf16[4,2,2,4,256]{4,3,0,1,2:T(4,128)(2,1)S(1)}, u32[]{:S(2)}, u32[]{:S(2)}) collective-permute-start(bf16[4,2,2,4,256]{4,3,0,1,2:T(4,128)(2,1)S(1)} %maximum_select_fusion.4), channel_id=1, source_target_pairs={{0,32},{8,40},{16,48},{24,56},{32,0},{40,8},{48,16},{56,24},{64,96... | collective-permute-start | bytes 98312 | tf_op jit(solution)/shard_map/ppermute | solution.py:101
  150.8 15.0 %collective-permute-start.19 = (f32[2,4,4,128]{3,2,1,0:T(4,128)S(1)}, f32[2,4,4,128]{3,2,1,0:T(4,128)S(1)}, u32[]{:S(2)}, u32[]{:S(2)}) collective-permute-start(f32[2,4,4,128]{3,2,1,0:T(4,128)S(1)} %slice_bitcast_fusion.28), channel_id=1, source_target_pairs={{0,1},{1,2},{2,3},{3,4},{4,5},{5,6},{6,7},{8,9},{9,10},{10,11},{11... | collective-permute-start | bytes 49160 | tf_op jit(solution)/shard_map/ppermute | solution.py:29
  153.8 14.3 %collective-permute-start.11 = (bf16[8,2,2,4,256]{4,3,0,1,2:T(4,128)(2,1)S(1)}, bf16[8,2,2,4,256]{4,3,0,1,2:T(4,128)(2,1)S(1)}, u32[]{:S(2)}, u32[]{:S(2)}) collective-permute-start(bf16[8,2,2,4,256]{4,3,0,1,2:T(4,128)(2,1)S(1)} %maximum_select_fusion.3), channel_id=1, source_target_pairs={{0,64},{8,72},{16,80},{24,88},{32,96},{40,104},{48,112},{56,120},{... | collective-permute-start | bytes 196616 | tf_op jit(solution)/shard_map/ppermute | solution.py:101
  168.2 14.2 %collective-permute-start.12 = (bf16[16,2,2,4,256]{4,3,0,1,2:T(4,128)(2,1)S(1)}, bf16[16,2,2,4,256]{4,3,0,1,2:T(4,128)(2,1)S(1)}, u32[]{:S(2)}, u32[]{:S(2)}) collective-permute-start(bf16[16,2,2,4,256]{4,3,0,1,2:T(4,128)(2,1)S(1)} %maximum_select_fusion.2), channel_id=1, source_target_pairs={{0,128},{8,136},{16,144},{24,152},{32,160},{40,168},{48,176},{56,1... | collective-permute-start | bytes 393224 | tf_op jit(solution)/shard_map/ppermute | solution.py:101
  174.6 11.3 %collective-permute-start.20 = (f32[2,4,4,128]{3,2,1,0:T(4,128)S(1)}, f32[2,4,4,128]{3,2,1,0:T(4,128)S(1)}, u32[]{:S(2)}, u32[]{:S(2)}) collective-permute-start(f32[2,4,4,128]{3,2,1,0:T(4,128)S(1)} %slice_bitcast_fusion.26), channel_id=1, source_target_pairs={{1,0},{2,1},{3,2},{4,3},{5,4},{6,5},{7,6},{9,8},{10,9},{11,10},{12... | collective-permute-start | bytes 49160 | tf_op jit(solution)/shard_map/ppermute | solution.py:29
  182.7 12.7 %collective-permute-start.13 = (bf16[32,2,2,4,256]{4,3,0,1,2:T(4,128)(2,1)S(1)}, bf16[32,2,2,4,256]{4,3,0,1,2:T(4,128)(2,1)S(1)}, u32[]{:S(2)}, u32[]{:S(2)}) collective-permute-start(bf16[32,2,2,4,256]{4,3,0,1,2:T(4,128)(2,1)S(1)} %maximum_select_fusion.1), channel_id=1, source_target_pairs={{0,256},{8,264},{16,272},{24,280},{32,288},{40,296},{48,304},{56,3... | collective-permute-start | bytes 786440 | tf_op jit(solution)/shard_map/ppermute | solution.py:101
  187.1 12.8 %collective-permute-start.7 = (f32[2,2,12,4,4,128]{5,4,3,2,0,1:T(4,128)S(1)}, f32[2,2,12,4,4,128]{5,4,3,2,0,1:T(4,128)S(1)}, u32[]{:S(2)}, u32[]{:S(2)}) collective-permute-start(f32[2,2,12,4,4,128]{5,4,3,2,0,1:T(4,128)S(1)} %pad_maximum_fusion.1), channel_id=1, source_target_pairs={{1,0},{2,1},{3,2},{4,3},{5,4},{6,5},{7,6},{9,8},{10,9},{11,10},{12... | collective-permute-start | bytes 1179656 | tf_op jit(solution)/shard_map/ppermute | solution.py:19
  192.2 7.8 %collective-permute-start.6 = (f32[2,2,12,4,4,128]{5,4,3,2,0,1:T(4,128)S(1)}, f32[2,2,12,4,4,128]{5,4,3,2,0,1:T(4,128)S(1)}, u32[]{:S(2)}, u32[]{:S(2)}) collective-permute-start(f32[2,2,12,4,4,128]{5,4,3,2,0,1:T(4,128)S(1)} %pad_maximum_fusion.1), channel_id=1, source_target_pairs={{0,1},{1,2},{2,3},{3,4},{4,5},{5,6},{6,7},{8,9},{9,10},{10,11},{11... | collective-permute-start | bytes 1179656 | tf_op jit(solution)/shard_map/ppermute | solution.py:17
  197.5 10.9 %collective-permute-start.14 = (f32[4,2,2,4,256]{4,0,3,1,2:T(4,128)S(1)}, f32[4,2,2,4,256]{4,0,3,1,2:T(4,128)S(1)}, u32[]{:S(2)}, u32[]{:S(2)}) collective-permute-start(f32[4,2,2,4,256]{4,0,3,1,2:T(4,128)S(1)} %slice_select_fusion), channel_id=1, source_target_pairs={{0,4},{1,5},{2,6},{3,7},{4,0},{5,1},{6,2},{7,3},{8,12},{9,13},{10,... | collective-permute-start | bytes 196616 | tf_op jit(solution)/shard_map/ppermute | solution.py:120
  208.4 4.7 %collective-permute-start.15 = (f32[2,2,2,4,256]{4,0,3,1,2:T(2,128)S(1)}, f32[2,2,2,4,256]{4,0,3,1,2:T(2,128)S(1)}, u32[]{:S(2)}, u32[]{:S(2)}) collective-permute-start(f32[2,2,2,4,256]{4,0,3,1,2:T(2,128)S(1)} %broadcast_select_fusion), channel_id=1, source_target_pairs={{0,2},{1,3},{2,0},{3,1},{4,6},{5,7},{6,4},{7,5},{8,10},{9,11},{10,... | collective-permute-start | bytes 98312 | tf_op jit(solution)/shard_map/ppermute | solution.py:120
  213.2 4.7 %collective-permute-start.16 = (f32[1,2,2,4,256]{4,0,3,1,2:T(1,128)S(1)}, f32[1,2,2,4,256]{4,0,3,1,2:T(1,128)S(1)}, u32[]{:S(2)}, u32[]{:S(2)}) collective-permute-start(f32[1,2,2,4,256]{4,0,3,1,2:T(1,128)S(1)} %broadcast_select_fusion.1), channel_id=1, source_target_pairs={{0,1},{1,0},{2,3},{3,2},{4,5},{5,4},{6,7},{7,6},{8,9},{9,8},{10,11... | collective-permute-start | bytes 49160 | tf_op jit(solution)/shard_map/ppermute | solution.py:120
  (109 other events, 779.1 us)
where the time goes:
time: 222 us; the launch traced here: 220 us
  starting transfers between devices  91.2 us (41%)
  local copies, waits for them, and re-layouts  78.9 us (36%)
  other arithmetic  28.9 us (13%)
  matrix products  10.1 us (5%)
  waiting for transfers between devices  8.37 us (4%)
  between operations  2.51 us (1%)
    ppermute x6, starting transfers between devices, gather_ordered(): other = lax.ppermute(held, axis, [(i, i ^ step) for i in range(count)])  37.4 us
    mul x30, local copies, waits for them, and re-layouts, complex_mul(): left_im * right_im  30.4 us
    ppermute x4, starting transfers between devices, with_halo(): lax.ppermute(tail, axis, [(i, (i + 1) % count) for i in range(ends)])  16.6 us
    ppermute x4, starting transfers between devices, from_behind(): return lax.ppermute(block, axis, route)  15.1 us
    mul x17, local copies, waits for them, and re-layouts, complex_mul(): left_re * right_re - left_im * right_im  14.9 us
    ppermute x4, starting transfers between devices, with_halo(): lax.ppermute(head, axis, [((i + 1) % count, i) for i in range(ends)])  13.8 us
    another operation x10, local copies, waits for them, and re-layouts, near_field(): jnp.stack([padded[:, offset_code // 3:offset_code // 3 + box_side, offset...  9.88 us
    dot_general x17, matrix products, product(): return jnp.einsum(form, left, right, preferred_element_type=jnp.float32)  8.31 us
  transfers between devices with their start and end apart: 21, of which 5 were waited for; matrix products, arithmetic and copies ran while one was open for 50% of the time, Pallas kernels for 0%

commit v1 on v0

--- a/solution.py
+++ b/solution.py
@@ -160,6 +160,31 @@
     return scatter_sum(parts, "col")
 
 
+def leaf_incoming(window, leaf_tab, box_side):
+    span = 3 * box_side
+    reach = 2 * box_side - 1
+    width = 2 * reach + 1
+    streams, _, _, _, rhs, dirs = window.shape
+    targets = jnp.arange(box_side * box_side)
+    cells = jnp.arange(span * span)
+    d_row = (cells // span)[None, :] - (targets // box_side)[:, None] + box_side - 1
+    d_col = (cells % span)[None, :] - (targets % box_side)[:, None] + box_side - 1
+    far_off = (jnp.abs(d_row - reach) > 1) | (jnp.abs(d_col - reach) > 1)
+    code = jnp.where(far_off, d_row * width + d_col, -1)
+    pick = (code[:, :, None] == jnp.arange(width * width)).astype(jnp.float32)
+    flat_tab = leaf_tab.reshape(streams, 2, width * width, dirs)
+    coef = jnp.einsum("tnp,sxpq->tnsxq", pick, flat_tab, precision=HIGH)
+    win = jnp.moveaxis(window, (2, 3), (0, 1)).reshape(span * span, streams, 2, rhs, dirs)
+    c_re = coef[:, :, :, 0, None, :]
+    c_im = coef[:, :, :, 1, None, :]
+    w_re = win[None, :, :, 0]
+    w_im = win[None, :, :, 1]
+    in_re = (c_re * w_re - c_im * w_im).sum(1)
+    in_im = (c_re * w_im + c_im * w_re).sum(1)
+    leaf_in = jnp.stack([in_re, in_im], 2).reshape(box_side, box_side, streams, 2, rhs, dirs)
+    return jnp.moveaxis(leaf_in, (0, 1), (2, 3))
+
+
 def far_field(vectors, rad_tab, rcv_tab, leaf_tab, coarse_tab, interp, phase):
     box_side = vectors.shape[2]
     span = 3 * box_side
@@ -172,23 +197,7 @@
     )
     leaf_out = jnp.stack([out_re, out_im], 1)
     window = with_halo(leaf_out, (("row", 2), ("col", 3)), box_side)
-    offsets = jnp.arange(2 * reach + 1) - reach
-    near_offset = jnp.abs(offsets) <= 1
-    keep = 1.0 - (near_offset[:, None] & near_offset[None, :]).astype(jnp.float32)
-    masked = leaf_tab * keep[None, None, :, :, None]
-    rows_in = []
-    for row_pos in range(box_side):
-        cols_in = []
-        for col_pos in range(box_side):
-            row_first = box_side - 1 - row_pos
-            col_first = box_side - 1 - col_pos
-            coeffs = masked[:, :, row_first : row_first + span, col_first : col_first + span]
-            part_re, part_im = complex_mul(
-                coeffs[:, 0, :, :, None], coeffs[:, 1, :, :, None], window[:, 0], window[:, 1]
-            )
-            cols_in.append(jnp.stack([part_re.sum((1, 2)), part_im.sum((1, 2))], 1))
-        rows_in.append(jnp.stack(cols_in, 2))
-    leaf_in = jnp.stack(rows_in, 2)
+    leaf_in = leaf_incoming(window, leaf_tab, box_side)
     interpolated = jnp.einsum("kq,sxrcmq->sxrcmk", interp, leaf_out, precision=HIGH)
     angles = phase.reshape(box_side, box_side, -1)
     cos_ph = jnp.cos(angles)[:, :, None, :]

time: 222 us -> 177 us (0.80)
  local copies, waits for them, and re-layouts: 78.9 us -> 30.1 us
  waiting for transfers between devices: 8.37 us -> 11.5 us
    mul x47 -> x4, local copies, waits for them, and re-layouts: 45.3 us -> 2.99 us  [leaf_incoming(): in_re = (c_re * w_re - c_im * w_im).sum(1)]
    slice x4 -> x0, local copies, waits for them, and re-layouts: 6.1 us -> none  [the longest x3 3.69 us: far_field(): coeffs[:, 0, :, :, None]]
    reduce_sum x3 -> x1, other arithmetic: 6.33 us -> 3.47 us  [leaf_incoming(): in_re = (c_re * w_re - c_im * w_im).sum(1)]
    ppermute x3, waiting for transfers between devices: 3.42 us -> 5.88 us  [scatter_sum(): lax.ppermute(send, axis, [(i, i ^ step) for i in range(count)])]
  transfers between devices with their start and end apart: 21 -> 21, of which waited for: 5 -> 5; matrix products, arithmetic and copies ran while one was open for 50% -> 36% of each run, Pallas kernels for 0% -> 0%
where the time goes in v1:
time: 177 us; the launch traced here: 175 us
  starting transfers between devices  90.7 us (51%)
  local copies, waits for them, and re-layouts  30.1 us (17%)
  other arithmetic  28.6 us (16%)
  matrix products  12.1 us (7%)
  waiting for transfers between devices  11.5 us (6%)
  between operations  1.79 us (1%)
    ppermute x6, starting transfers between devices, gather_ordered(): other = lax.ppermute(held, axis, [(i, i ^ step) for i in range(count)])  37.7 us
    ppermute x4, starting transfers between devices, with_halo(): lax.ppermute(tail, axis, [(i, (i + 1) % count) for i in range(ends)])  16.8 us
    ppermute x4, starting transfers between devices, from_behind(): return lax.ppermute(block, axis, route)  15 us
    ppermute x4, starting transfers between devices, with_halo(): lax.ppermute(head, axis, [((i + 1) % count, i) for i in range(ends)])  13.7 us
    another operation x10, local copies, waits for them, and re-layouts, near_field(): jnp.stack([padded[:, offset_code // 3:offset_code // 3 + box_side, offset...  10.6 us
    dot_general x17, matrix products, product(): return jnp.einsum(form, left, right, preferred_element_type=jnp.float32)  8.3 us
    ppermute x3, starting transfers between devices, scatter_sum(): lax.ppermute(send, axis, [(i, i ^ step) for i in range(count)])  7.42 us
    ppermute x3, waiting for transfers between devices, scatter_sum(): lax.ppermute(send, axis, [(i, i ^ step) for i in range(count)])  5.88 us
  transfers between devices with their start and end apart: 21, of which 5 were waited for; matrix products, arithmetic and copies ran while one was open for 36% of the time, Pallas kernels for 0%

profile of v1, /device:TPU:1, one launch (start us, length us, event | category | flops | bytes accessed | tf_op | source)
XLA Modules:
  0.0 174.9 jit_solution(4172672838956095371)
XLA Ops:
  7.7 5.6 %collective-permute-start.4 = (f32[2,2,4,4,4,128]{5,4,3,2,0,1:T(4,128)}, f32[2,2,4,4,4,128]{5,4,3,2,0,1:T(4,128)}, u32[]{:S(2)}, u32[]{:S(2)}) collective-permute-start(f32[2,2,4,4,4,128]{5,4,3,2,0,1:T(4,128)} %pad_maximum_fusion.3), channel_id=1, source_target_pairs={{0,8},{8,16},{16,24},{24,32},{32,40},{40,48},{48,56},{56,64},{64,7... | collective-permute-start | bytes 393224 | tf_op jit(solution)/shard_map/ppermute | solution.py:17
  14.7 3.0 %collective-permute-start.8 = (bf16[1,2,2,4,256]{4,3,0,1,2:T(4,128)(2,1)}, bf16[1,2,2,4,256]{4,3,0,1,2:T(4,128)(2,1)}, u32[]{:S(2)}, u32[]{:S(2)}) collective-permute-start(bf16[1,2,2,4,256]{4,3,0,1,2:T(4,128)(2,1)} %pad_maximum_fusion.13), channel_id=1, source_target_pairs={{0,8},{8,0},{16,24},{24,16},{32,40},{40,32},{48,56},{56,48},{64,72... | collective-permute-start | bytes 24584 | tf_op jit(solution)/shard_map/ppermute | solution.py:101
  26.2 3.0 %collective-permute-start.17 = (f32[2,6,4,128]{3,2,0,1:T(4,128)}, f32[2,6,4,128]{3,2,0,1:T(4,128)}, u32[]{:S(2)}, u32[]{:S(2)}) collective-permute-start(f32[2,6,4,128]{3,2,0,1:T(4,128)} %slice_bitcast_fusion.27), channel_id=1, source_target_pairs={{0,8},{8,16},{16,24},{24,32},{32,40},{40,48},{48,56},{56,64},{64,7... | collective-permute-start | bytes 73736 | tf_op jit(solution)/shard_map/ppermute | solution.py:29
  29.8 5.9 %collective-permute-start = (bf16[2,1,4,4,128]{4,3,2,1,0:T(4,128)(2,1)}, bf16[2,1,4,4,128]{4,3,2,1,0:T(4,128)(2,1)}, u32[]{:S(2)}, u32[]{:S(2)}) collective-permute-start(bf16[2,1,4,4,128]{4,3,2,1,0:T(4,128)(2,1)} %get-tuple-element.201), channel_id=1, source_target_pairs={{0,8},{8,16},{16,24},{24,32},{32,40},{40,48},{48,56},{56,64},{64,7... | collective-permute-start | bytes 24584 | tf_op jit(solution)/shard_map/ppermute | solution.py:17
  38.6 2.9 %constant_dynamic-slice_fusion = (bf16[1,64,8,256]{3,0,2,1:T(2,128)(2,1)}, bf16[1,64,8,256]{3,0,2,1:T(2,128)(2,1)S(1)}) fusion(bf16[2,127,15,256]{3,0,2,1:T(2,128)(2,1)} %param.45, s32[]{:T(128)S(6)} %select_n.153, s32[]{:T(128)S(6)} %select_n.154, s32[]{:T(128)S(6)} %add.266), kind=kLoop, calls=%fused_computation.241 | loop fusion | bytes 1048588 | tf_op jit(solution)/shard_map/slice | solution.py:145
  47.8 3.0 %fusion.147 = (f32[2,1,64,8,256]{4,1,3,2,0:T(1,128)}, f32[2,1,64,8,256]{4,1,3,2,0:T(1,128)}) fusion(f32[2,2,64,8,256]{4,1,3,2,0:T(2,128)S(1)} %maximum_convert_fusion), kind=kLoop, calls=%fused_computation.273 | loop fusion | bytes 4194304 | tf_op jit(solution)/shard_map/slice | solution.py:151
  54.5 2.8 %slice_bitcast_fusion.1 = (f32[16,144,2,128]{3,1,2,0:T(8,128)}, f32[16,144,2,128]{3,1,2,0:T(8,128)}) fusion(f32[16,144,2,2,128]{4,1,3,2,0:T(8,128)S(1)} %fusion.1), kind=kLoop, calls=%fused_computation.5 | loop fusion | bytes 9437184 | tf_op jit(solution)/shard_map/mul | solution.py:182
  58.8 2.8 %fusion.16 = (f32[2,64,8,256]{3,2,1,0:T(8,128)S(1)}, f32[2,64,8,256]{3,2,1,0:T(8,128)}) fusion(f32[2,1,64,8,256]{4,1,3,2,0:T(1,128)} %get-tuple-element.166, f32[64,8]{1,0:T(8,128)} %copy.357, f32[2,1,64,8,256]{4,1,3,2,0:T(1,128)} %get-tuple-element.167), kind=kLoop, calls=%fused_computation.37 | loop fusion | flops 524288 | bytes 4196352 | tf_op jit(solution)/shard_map/mul | solution.py:151
  65.7 2.6 %collective-permute-done.1 = bf16[2,1,4,4,128]{4,3,2,1,0:T(4,128)(2,1)S(1)} collective-permute-done((bf16[2,1,4,4,128]{4,3,2,1,0:T(4,128)(2,1)}, bf16[2,1,4,4,128]{4,3,2,1,0:T(4,128)(2,1)S(1)}, u32[]{:S(2)}, u32[]{:S(2)}) %collective-permute-start.1) | collective-permute-done | bytes 8224 | tf_op jit(solution)/shard_map/ppermute | solution.py:19
  69.2 6.0 %collective-permute-start.3 = (bf16[2,6,1,4,128]{4,3,2,1,0:T(4,128)(2,1)S(1)}, bf16[2,6,1,4,128]{4,3,2,1,0:T(4,128)(2,1)S(1)}, u32[]{:S(2)}, u32[]{:S(2)}) collective-permute-start(bf16[2,6,1,4,128]{4,3,2,1,0:T(4,128)(2,1)S(1)} %get-tuple-element.193), channel_id=1, source_target_pairs={{1,0},{2,1},{3,2},{4,3},{5,4},{6,5},{7,6},{9,8},{10,9},{11,10},{12... | collective-permute-start | bytes 36872 | tf_op jit(solution)/shard_map/ppermute | solution.py:19
  80.0 4.7 %collective-permute-start.9 = (bf16[2,2,2,4,256]{4,3,0,1,2:T(4,128)(2,1)}, bf16[2,2,2,4,256]{4,3,0,1,2:T(4,128)(2,1)}, u32[]{:S(2)}, u32[]{:S(2)}) collective-permute-start(bf16[2,2,2,4,256]{4,3,0,1,2:T(4,128)(2,1)} %maximum_select_fusion.5), channel_id=1, source_target_pairs={{0,16},{8,24},{16,0},{24,8},{32,48},{40,56},{48,32},{56,40},{64,80... | collective-permute-start | bytes 49160 | tf_op jit(solution)/shard_map/ppermute | solution.py:101
  88.9 3.8 %stack.176 = bf16[9,2,4,4,4,128]{5,0,4,1,3,2:T(8,128)(2,1)} concatenate(bf16[1,2,4,4,4,128]{5,0,4,1,3,2:T(2,128)(2,1)} %copy.332, bf16[1,2,4,4,4,128]{5,0,4,1,3,2:T(2,128)(2,1)} %copy.333, bf16[1,2,4,4,4,128]{5,0,4,1,3,2:T(2,128)(2,1)} %copy.334, bf16[1,2,4,4,4,128]{5,0,4,1,3,2:T(2,128)(2,1)} %copy.335, bf16[1,2,4,4,4,128]{5,0,4,1,3,2:T(2,128)(2,1)} %copy.336, ...), dimensions={0} | concatenate | bytes 589824 | tf_op jit(solution)/shard_map/stack | solution.py:51
  98.5 8.6 %collective-permute-start.10 = (bf16[4,2,2,4,256]{4,3,0,1,2:T(4,128)(2,1)S(1)}, bf16[4,2,2,4,256]{4,3,0,1,2:T(4,128)(2,1)S(1)}, u32[]{:S(2)}, u32[]{:S(2)}) collective-permute-start(bf16[4,2,2,4,256]{4,3,0,1,2:T(4,128)(2,1)S(1)} %maximum_select_fusion.4), channel_id=1, source_target_pairs={{0,32},{8,40},{16,48},{24,56},{32,0},{40,8},{48,16},{56,24},{64,96... | collective-permute-start | bytes 98312 | tf_op jit(solution)/shard_map/ppermute | solution.py:101
  107.2 3.0 %collective-permute-start.19 = (f32[2,4,4,128]{3,2,1,0:T(4,128)S(1)}, f32[2,4,4,128]{3,2,1,0:T(4,128)S(1)}, u32[]{:S(2)}, u32[]{:S(2)}) collective-permute-start(f32[2,4,4,128]{3,2,1,0:T(4,128)S(1)} %slice_bitcast_fusion.30), channel_id=1, source_target_pairs={{0,1},{1,2},{2,3},{3,4},{4,5},{5,6},{6,7},{8,9},{9,10},{10,11},{11... | collective-permute-start | bytes 49160 | tf_op jit(solution)/shard_map/ppermute | solution.py:29
  110.3 11.9 %collective-permute-start.11 = (bf16[8,2,2,4,256]{4,3,0,1,2:T(4,128)(2,1)S(1)}, bf16[8,2,2,4,256]{4,3,0,1,2:T(4,128)(2,1)S(1)}, u32[]{:S(2)}, u32[]{:S(2)}) collective-permute-start(bf16[8,2,2,4,256]{4,3,0,1,2:T(4,128)(2,1)S(1)} %maximum_select_fusion.3), channel_id=1, source_target_pairs={{0,64},{8,72},{16,80},{24,88},{32,96},{40,104},{48,112},{56,120},{... | collective-permute-start | bytes 196616 | tf_op jit(solution)/shard_map/ppermute | solution.py:101
  124.7 6.4 %collective-permute-start.12 = (bf16[16,2,2,4,256]{4,3,0,1,2:T(4,128)(2,1)S(1)}, bf16[16,2,2,4,256]{4,3,0,1,2:T(4,128)(2,1)S(1)}, u32[]{:S(2)}, u32[]{:S(2)}) collective-permute-start(bf16[16,2,2,4,256]{4,3,0,1,2:T(4,128)(2,1)S(1)} %maximum_select_fusion.2), channel_id=1, source_target_pairs={{0,128},{8,136},{16,144},{24,152},{32,160},{40,168},{48,176},{56,1... | collective-permute-start | bytes 393224 | tf_op jit(solution)/shard_map/ppermute | solution.py:101
  131.1 7.8 %collective-permute-start.20 = (f32[2,4,4,128]{3,2,1,0:T(4,128)S(1)}, f32[2,4,4,128]{3,2,1,0:T(4,128)S(1)}, u32[]{:S(2)}, u32[]{:S(2)}) collective-permute-start(f32[2,4,4,128]{3,2,1,0:T(4,128)S(1)} %slice_bitcast_fusion.28), channel_id=1, source_target_pairs={{1,0},{2,1},{3,2},{4,3},{5,4},{6,5},{7,6},{9,8},{10,9},{11,10},{12... | collective-permute-start | bytes 49160 | tf_op jit(solution)/shard_map/ppermute | solution.py:29
  139.1 3.1 %collective-permute-start.13 = (bf16[32,2,2,4,256]{4,3,0,1,2:T(4,128)(2,1)S(1)}, bf16[32,2,2,4,256]{4,3,0,1,2:T(4,128)(2,1)S(1)}, u32[]{:S(2)}, u32[]{:S(2)}) collective-permute-start(bf16[32,2,2,4,256]{4,3,0,1,2:T(4,128)(2,1)S(1)} %maximum_select_fusion.1), channel_id=1, source_target_pairs={{0,256},{8,264},{16,272},{24,280},{32,288},{40,296},{48,304},{56,3... | collective-permute-start | bytes 786440 | tf_op jit(solution)/shard_map/ppermute | solution.py:101
  143.4 5.2 %collective-permute-start.7 = (f32[2,2,12,4,4,128]{5,4,3,2,0,1:T(4,128)S(1)}, f32[2,2,12,4,4,128]{5,4,3,2,0,1:T(4,128)S(1)}, u32[]{:S(2)}, u32[]{:S(2)}) collective-permute-start(f32[2,2,12,4,4,128]{5,4,3,2,0,1:T(4,128)S(1)} %pad_maximum_fusion.1), channel_id=1, source_target_pairs={{1,0},{2,1},{3,2},{4,3},{5,4},{6,5},{7,6},{9,8},{10,9},{11,10},{12... | collective-permute-start | bytes 1179656 | tf_op jit(solution)/shard_map/ppermute | solution.py:19
  148.6 3.1 %collective-permute-start.6 = (f32[2,2,12,4,4,128]{5,4,3,2,0,1:T(4,128)S(1)}, f32[2,2,12,4,4,128]{5,4,3,2,0,1:T(4,128)S(1)}, u32[]{:S(2)}, u32[]{:S(2)}) collective-permute-start(f32[2,2,12,4,4,128]{5,4,3,2,0,1:T(4,128)S(1)} %pad_maximum_fusion.1), channel_id=1, source_target_pairs={{0,1},{1,2},{2,3},{3,4},{4,5},{5,6},{6,7},{8,9},{9,10},{10,11},{11... | collective-permute-start | bytes 1179656 | tf_op jit(solution)/shard_map/ppermute | solution.py:17
  157.7 3.3 %collective-permute-done.14 = f32[4,2,2,4,256]{4,0,3,1,2:T(4,128)S(1)} collective-permute-done((f32[4,2,2,4,256]{4,0,3,1,2:T(4,128)S(1)}, f32[4,2,2,4,256]{4,0,3,1,2:T(4,128)S(1)}, u32[]{:S(2)}, u32[]{:S(2)}) %collective-permute-start.14) | collective-permute-done | bytes 65568 | tf_op jit(solution)/shard_map/ppermute | solution.py:120
  163.2 2.5 %collective-permute-done.15 = f32[2,2,2,4,256]{4,0,3,1,2:T(2,128)S(1)} collective-permute-done((f32[2,2,2,4,256]{4,0,3,1,2:T(2,128)S(1)}, f32[2,2,2,4,256]{4,0,3,1,2:T(2,128)S(1)}, u32[]{:S(2)}, u32[]{:S(2)}) %collective-permute-start.15) | collective-permute-done | bytes 32800 | tf_op jit(solution)/shard_map/ppermute | solution.py:120
  165.8 3.5 %collective-permute-start.16 = (f32[1,2,2,4,256]{4,0,3,1,2:T(1,128)S(1)}, f32[1,2,2,4,256]{4,0,3,1,2:T(1,128)S(1)}, u32[]{:S(2)}, u32[]{:S(2)}) collective-permute-start(f32[1,2,2,4,256]{4,0,3,1,2:T(1,128)S(1)} %broadcast_select_fusion.1), channel_id=1, source_target_pairs={{0,1},{1,0},{2,3},{3,2},{4,5},{5,4},{6,7},{7,6},{8,9},{9,8},{10,11... | collective-permute-start | bytes 49160 | tf_op jit(solution)/shard_map/ppermute | solution.py:120
  169.4 3.5 %subtract_reduce_fusion = (f32[16,2,4,128]{3,2,1,0:T(4,128)S(1)}, f32[16,2,4,128]{3,2,1,0:T(4,128)S(1)}) fusion(f32[144,2,4,128]{3,0,2,1:T(8,128)S(1)} %copy.353, f32[16,144,2,128]{3,1,2,0:T(8,128)S(1)} %copy-done.3, f32[144,2,4,128]{3,0,2,1:T(8,128)S(1)} %copy.352, f32[16,144,2,128]{3,1,2,0:T(8,128)S(1)} %copy-done.2), kind=kLoop, calls=%fused_computation.1 | loop fusion | flops 18841600 | bytes 6029312 | tf_op jit(solution)/shard_map/reduce_sum | solution.py:182
  (211 shorter events, 65.1 us)
Async XLA Ops:
  0.6 17.1 %copy-start.10 = (bf16[2,4,4,4,128]{4,3,2,1,0:T(4,128)(2,1)S(1)}, bf16[2,4,4,4,128]{4,3,2,1,0:T(4,128)(2,1)}, u32[]{:S(2)}) copy-start(bf16[2,4,4,4,128]{4,3,2,1,0:T(4,128)(2,1)} %param.37) | copy-start | bytes 98308
  0.7 17.1 %copy-start.1 = (bf16[2,4,4,2,128,128]{5,4,3,2,1,0:T(8,128)(2,1)S(1)}, bf16[2,4,4,2,128,128]{5,4,3,2,1,0:T(8,128)(2,1)}, u32[]{:S(2)}) copy-start(bf16[2,4,4,2,128,128]{5,4,3,2,1,0:T(8,128)(2,1)} %param.39) | copy-start | bytes 6291460
  6.4 135.9 %collective-permute-start.5 = (f32[2,2,4,4,4,128]{5,4,3,2,0,1:T(4,128)}, f32[2,2,4,4,4,128]{5,4,3,2,0,1:T(4,128)}, u32[]{:S(2)}, u32[]{:S(2)}) collective-permute-start(f32[2,2,4,4,4,128]{5,4,3,2,0,1:T(4,128)} %pad_maximum_fusion.3), channel_id=1, source_target_pairs={{8,0},{16,8},{24,16},{32,24},{40,32},{48,40},{56,48},{64,56},{72,6... | collective-permute-start | bytes 393224 | tf_op jit(solution)/shard_map/ppermute | solution.py:19
  7.7 134.6 %collective-permute-start.4 = (f32[2,2,4,4,4,128]{5,4,3,2,0,1:T(4,128)}, f32[2,2,4,4,4,128]{5,4,3,2,0,1:T(4,128)}, u32[]{:S(2)}, u32[]{:S(2)}) collective-permute-start(f32[2,2,4,4,4,128]{5,4,3,2,0,1:T(4,128)} %pad_maximum_fusion.3), channel_id=1, source_target_pairs={{0,8},{8,16},{16,24},{24,32},{32,40},{40,48},{48,56},{56,64},{64,7... | collective-permute-start | bytes 393224 | tf_op jit(solution)/shard_map/ppermute | solution.py:17
  14.7 60.5 %collective-permute-start.8 = (bf16[1,2,2,4,256]{4,3,0,1,2:T(4,128)(2,1)}, bf16[1,2,2,4,256]{4,3,0,1,2:T(4,128)(2,1)}, u32[]{:S(2)}, u32[]{:S(2)}) collective-permute-start(bf16[1,2,2,4,256]{4,3,0,1,2:T(4,128)(2,1)} %pad_maximum_fusion.13), channel_id=1, source_target_pairs={{0,8},{8,0},{16,24},{24,16},{32,40},{40,32},{48,56},{56,48},{64,72... | collective-permute-start | bytes 24584 | tf_op jit(solution)/shard_map/ppermute | solution.py:101
  19.8 18.2 %copy-start.9 = (bf16[2,128,128]{2,1,0:T(8,128)(2,1)S(1)}, bf16[2,128,128]{2,1,0:T(8,128)(2,1)}, u32[]{:S(2)}) copy-start(bf16[2,128,128]{2,1,0:T(8,128)(2,1)} %param.40) | copy-start | bytes 196612
  26.2 69.4 %collective-permute-start.17 = (f32[2,6,4,128]{3,2,0,1:T(4,128)}, f32[2,6,4,128]{3,2,0,1:T(4,128)}, u32[]{:S(2)}, u32[]{:S(2)}) collective-permute-start(f32[2,6,4,128]{3,2,0,1:T(4,128)} %slice_bitcast_fusion.27), channel_id=1, source_target_pairs={{0,8},{8,16},{16,24},{24,32},{32,40},{40,48},{48,56},{56,64},{64,7... | collective-permute-start | bytes 73736 | tf_op jit(solution)/shard_map/ppermute | solution.py:29
  29.8 33.9 %collective-permute-start = (bf16[2,1,4,4,128]{4,3,2,1,0:T(4,128)(2,1)}, bf16[2,1,4,4,128]{4,3,2,1,0:T(4,128)(2,1)}, u32[]{:S(2)}, u32[]{:S(2)}) collective-permute-start(bf16[2,1,4,4,128]{4,3,2,1,0:T(4,128)(2,1)} %get-tuple-element.201), channel_id=1, source_target_pairs={{0,8},{8,16},{16,24},{24,32},{32,40},{40,48},{48,56},{56,64},{64,7... | collective-permute-start | bytes 24584 | tf_op jit(solution)/shard_map/ppermute | solution.py:17
  63.7 4.6 %collective-permute-start.1 = (bf16[2,1,4,4,128]{4,3,2,1,0:T(4,128)(2,1)}, bf16[2,1,4,4,128]{4,3,2,1,0:T(4,128)(2,1)S(1)}, u32[]{:S(2)}, u32[]{:S(2)}) collective-permute-start(bf16[2,1,4,4,128]{4,3,2,1,0:T(4,128)(2,1)} %get-tuple-element.200), channel_id=1, source_target_pairs={{8,0},{16,8},{24,16},{32,24},{40,32},{48,40},{56,48},{64,56},{72,6... | collective-permute-start | bytes 24584 | tf_op jit(solution)/shard_map/ppermute | solution.py:19
  69.2 10.8 %collective-permute-start.3 = (bf16[2,6,1,4,128]{4,3,2,1,0:T(4,128)(2,1)S(1)}, bf16[2,6,1,4,128]{4,3,2,1,0:T(4,128)(2,1)S(1)}, u32[]{:S(2)}, u32[]{:S(2)}) collective-permute-start(bf16[2,6,1,4,128]{4,3,2,1,0:T(4,128)(2,1)S(1)} %get-tuple-element.193), channel_id=1, source_target_pairs={{1,0},{2,1},{3,2},{4,3},{5,4},{6,5},{7,6},{9,8},{10,9},{11,10},{12... | collective-permute-start | bytes 36872 | tf_op jit(solution)/shard_map/ppermute | solution.py:19
  75.2 9.5 %collective-permute-start.2 = (bf16[2,6,1,4,128]{4,3,2,1,0:T(4,128)(2,1)S(1)}, bf16[2,6,1,4,128]{4,3,2,1,0:T(4,128)(2,1)S(1)}, u32[]{:S(2)}, u32[]{:S(2)}) collective-permute-start(bf16[2,6,1,4,128]{4,3,2,1,0:T(4,128)(2,1)S(1)} %get-tuple-element.194), channel_id=1, source_target_pairs={{0,1},{1,2},{2,3},{3,4},{4,5},{5,6},{6,7},{8,9},{9,10},{10,11},{11... | collective-permute-start | bytes 36872 | tf_op jit(solution)/shard_map/ppermute | solution.py:17
  80.0 17.6 %collective-permute-start.9 = (bf16[2,2,2,4,256]{4,3,0,1,2:T(4,128)(2,1)}, bf16[2,2,2,4,256]{4,3,0,1,2:T(4,128)(2,1)}, u32[]{:S(2)}, u32[]{:S(2)}) collective-permute-start(bf16[2,2,2,4,256]{4,3,0,1,2:T(4,128)(2,1)} %maximum_select_fusion.5), channel_id=1, source_target_pairs={{0,16},{8,24},{16,0},{24,8},{32,48},{40,56},{48,32},{56,40},{64,80... | collective-permute-start | bytes 49160 | tf_op jit(solution)/shard_map/ppermute | solution.py:101
  96.4 10.8 %collective-permute-start.18 = (f32[2,6,4,128]{3,2,0,1:T(4,128)S(1)}, f32[2,6,4,128]{3,2,0,1:T(4,128)S(1)}, u32[]{:S(2)}, u32[]{:S(2)}) collective-permute-start(f32[2,6,4,128]{3,2,0,1:T(4,128)S(1)} %slice_bitcast_fusion.25), channel_id=1, source_target_pairs={{8,0},{16,8},{24,16},{32,24},{40,32},{48,40},{56,48},{64,56},{72,6... | collective-permute-start | bytes 73736 | tf_op jit(solution)/shard_map/ppermute | solution.py:29
  98.5 11.6 %collective-permute-start.10 = (bf16[4,2,2,4,256]{4,3,0,1,2:T(4,128)(2,1)S(1)}, bf16[4,2,2,4,256]{4,3,0,1,2:T(4,128)(2,1)S(1)}, u32[]{:S(2)}, u32[]{:S(2)}) collective-permute-start(bf16[4,2,2,4,256]{4,3,0,1,2:T(4,128)(2,1)S(1)} %maximum_select_fusion.4), channel_id=1, source_target_pairs={{0,32},{8,40},{16,48},{24,56},{32,0},{40,8},{48,16},{56,24},{64,96... | collective-permute-start | bytes 98312 | tf_op jit(solution)/shard_map/ppermute | solution.py:101
  107.2 15.0 %collective-permute-start.19 = (f32[2,4,4,128]{3,2,1,0:T(4,128)S(1)}, f32[2,4,4,128]{3,2,1,0:T(4,128)S(1)}, u32[]{:S(2)}, u32[]{:S(2)}) collective-permute-start(f32[2,4,4,128]{3,2,1,0:T(4,128)S(1)} %slice_bitcast_fusion.30), channel_id=1, source_target_pairs={{0,1},{1,2},{2,3},{3,4},{4,5},{5,6},{6,7},{8,9},{9,10},{10,11},{11... | collective-permute-start | bytes 49160 | tf_op jit(solution)/shard_map/ppermute | solution.py:29
  110.3 14.3 %collective-permute-start.11 = (bf16[8,2,2,4,256]{4,3,0,1,2:T(4,128)(2,1)S(1)}, bf16[8,2,2,4,256]{4,3,0,1,2:T(4,128)(2,1)S(1)}, u32[]{:S(2)}, u32[]{:S(2)}) collective-permute-start(bf16[8,2,2,4,256]{4,3,0,1,2:T(4,128)(2,1)S(1)} %maximum_select_fusion.3), channel_id=1, source_target_pairs={{0,64},{8,72},{16,80},{24,88},{32,96},{40,104},{48,112},{56,120},{... | collective-permute-start | bytes 196616 | tf_op jit(solution)/shard_map/ppermute | solution.py:101
  124.7 14.2 %collective-permute-start.12 = (bf16[16,2,2,4,256]{4,3,0,1,2:T(4,128)(2,1)S(1)}, bf16[16,2,2,4,256]{4,3,0,1,2:T(4,128)(2,1)S(1)}, u32[]{:S(2)}, u32[]{:S(2)}) collective-permute-start(bf16[16,2,2,4,256]{4,3,0,1,2:T(4,128)(2,1)S(1)} %maximum_select_fusion.2), channel_id=1, source_target_pairs={{0,128},{8,136},{16,144},{24,152},{32,160},{40,168},{48,176},{56,1... | collective-permute-start | bytes 393224 | tf_op jit(solution)/shard_map/ppermute | solution.py:101
  131.1 11.1 %collective-permute-start.20 = (f32[2,4,4,128]{3,2,1,0:T(4,128)S(1)}, f32[2,4,4,128]{3,2,1,0:T(4,128)S(1)}, u32[]{:S(2)}, u32[]{:S(2)}) collective-permute-start(f32[2,4,4,128]{3,2,1,0:T(4,128)S(1)} %slice_bitcast_fusion.28), channel_id=1, source_target_pairs={{1,0},{2,1},{3,2},{4,3},{5,4},{6,5},{7,6},{9,8},{10,9},{11,10},{12... | collective-permute-start | bytes 49160 | tf_op jit(solution)/shard_map/ppermute | solution.py:29
  139.1 12.6 %collective-permute-start.13 = (bf16[32,2,2,4,256]{4,3,0,1,2:T(4,128)(2,1)S(1)}, bf16[32,2,2,4,256]{4,3,0,1,2:T(4,128)(2,1)S(1)}, u32[]{:S(2)}, u32[]{:S(2)}) collective-permute-start(bf16[32,2,2,4,256]{4,3,0,1,2:T(4,128)(2,1)S(1)} %maximum_select_fusion.1), channel_id=1, source_target_pairs={{0,256},{8,264},{16,272},{24,280},{32,288},{40,296},{48,304},{56,3... | collective-permute-start | bytes 786440 | tf_op jit(solution)/shard_map/ppermute | solution.py:101
  143.4 12.3 %collective-permute-start.7 = (f32[2,2,12,4,4,128]{5,4,3,2,0,1:T(4,128)S(1)}, f32[2,2,12,4,4,128]{5,4,3,2,0,1:T(4,128)S(1)}, u32[]{:S(2)}, u32[]{:S(2)}) collective-permute-start(f32[2,2,12,4,4,128]{5,4,3,2,0,1:T(4,128)S(1)} %pad_maximum_fusion.1), channel_id=1, source_target_pairs={{1,0},{2,1},{3,2},{4,3},{5,4},{6,5},{7,6},{9,8},{10,9},{11,10},{12... | collective-permute-start | bytes 1179656 | tf_op jit(solution)/shard_map/ppermute | solution.py:19
  148.6 7.8 %collective-permute-start.6 = (f32[2,2,12,4,4,128]{5,4,3,2,0,1:T(4,128)S(1)}, f32[2,2,12,4,4,128]{5,4,3,2,0,1:T(4,128)S(1)}, u32[]{:S(2)}, u32[]{:S(2)}) collective-permute-start(f32[2,2,12,4,4,128]{5,4,3,2,0,1:T(4,128)S(1)} %pad_maximum_fusion.1), channel_id=1, source_target_pairs={{0,1},{1,2},{2,3},{3,4},{4,5},{5,6},{6,7},{8,9},{9,10},{10,11},{11... | collective-permute-start | bytes 1179656 | tf_op jit(solution)/shard_map/ppermute | solution.py:17
  153.7 7.4 %collective-permute-start.14 = (f32[4,2,2,4,256]{4,0,3,1,2:T(4,128)S(1)}, f32[4,2,2,4,256]{4,0,3,1,2:T(4,128)S(1)}, u32[]{:S(2)}, u32[]{:S(2)}) collective-permute-start(f32[4,2,2,4,256]{4,0,3,1,2:T(4,128)S(1)} %slice_select_fusion), channel_id=1, source_target_pairs={{0,4},{1,5},{2,6},{3,7},{4,0},{5,1},{6,2},{7,3},{8,12},{9,13},{10,... | collective-permute-start | bytes 196616 | tf_op jit(solution)/shard_map/ppermute | solution.py:120
  161.1 4.7 %collective-permute-start.15 = (f32[2,2,2,4,256]{4,0,3,1,2:T(2,128)S(1)}, f32[2,2,2,4,256]{4,0,3,1,2:T(2,128)S(1)}, u32[]{:S(2)}, u32[]{:S(2)}) collective-permute-start(f32[2,2,2,4,256]{4,0,3,1,2:T(2,128)S(1)} %broadcast_select_fusion), channel_id=1, source_target_pairs={{0,2},{1,3},{2,0},{3,1},{4,6},{5,7},{6,4},{7,5},{8,10},{9,11},{10,... | collective-permute-start | bytes 98312 | tf_op jit(solution)/shard_map/ppermute | solution.py:120
  165.8 7.0 %collective-permute-start.16 = (f32[1,2,2,4,256]{4,0,3,1,2:T(1,128)S(1)}, f32[1,2,2,4,256]{4,0,3,1,2:T(1,128)S(1)}, u32[]{:S(2)}, u32[]{:S(2)}) collective-permute-start(f32[1,2,2,4,256]{4,0,3,1,2:T(1,128)S(1)} %broadcast_select_fusion.1), channel_id=1, source_target_pairs={{0,1},{1,0},{2,3},{3,2},{4,5},{5,4},{6,7},{7,6},{8,9},{9,8},{10,11... | collective-permute-start | bytes 49160 | tf_op jit(solution)/shard_map/ppermute | solution.py:120
  (28 other events, 129.1 us)

commit v2 on v1

--- a/solution.py
+++ b/solution.py
@@ -122,12 +122,43 @@
     return held[0]
 
 
+def gather_radix(block, axis, radix):
+    count = lax.axis_size(axis)
+    index = lax.axis_index(axis)
+    held = block[None]
+    stride = 1
+    while stride < count:
+        width = min(radix, count // stride)
+        digit = (index // stride) % width
+        pieces = [held]
+        for step in range(1, width):
+            pairs = [
+                (i, i + (((i // stride) % width - step) % width - (i // stride) % width) * stride)
+                for i in range(count)
+            ]
+            pieces.append(lax.ppermute(held, axis, pairs))
+        ordered = jnp.roll(jnp.stack(pieces), digit, axis=0)
+        held = ordered.reshape((width * held.shape[0],) + held.shape[1:])
+        stride *= width
+    return held
+
+
+def scatter_sum_direct(parts, axis):
+    count = lax.axis_size(axis)
+    index = lax.axis_index(axis)
+    total = lax.dynamic_index_in_dim(parts, index, 0, keepdims=False)
+    for step in range(1, count):
+        piece = lax.dynamic_index_in_dim(parts, (index + step) % count, 0, keepdims=False)
+        total = total + lax.ppermute(piece, axis, [(i, (i + step) % count) for i in range(count)])
+    return total
+
+
 def coarse_exchange(top_b, coarse_tab):
     row_count = lax.axis_size("row")
     col_count = lax.axis_size("col")
     row_idx = lax.axis_index("row")
     col_idx = lax.axis_index("col")
-    sources = gather_ordered(top_b, "row").astype(jnp.float32)
+    sources = gather_radix(top_b, "row", 8).astype(jnp.float32)
     zero = jnp.zeros((), jnp.int32)
     fwd_tab = coarse_tab[0]
     fwd = lax.dynamic_slice(
@@ -157,7 +188,7 @@
     got_re = (c_re * val_re - c_im * val_im).sum(1)
     got_im = (c_re * val_im + c_im * val_re).sum(1)
     parts = jnp.moveaxis(jnp.stack([got_re, got_im], 1), 2, 0)
-    return scatter_sum(parts, "col")
+    return scatter_sum_direct(parts, "col")
 
 
 def leaf_incoming(window, leaf_tab, box_side):

time: 177 us -> 251 us (1.42)
  the two profiles are of different devices: /device:TPU:1 before, /device:TPU:12 now
where the time goes in v2:
time: 251 us; the launch traced here: 248 us
  starting transfers between devices  127 us (51%)
  local copies, waits for them, and re-layouts  59.3 us (24%)
  waiting for transfers between devices  24 us (10%)
  other arithmetic  23.2 us (9%)
  matrix products  12.7 us (5%)
    ppermute x14, starting transfers between devices, gather_radix(): pieces.append(lax.ppermute(held, axis, pairs))  74.8 us
    unnamed x109, local copies, waits for them, and re-layouts  27.8 us
    ppermute x7, starting transfers between devices, scatter_sum_direct(): lax.ppermute(piece, axis, [(i, (i + step) % count) for i in range(count)])  17.3 us
    ppermute x4, starting transfers between devices, with_halo(): lax.ppermute(head, axis, [((i + 1) % count, i) for i in range(ends)])  14.6 us
    ppermute x4, waiting for transfers between devices, with_halo(): lax.ppermute(tail, axis, [(i, (i + 1) % count) for i in range(ends)])  11 us
    another operation x10, local copies, waits for them, and re-layouts, near_field(): jnp.stack([padded[:, offset_code // 3:offset_code // 3 + box_side, offset...  10.7 us
    ppermute x4, starting transfers between devices, from_behind(): return lax.ppermute(block, axis, route)  10.6 us
    ppermute x4, starting transfers between devices, with_halo(): lax.ppermute(tail, axis, [(i, (i + 1) % count) for i in range(ends)])  9.37 us
  transfers between devices with their start and end apart: 33, of which 8 were waited for; matrix products, arithmetic and copies ran while one was open for 32% of the time, Pallas kernels for 0%

profile of v2, /device:TPU:12, one launch (start us, length us, event | category | flops | bytes accessed | tf_op | source)
XLA Modules:
  0.0 247.9 jit_solution(11494317113630060140)
XLA Ops:
  7.8 13.1 %collective-permute-start.8 = (bf16[1,2,2,4,256]{4,3,1,2,0:T(4,128)(2,1)}, bf16[1,2,2,4,256]{4,3,1,2,0:T(4,128)(2,1)}, u32[]{:S(2)}, u32[]{:S(2)}) collective-permute-start(bf16[1,2,2,4,256]{4,3,1,2,0:T(4,128)(2,1)} %pad_maximum_fusion.13), channel_id=1, source_target_pairs={{0,56},{8,0},{16,8},{24,16},{32,24},{40,32},{48,40},{56,48},{64,12... | collective-permute-start | bytes 24584 | tf_op jit(solution)/shard_map/ppermute | solution.py:139
  24.8 7.0 %collective-permute-start.11 = (bf16[1,2,2,4,256]{4,3,1,2,0:T(4,128)(2,1)}, bf16[1,2,2,4,256]{4,3,1,2,0:T(4,128)(2,1)}, u32[]{:S(2)}, u32[]{:S(2)}) collective-permute-start(bf16[1,2,2,4,256]{4,3,1,2,0:T(4,128)(2,1)} %pad_maximum_fusion.13), channel_id=1, source_target_pairs={{0,32},{8,40},{16,48},{24,56},{32,0},{40,8},{48,16},{56,24},{64,96... | collective-permute-start | bytes 24584 | tf_op jit(solution)/shard_map/ppermute | solution.py:139
  38.5 2.9 %constant_dynamic-slice_fusion = (bf16[1,64,8,256]{3,0,2,1:T(2,128)(2,1)}, bf16[1,64,8,256]{3,0,2,1:T(2,128)(2,1)S(1)}) fusion(bf16[2,127,15,256]{3,0,2,1:T(2,128)(2,1)} %param.45, s32[]{:T(128)S(6)} %select_n.156, s32[]{:T(128)S(6)} %select_n.157, s32[]{:T(128)S(6)} %add.405), kind=kLoop, calls=%fused_computation.291 | loop fusion | bytes 1048588 | tf_op jit(solution)/shard_map/slice | solution.py:176
  47.9 3.0 %fusion.159 = (f32[2,1,64,8,256]{4,1,3,2,0:T(1,128)}, f32[2,1,64,8,256]{4,1,3,2,0:T(1,128)}) fusion(f32[2,2,64,8,256]{4,1,3,2,0:T(2,128)S(1)} %maximum_convert_fusion), kind=kLoop, calls=%fused_computation.332 | loop fusion | bytes 4194304 | tf_op jit(solution)/shard_map/slice | solution.py:182
  70.6 4.7 %collective-permute-start.13 = (bf16[1,2,2,4,256]{4,3,1,2,0:T(4,128)(2,1)}, bf16[1,2,2,4,256]{4,3,1,2,0:T(4,128)(2,1)S(1)}, u32[]{:S(2)}, u32[]{:S(2)}) collective-permute-start(bf16[1,2,2,4,256]{4,3,1,2,0:T(4,128)(2,1)} %pad_maximum_fusion.13), channel_id=1, source_target_pairs={{0,16},{8,24},{16,32},{24,40},{32,48},{40,56},{48,0},{56,8},{64,80... | collective-permute-start | bytes 24584 | tf_op jit(solution)/shard_map/ppermute | solution.py:139
  76.6 3.4 %collective-permute-start.14 = (bf16[1,2,2,4,256]{4,3,1,2,0:T(4,128)(2,1)}, bf16[1,2,2,4,256]{4,3,1,2,0:T(4,128)(2,1)S(1)}, u32[]{:S(2)}, u32[]{:S(2)}) collective-permute-start(bf16[1,2,2,4,256]{4,3,1,2,0:T(4,128)(2,1)} %pad_maximum_fusion.13), channel_id=1, source_target_pairs={{0,8},{8,16},{16,24},{24,32},{32,40},{40,48},{48,56},{56,0},{64,72... | collective-permute-start | bytes 24584 | tf_op jit(solution)/shard_map/ppermute | solution.py:139
  81.3 3.3 %collective-permute-start.29 = (f32[2,6,4,128]{3,2,0,1:T(4,128)}, f32[2,6,4,128]{3,2,0,1:T(4,128)}, u32[]{:S(2)}, u32[]{:S(2)}) collective-permute-start(f32[2,6,4,128]{3,2,0,1:T(4,128)} %slice_bitcast_fusion.27), channel_id=1, source_target_pairs={{0,8},{8,16},{16,24},{24,32},{32,40},{40,48},{48,56},{56,64},{64,7... | collective-permute-start | bytes 73736 | tf_op jit(solution)/shard_map/ppermute | solution.py:29
  85.9 7.6 %collective-permute-start.1 = (bf16[2,1,4,4,128]{4,3,2,1,0:T(4,128)(2,1)}, bf16[2,1,4,4,128]{4,3,2,1,0:T(4,128)(2,1)S(1)}, u32[]{:S(2)}, u32[]{:S(2)}) collective-permute-start(bf16[2,1,4,4,128]{4,3,2,1,0:T(4,128)(2,1)} %get-tuple-element.208), channel_id=1, source_target_pairs={{8,0},{16,8},{24,16},{32,24},{40,32},{48,40},{56,48},{64,56},{72,6... | collective-permute-start | bytes 24584 | tf_op jit(solution)/shard_map/ppermute | solution.py:19
  118.6 4.0 %collective-permute-start.15 = (bf16[8,2,2,4,256]{4,3,0,1,2:T(4,128)(2,1)}, bf16[8,2,2,4,256]{4,3,0,1,2:T(4,128)(2,1)}, u32[]{:S(2)}, u32[]{:S(2)}) collective-permute-start(bf16[8,2,2,4,256]{4,3,0,1,2:T(4,128)(2,1)} %dynamic-slice_bitcast_fusion), channel_id=1, source_target_pairs={{0,448},{8,456},{16,464},{24,472},{32,480},{40,488},{48,496},{56,5... | collective-permute-start | bytes 196616 | tf_op jit(solution)/shard_map/ppermute | solution.py:139
  126.6 12.9 %collective-permute-start.17 = (bf16[8,2,2,4,256]{4,3,0,1,2:T(4,128)(2,1)}, bf16[8,2,2,4,256]{4,3,0,1,2:T(4,128)(2,1)}, u32[]{:S(2)}, u32[]{:S(2)}) collective-permute-start(bf16[8,2,2,4,256]{4,3,0,1,2:T(4,128)(2,1)} %dynamic-slice_bitcast_fusion), channel_id=1, source_target_pairs={{0,320},{8,328},{16,336},{24,344},{32,352},{40,360},{48,368},{56,3... | collective-permute-start | bytes 196616 | tf_op jit(solution)/shard_map/ppermute | solution.py:139
  146.0 3.9 %stack.226 = bf16[9,2,4,4,4,128]{5,0,4,1,3,2:T(8,128)(2,1)} concatenate(bf16[1,2,4,4,4,128]{5,0,4,1,3,2:T(2,128)(2,1)} %copy.540, bf16[1,2,4,4,4,128]{5,0,4,1,3,2:T(2,128)(2,1)} %copy.541, bf16[1,2,4,4,4,128]{5,0,4,1,3,2:T(2,128)(2,1)} %copy.542, bf16[1,2,4,4,4,128]{5,0,4,1,3,2:T(2,128)(2,1)} %copy.543, bf16[1,2,4,4,4,128]{5,0,4,1,3,2:T(2,128)(2,1)} %copy.544, ...), dimensions={0} | concatenate | bytes 589824 | tf_op jit(solution)/shard_map/stack | solution.py:51
  152.9 3.4 %collective-permute-start.30 = (f32[2,6,4,128]{3,2,0,1:T(4,128)S(1)}, f32[2,6,4,128]{3,2,0,1:T(4,128)S(1)}, u32[]{:S(2)}, u32[]{:S(2)}) collective-permute-start(f32[2,6,4,128]{3,2,0,1:T(4,128)S(1)} %slice_bitcast_fusion.25), channel_id=1, source_target_pairs={{8,0},{16,8},{24,16},{32,24},{40,32},{48,40},{56,48},{64,56},{72,6... | collective-permute-start | bytes 73736 | tf_op jit(solution)/shard_map/ppermute | solution.py:29
  163.7 5.6 %collective-permute-start.19 = (bf16[8,2,2,4,256]{4,3,0,1,2:T(4,128)(2,1)}, bf16[8,2,2,4,256]{4,3,0,1,2:T(4,128)(2,1)S(1)}, u32[]{:S(2)}, u32[]{:S(2)}) collective-permute-start(bf16[8,2,2,4,256]{4,3,0,1,2:T(4,128)(2,1)} %dynamic-slice_bitcast_fusion), channel_id=1, source_target_pairs={{0,192},{8,200},{16,208},{24,216},{32,224},{40,232},{48,240},{56,2... | collective-permute-start | bytes 196616 | tf_op jit(solution)/shard_map/ppermute | solution.py:139
  169.4 3.7 %collective-permute-start.20 = (bf16[8,2,2,4,256]{4,3,0,1,2:T(4,128)(2,1)}, bf16[8,2,2,4,256]{4,3,0,1,2:T(4,128)(2,1)S(1)}, u32[]{:S(2)}, u32[]{:S(2)}) collective-permute-start(bf16[8,2,2,4,256]{4,3,0,1,2:T(4,128)(2,1)} %dynamic-slice_bitcast_fusion), channel_id=1, source_target_pairs={{0,128},{8,136},{16,144},{24,152},{32,160},{40,168},{48,176},{56,1... | collective-permute-start | bytes 196616 | tf_op jit(solution)/shard_map/ppermute | solution.py:139
  174.0 9.6 %collective-permute-start.21 = (bf16[8,2,2,4,256]{4,3,0,1,2:T(4,128)(2,1)}, bf16[8,2,2,4,256]{4,3,0,1,2:T(4,128)(2,1)S(1)}, u32[]{:S(2)}, u32[]{:S(2)}) collective-permute-start(bf16[8,2,2,4,256]{4,3,0,1,2:T(4,128)(2,1)} %dynamic-slice_bitcast_fusion), channel_id=1, source_target_pairs={{0,64},{8,72},{16,80},{24,88},{32,96},{40,104},{48,112},{56,120},{... | collective-permute-start | bytes 196616 | tf_op jit(solution)/shard_map/ppermute | solution.py:139
  188.3 3.2 %collective-permute-done.21 = bf16[8,2,2,4,256]{4,3,0,1,2:T(4,128)(2,1)S(1)} collective-permute-done((bf16[8,2,2,4,256]{4,3,0,1,2:T(4,128)(2,1)}, bf16[8,2,2,4,256]{4,3,0,1,2:T(4,128)(2,1)S(1)}, u32[]{:S(2)}, u32[]{:S(2)}) %collective-permute-start.21) | collective-permute-done | bytes 65568 | tf_op jit(solution)/shard_map/ppermute | solution.py:139
  200.3 5.6 %collective-permute-start.26 = (f32[2,2,4,256]{3,2,0,1:T(4,128)S(1)}, f32[2,2,4,256]{3,2,0,1:T(4,128)S(1)}, u32[]{:S(2)}, u32[]{:S(2)}) collective-permute-start(f32[2,2,4,256]{3,2,0,1:T(4,128)S(1)} %bitcast.538), channel_id=1, source_target_pairs={{0,5},{1,6},{2,7},{3,0},{4,1},{5,2},{6,3},{7,4},{8,13},{9,14},{10,... | collective-permute-start | bytes 49160 | tf_op jit(solution)/shard_map/ppermute | solution.py:152
  208.2 4.0 %collective-permute-start.24 = (f32[2,2,4,256]{3,2,0,1:T(4,128)S(1)}, f32[2,2,4,256]{3,2,0,1:T(4,128)S(1)}, u32[]{:S(2)}, u32[]{:S(2)}) collective-permute-start(f32[2,2,4,256]{3,2,0,1:T(4,128)S(1)} %bitcast.536), channel_id=1, source_target_pairs={{0,3},{1,4},{2,5},{3,6},{4,7},{5,0},{6,1},{7,2},{8,11},{9,12},{10,... | collective-permute-start | bytes 49160 | tf_op jit(solution)/shard_map/ppermute | solution.py:152
  215.5 2.9 %collective-permute-start.5 = (f32[2,2,4,4,4,128]{5,4,3,2,0,1:T(4,128)S(1)}, f32[2,2,4,4,4,128]{5,4,3,2,0,1:T(4,128)S(1)}, u32[]{:S(2)}, u32[]{:S(2)}) collective-permute-start(f32[2,2,4,4,4,128]{5,4,3,2,0,1:T(4,128)S(1)} %copy-done.21), channel_id=1, source_target_pairs={{8,0},{16,8},{24,16},{32,24},{40,32},{48,40},{56,48},{64,56},{72,6... | collective-permute-start | bytes 393224 | tf_op jit(solution)/shard_map/ppermute | solution.py:19
  218.4 2.9 %collective-permute-start.4 = (f32[2,2,4,4,4,128]{5,4,3,2,0,1:T(4,128)S(1)}, f32[2,2,4,4,4,128]{5,4,3,2,0,1:T(4,128)S(1)}, u32[]{:S(2)}, u32[]{:S(2)}) collective-permute-start(f32[2,2,4,4,4,128]{5,4,3,2,0,1:T(4,128)S(1)} %copy-done.21), channel_id=1, source_target_pairs={{0,8},{8,16},{16,24},{24,32},{32,40},{40,48},{48,56},{56,64},{64,7... | collective-permute-start | bytes 393224 | tf_op jit(solution)/shard_map/ppermute | solution.py:17
  223.4 5.1 %collective-permute-done.4 = f32[2,2,4,4,4,128]{5,4,3,2,0,1:T(4,128)S(1)} collective-permute-done((f32[2,2,4,4,4,128]{5,4,3,2,0,1:T(4,128)S(1)}, f32[2,2,4,4,4,128]{5,4,3,2,0,1:T(4,128)S(1)}, u32[]{:S(2)}, u32[]{:S(2)}) %collective-permute-start.4) | collective-permute-done | bytes 131104 | tf_op jit(solution)/shard_map/ppermute | solution.py:17
  233.0 3.1 %collective-permute-done.7 = f32[2,2,12,4,4,128]{5,4,3,2,0,1:T(4,128)S(1)} collective-permute-done((f32[2,2,12,4,4,128]{5,4,3,2,0,1:T(4,128)S(1)}, f32[2,2,12,4,4,128]{5,4,3,2,0,1:T(4,128)S(1)}, u32[]{:S(2)}, u32[]{:S(2)}) %collective-permute-start.7) | collective-permute-done | bytes 393248 | tf_op jit(solution)/shard_map/ppermute | solution.py:19
  236.0 3.8 %collective-permute-done.6 = f32[2,2,12,4,4,128]{5,4,3,2,0,1:T(4,128)S(1)} collective-permute-done((f32[2,2,12,4,4,128]{5,4,3,2,0,1:T(4,128)S(1)}, f32[2,2,12,4,4,128]{5,4,3,2,0,1:T(4,128)S(1)}, u32[]{:S(2)}, u32[]{:S(2)}) %collective-permute-start.6) | collective-permute-done | bytes 393248 | tf_op jit(solution)/shard_map/ppermute | solution.py:17
  242.5 3.5 %subtract_reduce_fusion = (f32[16,2,4,128]{3,2,1,0:T(4,128)S(1)}, f32[16,2,4,128]{3,2,1,0:T(4,128)S(1)}) fusion(f32[144,2,4,128]{3,0,2,1:T(8,128)S(1)} %copy.561, f32[16,144,2,128]{3,1,2,0:T(8,128)S(1)} %copy-done.3, f32[144,2,4,128]{3,0,2,1:T(8,128)S(1)} %copy.560, f32[16,144,2,128]{3,1,2,0:T(8,128)S(1)} %copy-done.2), kind=kLoop, calls=%fused_computation.1 | loop fusion | flops 18841600 | bytes 6029312 | tf_op jit(solution)/shard_map/reduce_sum | solution.py:213
  (272 shorter events, 123.7 us)
Async XLA Ops:
  7.8 62.8 %collective-permute-start.8 = (bf16[1,2,2,4,256]{4,3,1,2,0:T(4,128)(2,1)}, bf16[1,2,2,4,256]{4,3,1,2,0:T(4,128)(2,1)}, u32[]{:S(2)}, u32[]{:S(2)}) collective-permute-start(bf16[1,2,2,4,256]{4,3,1,2,0:T(4,128)(2,1)} %pad_maximum_fusion.13), channel_id=1, source_target_pairs={{0,56},{8,0},{16,8},{24,16},{32,24},{40,32},{48,40},{56,48},{64,12... | collective-permute-start | bytes 24584 | tf_op jit(solution)/shard_map/ppermute | solution.py:139
  21.0 55.7 %collective-permute-start.9 = (bf16[1,2,2,4,256]{4,3,1,2,0:T(4,128)(2,1)}, bf16[1,2,2,4,256]{4,3,1,2,0:T(4,128)(2,1)}, u32[]{:S(2)}, u32[]{:S(2)}) collective-permute-start(bf16[1,2,2,4,256]{4,3,1,2,0:T(4,128)(2,1)} %pad_maximum_fusion.13), channel_id=1, source_target_pairs={{0,48},{8,56},{16,0},{24,8},{32,16},{40,24},{48,32},{56,40},{64,11... | collective-permute-start | bytes 24584 | tf_op jit(solution)/shard_map/ppermute | solution.py:139
  22.9 58.4 %collective-permute-start.10 = (bf16[1,2,2,4,256]{4,3,1,2,0:T(4,128)(2,1)}, bf16[1,2,2,4,256]{4,3,1,2,0:T(4,128)(2,1)}, u32[]{:S(2)}, u32[]{:S(2)}) collective-permute-start(bf16[1,2,2,4,256]{4,3,1,2,0:T(4,128)(2,1)} %pad_maximum_fusion.13), channel_id=1, source_target_pairs={{0,40},{8,48},{16,56},{24,0},{32,8},{40,16},{48,24},{56,32},{64,10... | collective-permute-start | bytes 24584 | tf_op jit(solution)/shard_map/ppermute | solution.py:139
  24.8 61.1 %collective-permute-start.11 = (bf16[1,2,2,4,256]{4,3,1,2,0:T(4,128)(2,1)}, bf16[1,2,2,4,256]{4,3,1,2,0:T(4,128)(2,1)}, u32[]{:S(2)}, u32[]{:S(2)}) collective-permute-start(bf16[1,2,2,4,256]{4,3,1,2,0:T(4,128)(2,1)} %pad_maximum_fusion.13), channel_id=1, source_target_pairs={{0,32},{8,40},{16,48},{24,56},{32,0},{40,8},{48,16},{56,24},{64,96... | collective-permute-start | bytes 24584 | tf_op jit(solution)/shard_map/ppermute | solution.py:139
  31.9 63.0 %collective-permute-start.12 = (bf16[1,2,2,4,256]{4,3,1,2,0:T(4,128)(2,1)}, bf16[1,2,2,4,256]{4,3,1,2,0:T(4,128)(2,1)}, u32[]{:S(2)}, u32[]{:S(2)}) collective-permute-start(bf16[1,2,2,4,256]{4,3,1,2,0:T(4,128)(2,1)} %pad_maximum_fusion.13), channel_id=1, source_target_pairs={{0,24},{8,32},{16,40},{24,48},{32,56},{40,0},{48,8},{56,16},{64,88... | collective-permute-start | bytes 24584 | tf_op jit(solution)/shard_map/ppermute | solution.py:139
  70.6 27.5 %collective-permute-start.13 = (bf16[1,2,2,4,256]{4,3,1,2,0:T(4,128)(2,1)}, bf16[1,2,2,4,256]{4,3,1,2,0:T(4,128)(2,1)S(1)}, u32[]{:S(2)}, u32[]{:S(2)}) collective-permute-start(bf16[1,2,2,4,256]{4,3,1,2,0:T(4,128)(2,1)} %pad_maximum_fusion.13), channel_id=1, source_target_pairs={{0,16},{8,24},{16,32},{24,40},{32,48},{40,56},{48,0},{56,8},{64,80... | collective-permute-start | bytes 24584 | tf_op jit(solution)/shard_map/ppermute | solution.py:139
  76.6 22.0 %collective-permute-start.14 = (bf16[1,2,2,4,256]{4,3,1,2,0:T(4,128)(2,1)}, bf16[1,2,2,4,256]{4,3,1,2,0:T(4,128)(2,1)S(1)}, u32[]{:S(2)}, u32[]{:S(2)}) collective-permute-start(bf16[1,2,2,4,256]{4,3,1,2,0:T(4,128)(2,1)} %pad_maximum_fusion.13), channel_id=1, source_target_pairs={{0,8},{8,16},{16,24},{24,32},{32,40},{40,48},{48,56},{56,0},{64,72... | collective-permute-start | bytes 24584 | tf_op jit(solution)/shard_map/ppermute | solution.py:139
  81.3 70.8 %collective-permute-start.29 = (f32[2,6,4,128]{3,2,0,1:T(4,128)}, f32[2,6,4,128]{3,2,0,1:T(4,128)}, u32[]{:S(2)}, u32[]{:S(2)}) collective-permute-start(f32[2,6,4,128]{3,2,0,1:T(4,128)} %slice_bitcast_fusion.27), channel_id=1, source_target_pairs={{0,8},{8,16},{16,24},{24,32},{32,40},{40,48},{48,56},{56,64},{64,7... | collective-permute-start | bytes 73736 | tf_op jit(solution)/shard_map/ppermute | solution.py:29
  85.9 16.8 %collective-permute-start.1 = (bf16[2,1,4,4,128]{4,3,2,1,0:T(4,128)(2,1)}, bf16[2,1,4,4,128]{4,3,2,1,0:T(4,128)(2,1)S(1)}, u32[]{:S(2)}, u32[]{:S(2)}) collective-permute-start(bf16[2,1,4,4,128]{4,3,2,1,0:T(4,128)(2,1)} %get-tuple-element.208), channel_id=1, source_target_pairs={{8,0},{16,8},{24,16},{32,24},{40,32},{48,40},{56,48},{64,56},{72,6... | collective-permute-start | bytes 24584 | tf_op jit(solution)/shard_map/ppermute | solution.py:19
  103.6 22.9 %collective-permute-start.3 = (bf16[2,6,1,4,128]{4,3,2,1,0:T(4,128)(2,1)S(1)}, bf16[2,6,1,4,128]{4,3,2,1,0:T(4,128)(2,1)S(1)}, u32[]{:S(2)}, u32[]{:S(2)}) collective-permute-start(bf16[2,6,1,4,128]{4,3,2,1,0:T(4,128)(2,1)S(1)} %get-tuple-element.201), channel_id=1, source_target_pairs={{1,0},{2,1},{3,2},{4,3},{5,4},{6,5},{7,6},{9,8},{10,9},{11,10},{12... | collective-permute-start | bytes 36872 | tf_op jit(solution)/shard_map/ppermute | solution.py:19
  105.6 33.9 %collective-permute-start.2 = (bf16[2,6,1,4,128]{4,3,2,1,0:T(4,128)(2,1)S(1)}, bf16[2,6,1,4,128]{4,3,2,1,0:T(4,128)(2,1)S(1)}, u32[]{:S(2)}, u32[]{:S(2)}) collective-permute-start(bf16[2,6,1,4,128]{4,3,2,1,0:T(4,128)(2,1)S(1)} %get-tuple-element.202), channel_id=1, source_target_pairs={{0,1},{1,2},{2,3},{3,4},{4,5},{5,6},{6,7},{8,9},{9,10},{10,11},{11... | collective-permute-start | bytes 36872 | tf_op jit(solution)/shard_map/ppermute | solution.py:17
  118.6 50.7 %collective-permute-start.15 = (bf16[8,2,2,4,256]{4,3,0,1,2:T(4,128)(2,1)}, bf16[8,2,2,4,256]{4,3,0,1,2:T(4,128)(2,1)}, u32[]{:S(2)}, u32[]{:S(2)}) collective-permute-start(bf16[8,2,2,4,256]{4,3,0,1,2:T(4,128)(2,1)} %dynamic-slice_bitcast_fusion), channel_id=1, source_target_pairs={{0,448},{8,456},{16,464},{24,472},{32,480},{40,488},{48,496},{56,5... | collective-permute-start | bytes 196616 | tf_op jit(solution)/shard_map/ppermute | solution.py:139
  122.6 51.3 %collective-permute-start.16 = (bf16[8,2,2,4,256]{4,3,0,1,2:T(4,128)(2,1)}, bf16[8,2,2,4,256]{4,3,0,1,2:T(4,128)(2,1)}, u32[]{:S(2)}, u32[]{:S(2)}) collective-permute-start(bf16[8,2,2,4,256]{4,3,0,1,2:T(4,128)(2,1)} %dynamic-slice_bitcast_fusion), channel_id=1, source_target_pairs={{0,384},{8,392},{16,400},{24,408},{32,416},{40,424},{48,432},{56,4... | collective-permute-start | bytes 196616 | tf_op jit(solution)/shard_map/ppermute | solution.py:139
  126.6 57.9 %collective-permute-start.17 = (bf16[8,2,2,4,256]{4,3,0,1,2:T(4,128)(2,1)}, bf16[8,2,2,4,256]{4,3,0,1,2:T(4,128)(2,1)}, u32[]{:S(2)}, u32[]{:S(2)}) collective-permute-start(bf16[8,2,2,4,256]{4,3,0,1,2:T(4,128)(2,1)} %dynamic-slice_bitcast_fusion), channel_id=1, source_target_pairs={{0,320},{8,328},{16,336},{24,344},{32,352},{40,360},{48,368},{56,3... | collective-permute-start | bytes 196616 | tf_op jit(solution)/shard_map/ppermute | solution.py:139
  139.5 47.8 %collective-permute-start.18 = (bf16[8,2,2,4,256]{4,3,0,1,2:T(4,128)(2,1)}, bf16[8,2,2,4,256]{4,3,0,1,2:T(4,128)(2,1)}, u32[]{:S(2)}, u32[]{:S(2)}) collective-permute-start(bf16[8,2,2,4,256]{4,3,0,1,2:T(4,128)(2,1)} %dynamic-slice_bitcast_fusion), channel_id=1, source_target_pairs={{0,256},{8,264},{16,272},{24,280},{32,288},{40,296},{48,304},{56,3... | collective-permute-start | bytes 196616 | tf_op jit(solution)/shard_map/ppermute | solution.py:139
  163.7 24.5 %collective-permute-start.19 = (bf16[8,2,2,4,256]{4,3,0,1,2:T(4,128)(2,1)}, bf16[8,2,2,4,256]{4,3,0,1,2:T(4,128)(2,1)S(1)}, u32[]{:S(2)}, u32[]{:S(2)}) collective-permute-start(bf16[8,2,2,4,256]{4,3,0,1,2:T(4,128)(2,1)} %dynamic-slice_bitcast_fusion), channel_id=1, source_target_pairs={{0,192},{8,200},{16,208},{24,216},{32,224},{40,232},{48,240},{56,2... | collective-permute-start | bytes 196616 | tf_op jit(solution)/shard_map/ppermute | solution.py:139
  169.4 18.8 %collective-permute-start.20 = (bf16[8,2,2,4,256]{4,3,0,1,2:T(4,128)(2,1)}, bf16[8,2,2,4,256]{4,3,0,1,2:T(4,128)(2,1)S(1)}, u32[]{:S(2)}, u32[]{:S(2)}) collective-permute-start(bf16[8,2,2,4,256]{4,3,0,1,2:T(4,128)(2,1)} %dynamic-slice_bitcast_fusion), channel_id=1, source_target_pairs={{0,128},{8,136},{16,144},{24,152},{32,160},{40,168},{48,176},{56,1... | collective-permute-start | bytes 196616 | tf_op jit(solution)/shard_map/ppermute | solution.py:139
  174.0 17.5 %collective-permute-start.21 = (bf16[8,2,2,4,256]{4,3,0,1,2:T(4,128)(2,1)}, bf16[8,2,2,4,256]{4,3,0,1,2:T(4,128)(2,1)S(1)}, u32[]{:S(2)}, u32[]{:S(2)}) collective-permute-start(bf16[8,2,2,4,256]{4,3,0,1,2:T(4,128)(2,1)} %dynamic-slice_bitcast_fusion), channel_id=1, source_target_pairs={{0,64},{8,72},{16,80},{24,88},{32,96},{40,104},{48,112},{56,120},{... | collective-permute-start | bytes 196616 | tf_op jit(solution)/shard_map/ppermute | solution.py:139
  184.5 23.7 %collective-permute-start.32 = (f32[2,4,4,128]{3,2,1,0:T(4,128)S(1)}, f32[2,4,4,128]{3,2,1,0:T(4,128)S(1)}, u32[]{:S(2)}, u32[]{:S(2)}) collective-permute-start(f32[2,4,4,128]{3,2,1,0:T(4,128)S(1)} %slice_bitcast_fusion.28), channel_id=1, source_target_pairs={{1,0},{2,1},{3,2},{4,3},{5,4},{6,5},{7,6},{9,8},{10,9},{11,10},{12... | collective-permute-start | bytes 49160 | tf_op jit(solution)/shard_map/ppermute | solution.py:29
  197.9 14.2 %collective-permute-start.28 = (f32[2,2,4,256]{3,2,0,1:T(4,128)S(1)}, f32[2,2,4,256]{3,2,0,1:T(4,128)S(1)}, u32[]{:S(2)}, u32[]{:S(2)}) collective-permute-start(f32[2,2,4,256]{3,2,0,1:T(4,128)S(1)} %bitcast.533), channel_id=1, source_target_pairs={{0,7},{1,0},{2,1},{3,2},{4,3},{5,4},{6,5},{7,6},{8,15},{9,8},{10,9... | collective-permute-start | bytes 49160 | tf_op jit(solution)/shard_map/ppermute | solution.py:152
  197.9 16.2 %collective-permute-start.27 = (f32[2,2,4,256]{3,2,0,1:T(4,128)S(1)}, f32[2,2,4,256]{3,2,0,1:T(4,128)S(1)}, u32[]{:S(2)}, u32[]{:S(2)}) collective-permute-start(f32[2,2,4,256]{3,2,0,1:T(4,128)S(1)} %bitcast.532), channel_id=1, source_target_pairs={{0,6},{1,7},{2,0},{3,1},{4,2},{5,3},{6,4},{7,5},{8,14},{9,15},{10,... | collective-permute-start | bytes 49160 | tf_op jit(solution)/shard_map/ppermute | solution.py:152
  200.3 15.2 %collective-permute-start.26 = (f32[2,2,4,256]{3,2,0,1:T(4,128)S(1)}, f32[2,2,4,256]{3,2,0,1:T(4,128)S(1)}, u32[]{:S(2)}, u32[]{:S(2)}) collective-permute-start(f32[2,2,4,256]{3,2,0,1:T(4,128)S(1)} %bitcast.538), channel_id=1, source_target_pairs={{0,5},{1,6},{2,7},{3,0},{4,1},{5,2},{6,3},{7,4},{8,13},{9,14},{10,... | collective-permute-start | bytes 49160 | tf_op jit(solution)/shard_map/ppermute | solution.py:152
  206.0 12.4 %collective-permute-start.25 = (f32[2,2,4,256]{3,2,0,1:T(4,128)S(1)}, f32[2,2,4,256]{3,2,0,1:T(4,128)S(1)}, u32[]{:S(2)}, u32[]{:S(2)}) collective-permute-start(f32[2,2,4,256]{3,2,0,1:T(4,128)S(1)} %bitcast.537), channel_id=1, source_target_pairs={{0,4},{1,5},{2,6},{3,7},{4,0},{5,1},{6,2},{7,3},{8,12},{9,13},{10,... | collective-permute-start | bytes 49160 | tf_op jit(solution)/shard_map/ppermute | solution.py:152
  208.2 13.2 %collective-permute-start.24 = (f32[2,2,4,256]{3,2,0,1:T(4,128)S(1)}, f32[2,2,4,256]{3,2,0,1:T(4,128)S(1)}, u32[]{:S(2)}, u32[]{:S(2)}) collective-permute-start(f32[2,2,4,256]{3,2,0,1:T(4,128)S(1)} %bitcast.536), channel_id=1, source_target_pairs={{0,3},{1,4},{2,5},{3,6},{4,7},{5,0},{6,1},{7,2},{8,11},{9,12},{10,... | collective-permute-start | bytes 49160 | tf_op jit(solution)/shard_map/ppermute | solution.py:152
  (43 other events, 605.8 us)

commit v3 on v1

--- a/solution.py
+++ b/solution.py
@@ -42,12 +42,11 @@
     return jnp.einsum(form, left, right, preferred_element_type=jnp.float32)
 
 
-def near_field(current, probe, near_list, near_blocks):
+def near_field(padded, current, probe, near_list, near_blocks):
     box_side = current.shape[1]
     one_hot = (near_list[..., None] == jnp.arange(9)).astype(jnp.bfloat16)
     blocks_re = near_blocks[0]
     blocks_im = near_blocks[1]
-    padded = with_halo(current, (("row", 1), ("col", 2)), 1)
     shifted = jnp.stack(
         [
             padded[
@@ -186,7 +185,7 @@
 
 
 def far_field(vectors, rad_tab, rcv_tab, leaf_tab, coarse_tab, interp, phase):
-    box_side = vectors.shape[2]
+    box_side = vectors.shape[2] // 3
     span = 3 * box_side
     reach = 2 * box_side - 1
     out_re = product("srcmp,sqp->srcmq", vectors[:, 0], rad_tab[:, 0]) - product(
@@ -195,8 +194,8 @@
     out_im = product("srcmp,sqp->srcmq", vectors[:, 0], rad_tab[:, 1]) + product(
         "srcmp,sqp->srcmq", vectors[:, 1], rad_tab[:, 0]
     )
-    leaf_out = jnp.stack([out_re, out_im], 1)
-    window = with_halo(leaf_out, (("row", 2), ("col", 3)), box_side)
+    window = jnp.stack([out_re, out_im], 1)
+    leaf_out = window[:, :, box_side : 2 * box_side, box_side : 2 * box_side]
     leaf_in = leaf_incoming(window, leaf_tab, box_side)
     interpolated = jnp.einsum("kq,sxrcmq->sxrcmk", interp, leaf_out, precision=HIGH)
     angles = phase.reshape(box_side, box_side, -1)
@@ -235,7 +234,10 @@
     leaf_table,
     coarse_table,
 ):
-    near_fwd, near_adj = near_field(current, probe, near_list, near_blocks)
+    box_side = current.shape[1]
+    vectors = with_halo(jnp.stack([current, probe]), (("row", 2), ("col", 3)), box_side)
+    padded = vectors[0][:, box_side - 1 : 2 * box_side + 1, box_side - 1 : 2 * box_side + 1]
+    near_fwd, near_adj = near_field(padded, current, probe, near_list, near_blocks)
     fwd_set = (radiation, reception, leaf_table, coarse_table)
     adj_set = (
         jnp.stack([reception[0].T, -reception[1].T]),
@@ -244,7 +246,7 @@
         None,
     )
     far_both = far_field(
-        jnp.stack([current, probe]),
+        vectors,
         jnp.stack([fwd_set[0], adj_set[0]]),
         jnp.stack([fwd_set[1], adj_set[1]]),
         jnp.stack([fwd_set[2], adj_set[2]]),

time: 177 us -> 172 us (0.972)
  starting transfers between devices: 90.7 us -> 76.6 us
  local copies, waits for them, and re-layouts: 30.1 us -> 34.2 us
  waiting for transfers between devices: 11.5 us -> 13.8 us
  other arithmetic: 28.6 us -> 30.9 us
    ppermute x3, starting transfers between devices: 7.42 us -> 18.4 us  [scatter_sum(): lax.ppermute(send, axis, [(i, i ^ step) for i in range(count)])]
    ppermute x4 -> x2, starting transfers between devices: 13.7 us -> 3.2 us  [with_halo(): lax.ppermute(head, axis, [((i + 1) % count, i) for i in range(ends)])]
    ppermute x6, waiting for transfers between devices: 2.34 us -> 10.3 us  [gather_ordered(): other = lax.ppermute(held, axis, [(i, i ^ step) for i in range(count)])]
    ppermute x4 -> x2, starting transfers between devices: 16.8 us -> 9.48 us  [with_halo(): lax.ppermute(tail, axis, [(i, (i + 1) % count) for i in range(ends)])]
    ppermute x6, starting transfers between devices: 37.7 us -> 31.7 us  [gather_ordered(): other = lax.ppermute(held, axis, [(i, i ^ step) for i in range(count)])]
    ppermute x3, waiting for transfers between devices: 5.88 us -> 2.69 us  [scatter_sum(): lax.ppermute(send, axis, [(i, i ^ step) for i in range(count)])]
    ppermute x4 -> x2, waiting for transfers between devices: 2.61 us -> 0.01 us  [with_halo(): lax.ppermute(head, axis, [((i + 1) % count, i) for i in range(ends)])]
    unnamed x69 -> x60, local copies, waits for them, and re-layouts: 2.03 us -> 4.08 us
  transfers between devices with their start and end apart: 21 -> 17, of which waited for: 5 -> 9; matrix products, arithmetic and copies ran while one was open for 36% -> 38% of each run, Pallas kernels for 0% -> 0%
where the time goes in v3:
time: 172 us; the launch traced here: 169 us
  starting transfers between devices  76.6 us (45%)
  local copies, waits for them, and re-layouts  34.2 us (20%)
  other arithmetic  30.9 us (18%)
  waiting for transfers between devices  13.8 us (8%)
  matrix products  11.9 us (7%)
    ppermute x6, starting transfers between devices, gather_ordered(): other = lax.ppermute(held, axis, [(i, i ^ step) for i in range(count)])  31.7 us
    ppermute x3, starting transfers between devices, scatter_sum(): lax.ppermute(send, axis, [(i, i ^ step) for i in range(count)])  18.4 us
    ppermute x4, starting transfers between devices, from_behind(): return lax.ppermute(block, axis, route)  13.9 us
    ppermute x6, waiting for transfers between devices, gather_ordered(): other = lax.ppermute(held, axis, [(i, i ^ step) for i in range(count)])  10.3 us
    ppermute x2, starting transfers between devices, with_halo(): lax.ppermute(tail, axis, [(i, (i + 1) % count) for i in range(ends)])  9.48 us
    another operation x11, local copies, waits for them, and re-layouts, near_field(): jnp.stack([padded[:, offset_code // 3:offset_code // 3 + box_side, offset...  8.63 us
    dot_general x17, matrix products, product(): return jnp.einsum(form, left, right, preferred_element_type=jnp.float32)  7.96 us
    unnamed x60, local copies, waits for them, and re-layouts  4.08 us
  transfers between devices with their start and end apart: 17, of which 9 were waited for; matrix products, arithmetic and copies ran while one was open for 38% of the time, Pallas kernels for 0%

profile of v3, /device:TPU:1, one launch (start us, length us, event | category | flops | bytes accessed | tf_op | source)
XLA Modules:
  0.0 169.0 jit_solution(2890259635624957095)
XLA Ops:
  3.6 5.6 %collective-permute-start = (bf16[2,2,4,4,4,128]{5,3,4,2,0,1:T(4,128)(2,1)}, bf16[2,2,4,4,4,128]{5,3,4,2,0,1:T(4,128)(2,1)}, u32[]{:S(2)}, u32[]{:S(2)}) collective-permute-start(bf16[2,2,4,4,4,128]{5,3,4,2,0,1:T(4,128)(2,1)} %pad_maximum_fusion.8), channel_id=1, source_target_pairs={{0,8},{8,16},{16,24},{24,32},{32,40},{40,48},{48,56},{56,64},{64,7... | collective-permute-start | bytes 196616 | tf_op jit(solution)/shard_map/ppermute | solution.py:17
  17.3 2.0 %fusion.51 = f32[2,6,6,4,128]{4,3,0,2,1:T(4,128)S(1)} fusion(f32[2,6,6,4,128]{4,3,0,2,1:T(4,128)S(1)} %fusion.74, s32[]{:T(128)} %bitcast.124, s32[]{:T(128)} %bitcast.125, f32[9,2,4,4,4,128]{5,4,1,3,2,0:T(4,128)S(1)} %bitcast.365, pred[]{:T(512)} %and_reduce_fusion), kind=kLoop, calls=%fused_computation.110 | loop fusion | flops 32768 | bytes 196617 | tf_op jit(solution)/shard_map/scatter-add | solution.py:84
  20.1 3.5 %collective-permute-start.13 = (f32[2,6,4,128]{3,2,0,1:T(4,128)}, f32[2,6,4,128]{3,2,0,1:T(4,128)}, u32[]{:S(2)}, u32[]{:S(2)}) collective-permute-start(f32[2,6,4,128]{3,2,0,1:T(4,128)} %slice_bitcast_fusion.43), channel_id=1, source_target_pairs={{0,8},{8,16},{16,24},{24,32},{32,40},{40,48},{48,56},{56,64},{64,7... | collective-permute-start | bytes 73736 | tf_op jit(solution)/shard_map/ppermute | solution.py:29
  30.2 3.0 %constant_dynamic-slice_fusion = (bf16[1,64,8,256]{3,0,2,1:T(2,128)(2,1)S(1)}, bf16[1,64,8,256]{3,0,2,1:T(2,128)(2,1)}) fusion(bf16[2,127,15,256]{3,0,2,1:T(2,128)(2,1)} %param.45, s32[]{:T(128)S(6)} %select_n.153, s32[]{:T(128)S(6)} %select_n.154, s32[]{:T(128)S(6)} %add.266), kind=kLoop, calls=%fused_computation.227 | loop fusion | bytes 1048588 | tf_op jit(solution)/shard_map/slice | solution.py:144
  39.6 1.6 fusion.130
  41.4 2.2 %fusion.1 = f32[16,144,2,2,128]{4,1,3,2,0:T(8,128)S(1)} fusion(s32[16,144]{1,0:T(8,128)S(1)} %fusion.92, f32[1,2,225,128]{3,2,1,0:T(8,128)S(1)} %copy-done.8, f32[1,2,225,128]{3,2,1,0:T(8,128)S(1)} %copy-done.9), kind=kOutput, calls=%fused_computation.8 | convolution fusion | flops 3185683200 | bytes 5188608 | tf_op jit(solution)/shard_map/tnp,sxpq->tnsxq/dot_general | solution.py:175
  43.6 2.7 %slice_bitcast_fusion.1 = (f32[16,144,2,128]{3,1,2,0:T(8,128)}, f32[16,144,2,128]{3,1,2,0:T(8,128)}) fusion(f32[16,144,2,2,128]{4,1,3,2,0:T(8,128)S(1)} %fusion.1), kind=kLoop, calls=%fused_computation.5 | loop fusion | bytes 9437184 | tf_op jit(solution)/shard_map/mul | solution.py:181
  56.8 5.6 %collective-permute-start.15 = (f32[2,4,4,128]{3,2,1,0:T(4,128)S(1)}, f32[2,4,4,128]{3,2,1,0:T(4,128)S(1)}, u32[]{:S(2)}, u32[]{:S(2)}) collective-permute-start(f32[2,4,4,128]{3,2,1,0:T(4,128)S(1)} %slice_bitcast_fusion.46), channel_id=1, source_target_pairs={{0,1},{1,2},{2,3},{3,4},{4,5},{5,6},{6,7},{8,9},{9,10},{10,11},{11... | collective-permute-start | bytes 49160 | tf_op jit(solution)/shard_map/ppermute | solution.py:29
  66.7 3.5 %collective-permute-start.16 = (f32[2,4,4,128]{3,2,1,0:T(4,128)S(1)}, f32[2,4,4,128]{3,2,1,0:T(4,128)S(1)}, u32[]{:S(2)}, u32[]{:S(2)}) collective-permute-start(f32[2,4,4,128]{3,2,1,0:T(4,128)S(1)} %slice_bitcast_fusion.44), channel_id=1, source_target_pairs={{1,0},{2,1},{3,2},{4,3},{5,4},{6,5},{7,6},{9,8},{10,9},{11,10},{12... | collective-permute-start | bytes 49160 | tf_op jit(solution)/shard_map/ppermute | solution.py:29
  71.3 1.9 %collective-permute-start.3 = (bf16[2,2,12,4,4,128]{5,3,4,2,0,1:T(4,128)(2,1)S(1)}, bf16[2,2,12,4,4,128]{5,3,4,2,0,1:T(4,128)(2,1)S(1)}, u32[]{:S(2)}, u32[]{:S(2)}) collective-permute-start(bf16[2,2,12,4,4,128]{5,3,4,2,0,1:T(4,128)(2,1)S(1)} %pad_maximum_fusion.3), channel_id=1, source_target_pairs={{1,0},{2,1},{3,2},{4,3},{5,4},{6,5},{7,6},{9,8},{10,9},{11,10},{12... | collective-permute-start | bytes 589832 | tf_op jit(solution)/shard_map/ppermute | solution.py:19
  73.2 3.9 %collective-permute-start.2 = (bf16[2,2,12,4,4,128]{5,3,4,2,0,1:T(4,128)(2,1)S(1)}, bf16[2,2,12,4,4,128]{5,3,4,2,0,1:T(4,128)(2,1)S(1)}, u32[]{:S(2)}, u32[]{:S(2)}) collective-permute-start(bf16[2,2,12,4,4,128]{5,3,4,2,0,1:T(4,128)(2,1)S(1)} %pad_maximum_fusion.3), channel_id=1, source_target_pairs={{0,1},{1,2},{2,3},{3,4},{4,5},{5,6},{6,7},{8,9},{9,10},{10,11},{11... | collective-permute-start | bytes 589832 | tf_op jit(solution)/shard_map/ppermute | solution.py:17
  83.1 2.6 %collective-permute-start.4 = (bf16[1,2,2,4,256]{4,3,0,1,2:T(4,128)(2,1)S(1)}, bf16[1,2,2,4,256]{4,3,0,1,2:T(4,128)(2,1)S(1)}, u32[]{:S(2)}, u32[]{:S(2)}) collective-permute-start(bf16[1,2,2,4,256]{4,3,0,1,2:T(4,128)(2,1)S(1)} %pad_maximum_fusion.9), channel_id=1, source_target_pairs={{0,8},{8,0},{16,24},{24,16},{32,40},{40,32},{48,56},{56,48},{64,72... | collective-permute-start | bytes 24584 | tf_op jit(solution)/shard_map/ppermute | solution.py:100
  87.5 5.6 %collective-permute-start.5 = (bf16[2,2,2,4,256]{4,3,0,1,2:T(4,128)(2,1)S(1)}, bf16[2,2,2,4,256]{4,3,0,1,2:T(4,128)(2,1)S(1)}, u32[]{:S(2)}, u32[]{:S(2)}) collective-permute-start(bf16[2,2,2,4,256]{4,3,0,1,2:T(4,128)(2,1)S(1)} %maximum_select_fusion.5), channel_id=1, source_target_pairs={{0,16},{8,24},{16,0},{24,8},{32,48},{40,56},{48,32},{56,40},{64,80... | collective-permute-start | bytes 49160 | tf_op jit(solution)/shard_map/ppermute | solution.py:100
  93.1 3.5 %subtract_reduce_fusion = (f32[16,2,4,128]{3,2,1,0:T(4,128)S(1)}, f32[16,2,4,128]{3,2,1,0:T(4,128)S(1)}) fusion(f32[144,2,4,128]{3,0,2,1:T(8,128)S(1)} %copy.499, f32[16,144,2,128]{3,1,2,0:T(8,128)S(1)} %copy-done.3, f32[144,2,4,128]{3,0,2,1:T(8,128)S(1)} %copy.498, f32[16,144,2,128]{3,1,2,0:T(8,128)S(1)} %copy-done.2), kind=kLoop, calls=%fused_computation.1 | loop fusion | flops 18841600 | bytes 6029312 | tf_op jit(solution)/shard_map/reduce_sum | solution.py:181
  96.7 8.8 %collective-permute-start.6 = (bf16[4,2,2,4,256]{4,3,0,1,2:T(4,128)(2,1)S(1)}, bf16[4,2,2,4,256]{4,3,0,1,2:T(4,128)(2,1)S(1)}, u32[]{:S(2)}, u32[]{:S(2)}) collective-permute-start(bf16[4,2,2,4,256]{4,3,0,1,2:T(4,128)(2,1)S(1)} %maximum_select_fusion.4), channel_id=1, source_target_pairs={{0,32},{8,40},{16,48},{24,56},{32,0},{40,8},{48,16},{56,24},{64,96... | collective-permute-start | bytes 98312 | tf_op jit(solution)/shard_map/ppermute | solution.py:100
  105.5 3.9 %collective-permute-done.6 = bf16[4,2,2,4,256]{4,3,0,1,2:T(4,128)(2,1)S(1)} collective-permute-done((bf16[4,2,2,4,256]{4,3,0,1,2:T(4,128)(2,1)S(1)}, bf16[4,2,2,4,256]{4,3,0,1,2:T(4,128)(2,1)S(1)}, u32[]{:S(2)}, u32[]{:S(2)}) %collective-permute-start.6) | collective-permute-done | bytes 32800 | tf_op jit(solution)/shard_map/ppermute | solution.py:100
  110.1 7.1 %collective-permute-start.7 = (bf16[8,2,2,4,256]{4,3,0,1,2:T(4,128)(2,1)}, bf16[8,2,2,4,256]{4,3,0,1,2:T(4,128)(2,1)}, u32[]{:S(2)}, u32[]{:S(2)}) collective-permute-start(bf16[8,2,2,4,256]{4,3,0,1,2:T(4,128)(2,1)} %maximum_select_fusion.3), channel_id=1, source_target_pairs={{0,64},{8,72},{16,80},{24,88},{32,96},{40,104},{48,112},{56,120},{... | collective-permute-start | bytes 196616 | tf_op jit(solution)/shard_map/ppermute | solution.py:100
  122.7 3.1 %stack.181 = bf16[9,2,4,4,4,128]{5,0,4,1,3,2:T(8,128)(2,1)} concatenate(bf16[1,2,4,4,4,128]{5,0,4,1,3,2:T(2,128)(2,1)} %copy.479, bf16[1,2,4,4,4,128]{5,0,4,1,3,2:T(2,128)(2,1)} %copy.480, bf16[1,2,4,4,4,128]{5,0,4,1,3,2:T(2,128)(2,1)} %copy.481, bf16[1,2,4,4,4,128]{5,0,4,1,3,2:T(2,128)(2,1)} %copy.482, bf16[1,2,4,4,4,128]{5,0,4,1,3,2:T(2,128)(2,1)} %copy.483, ...), dimensions={0} | concatenate | bytes 589824 | tf_op jit(solution)/shard_map/stack | solution.py:50
  126.9 3.1 %collective-permute-start.8 = (bf16[16,2,2,4,256]{4,3,0,1,2:T(4,128)(2,1)S(1)}, bf16[16,2,2,4,256]{4,3,0,1,2:T(4,128)(2,1)S(1)}, u32[]{:S(2)}, u32[]{:S(2)}) collective-permute-start(bf16[16,2,2,4,256]{4,3,0,1,2:T(4,128)(2,1)S(1)} %maximum_select_fusion.2), channel_id=1, source_target_pairs={{0,128},{8,136},{16,144},{24,152},{32,160},{40,168},{48,176},{56,1... | collective-permute-start | bytes 393224 | tf_op jit(solution)/shard_map/ppermute | solution.py:100
  132.8 4.6 %collective-permute-start.9 = (bf16[32,2,2,4,256]{4,3,0,1,2:T(4,128)(2,1)S(1)}, bf16[32,2,2,4,256]{4,3,0,1,2:T(4,128)(2,1)S(1)}, u32[]{:S(2)}, u32[]{:S(2)}) collective-permute-start(bf16[32,2,2,4,256]{4,3,0,1,2:T(4,128)(2,1)S(1)} %maximum_select_fusion.1), channel_id=1, source_target_pairs={{0,256},{8,264},{16,272},{24,280},{32,288},{40,296},{48,304},{56,3... | collective-permute-start | bytes 786440 | tf_op jit(solution)/shard_map/ppermute | solution.py:100
  137.8 3.8 %collective-permute-done.9 = bf16[32,2,2,4,256]{4,3,0,1,2:T(4,128)(2,1)S(1)} collective-permute-done((bf16[32,2,2,4,256]{4,3,0,1,2:T(4,128)(2,1)S(1)}, bf16[32,2,2,4,256]{4,3,0,1,2:T(4,128)(2,1)S(1)}, u32[]{:S(2)}, u32[]{:S(2)}) %collective-permute-start.9) | collective-permute-done | bytes 262176 | tf_op jit(solution)/shard_map/ppermute | solution.py:100
  143.8 5.4 %collective-permute-start.10 = (f32[4,2,2,4,256]{4,0,3,1,2:T(4,128)S(1)}, f32[4,2,2,4,256]{4,0,3,1,2:T(4,128)S(1)}, u32[]{:S(2)}, u32[]{:S(2)}) collective-permute-start(f32[4,2,2,4,256]{4,0,3,1,2:T(4,128)S(1)} %slice_select_fusion), channel_id=1, source_target_pairs={{0,4},{1,5},{2,6},{3,7},{4,0},{5,1},{6,2},{7,3},{8,12},{9,13},{10,... | collective-permute-start | bytes 196616 | tf_op jit(solution)/shard_map/ppermute | solution.py:119
  150.8 3.2 %collective-permute-start.11 = (f32[2,2,2,4,256]{4,0,3,1,2:T(2,128)S(1)}, f32[2,2,2,4,256]{4,0,3,1,2:T(2,128)S(1)}, u32[]{:S(2)}, u32[]{:S(2)}) collective-permute-start(f32[2,2,2,4,256]{4,0,3,1,2:T(2,128)S(1)} %broadcast_select_fusion), channel_id=1, source_target_pairs={{0,2},{1,3},{2,0},{3,1},{4,6},{5,7},{6,4},{7,5},{8,10},{9,11},{10,... | collective-permute-start | bytes 98312 | tf_op jit(solution)/shard_map/ppermute | solution.py:119
  155.6 9.8 %collective-permute-start.12 = (f32[1,2,2,4,256]{4,0,3,1,2:T(1,128)S(1)}, f32[1,2,2,4,256]{4,0,3,1,2:T(1,128)S(1)}, u32[]{:S(2)}, u32[]{:S(2)}) collective-permute-start(f32[1,2,2,4,256]{4,0,3,1,2:T(1,128)S(1)} %broadcast_select_fusion.1), channel_id=1, source_target_pairs={{0,1},{1,0},{2,3},{3,2},{4,5},{5,4},{6,7},{7,6},{8,9},{9,8},{10,11... | collective-permute-start | bytes 49160 | tf_op jit(solution)/shard_map/ppermute | solution.py:119
  (195 shorter events, 67.6 us)
Async XLA Ops:
  0.6 81.9 %copy-start = (f32[256,128]{1,0:T(8,128)S(1)}, f32[256,128]{1,0:T(8,128)}, u32[]{:S(2)}) copy-start(f32[256,128]{1,0:T(8,128)} %param.42) | copy-start | bytes 393220
  0.6 12.9 %copy-start.15 = (bf16[2,4,4,4,128]{4,3,2,1,0:T(4,128)(2,1)S(1)}, bf16[2,4,4,4,128]{4,3,2,1,0:T(4,128)(2,1)}, u32[]{:S(2)}) copy-start(bf16[2,4,4,4,128]{4,3,2,1,0:T(4,128)(2,1)} %param.37) | copy-start | bytes 98308
  0.7 12.9 %copy-start.1 = (bf16[2,4,4,2,128,128]{5,4,3,2,1,0:T(8,128)(2,1)S(1)}, bf16[2,4,4,2,128,128]{5,4,3,2,1,0:T(8,128)(2,1)}, u32[]{:S(2)}) copy-start(bf16[2,4,4,2,128,128]{5,4,3,2,1,0:T(8,128)(2,1)} %param.39) | copy-start | bytes 6291460
  2.3 67.9 %collective-permute-start.1 = (bf16[2,2,4,4,4,128]{5,3,4,2,0,1:T(4,128)(2,1)}, bf16[2,2,4,4,4,128]{5,3,4,2,0,1:T(4,128)(2,1)}, u32[]{:S(2)}, u32[]{:S(2)}) collective-permute-start(bf16[2,2,4,4,4,128]{5,3,4,2,0,1:T(4,128)(2,1)} %pad_maximum_fusion.8), channel_id=1, source_target_pairs={{8,0},{16,8},{24,16},{32,24},{40,32},{48,40},{56,48},{64,56},{72,6... | collective-permute-start | bytes 196616 | tf_op jit(solution)/shard_map/ppermute | solution.py:19
  3.6 66.6 %collective-permute-start = (bf16[2,2,4,4,4,128]{5,3,4,2,0,1:T(4,128)(2,1)}, bf16[2,2,4,4,4,128]{5,3,4,2,0,1:T(4,128)(2,1)}, u32[]{:S(2)}, u32[]{:S(2)}) collective-permute-start(bf16[2,2,4,4,4,128]{5,3,4,2,0,1:T(4,128)(2,1)} %pad_maximum_fusion.8), channel_id=1, source_target_pairs={{0,8},{8,16},{16,24},{24,32},{32,40},{40,48},{48,56},{56,64},{64,7... | collective-permute-start | bytes 196616 | tf_op jit(solution)/shard_map/ppermute | solution.py:17
  15.0 13.2 %copy-start.10 = (f32[2,15,15,128]{3,0,2,1:T(2,128)S(1)}, f32[2,15,15,128]{3,0,2,1:T(2,128)}, u32[]{:S(2)}) copy-start(f32[2,15,15,128]{3,0,2,1:T(2,128)} %param.44) | copy-start | bytes 691204
  20.1 29.7 %collective-permute-start.13 = (f32[2,6,4,128]{3,2,0,1:T(4,128)}, f32[2,6,4,128]{3,2,0,1:T(4,128)}, u32[]{:S(2)}, u32[]{:S(2)}) collective-permute-start(f32[2,6,4,128]{3,2,0,1:T(4,128)} %slice_bitcast_fusion.43), channel_id=1, source_target_pairs={{0,8},{8,16},{16,24},{24,32},{32,40},{40,48},{48,56},{56,64},{64,7... | collective-permute-start | bytes 73736 | tf_op jit(solution)/shard_map/ppermute | solution.py:29
  51.1 4.9 %collective-permute-start.14 = (f32[2,6,4,128]{3,2,0,1:T(4,128)}, f32[2,6,4,128]{3,2,0,1:T(4,128)}, u32[]{:S(2)}, u32[]{:S(2)}) collective-permute-start(f32[2,6,4,128]{3,2,0,1:T(4,128)} %slice_bitcast_fusion.41), channel_id=1, source_target_pairs={{8,0},{16,8},{24,16},{32,24},{40,32},{48,40},{56,48},{64,56},{72,6... | collective-permute-start | bytes 73736 | tf_op jit(solution)/shard_map/ppermute | solution.py:29
  56.8 7.9 %collective-permute-start.15 = (f32[2,4,4,128]{3,2,1,0:T(4,128)S(1)}, f32[2,4,4,128]{3,2,1,0:T(4,128)S(1)}, u32[]{:S(2)}, u32[]{:S(2)}) collective-permute-start(f32[2,4,4,128]{3,2,1,0:T(4,128)S(1)} %slice_bitcast_fusion.46), channel_id=1, source_target_pairs={{0,1},{1,2},{2,3},{3,4},{4,5},{5,6},{6,7},{8,9},{9,10},{10,11},{11... | collective-permute-start | bytes 49160 | tf_op jit(solution)/shard_map/ppermute | solution.py:29
  64.6 18.4 %copy-start.16 = (f32[4,4,256]{2,1,0:T(4,128)}, f32[4,4,256]{2,1,0:T(4,128)S(1)}, u32[]{:S(2)}) copy-start(f32[4,4,256]{2,1,0:T(4,128)S(1)} %sin.11) | copy-start | bytes 49156
  66.7 11.3 %collective-permute-start.16 = (f32[2,4,4,128]{3,2,1,0:T(4,128)S(1)}, f32[2,4,4,128]{3,2,1,0:T(4,128)S(1)}, u32[]{:S(2)}, u32[]{:S(2)}) collective-permute-start(f32[2,4,4,128]{3,2,1,0:T(4,128)S(1)} %slice_bitcast_fusion.44), channel_id=1, source_target_pairs={{1,0},{2,1},{3,2},{4,3},{5,4},{6,5},{7,6},{9,8},{10,9},{11,10},{12... | collective-permute-start | bytes 49160 | tf_op jit(solution)/shard_map/ppermute | solution.py:29
  71.3 7.5 %collective-permute-start.3 = (bf16[2,2,12,4,4,128]{5,3,4,2,0,1:T(4,128)(2,1)S(1)}, bf16[2,2,12,4,4,128]{5,3,4,2,0,1:T(4,128)(2,1)S(1)}, u32[]{:S(2)}, u32[]{:S(2)}) collective-permute-start(bf16[2,2,12,4,4,128]{5,3,4,2,0,1:T(4,128)(2,1)S(1)} %pad_maximum_fusion.3), channel_id=1, source_target_pairs={{1,0},{2,1},{3,2},{4,3},{5,4},{6,5},{7,6},{9,8},{10,9},{11,10},{12... | collective-permute-start | bytes 589832 | tf_op jit(solution)/shard_map/ppermute | solution.py:19
  73.2 6.2 %collective-permute-start.2 = (bf16[2,2,12,4,4,128]{5,3,4,2,0,1:T(4,128)(2,1)S(1)}, bf16[2,2,12,4,4,128]{5,3,4,2,0,1:T(4,128)(2,1)S(1)}, u32[]{:S(2)}, u32[]{:S(2)}) collective-permute-start(bf16[2,2,12,4,4,128]{5,3,4,2,0,1:T(4,128)(2,1)S(1)} %pad_maximum_fusion.3), channel_id=1, source_target_pairs={{0,1},{1,2},{2,3},{3,4},{4,5},{5,6},{6,7},{8,9},{9,10},{10,11},{11... | collective-permute-start | bytes 589832 | tf_op jit(solution)/shard_map/ppermute | solution.py:17
  83.1 4.4 %collective-permute-start.4 = (bf16[1,2,2,4,256]{4,3,0,1,2:T(4,128)(2,1)S(1)}, bf16[1,2,2,4,256]{4,3,0,1,2:T(4,128)(2,1)S(1)}, u32[]{:S(2)}, u32[]{:S(2)}) collective-permute-start(bf16[1,2,2,4,256]{4,3,0,1,2:T(4,128)(2,1)S(1)} %pad_maximum_fusion.9), channel_id=1, source_target_pairs={{0,8},{8,0},{16,24},{24,16},{32,40},{40,32},{48,56},{56,48},{64,72... | collective-permute-start | bytes 24584 | tf_op jit(solution)/shard_map/ppermute | solution.py:100
  87.5 9.1 %collective-permute-start.5 = (bf16[2,2,2,4,256]{4,3,0,1,2:T(4,128)(2,1)S(1)}, bf16[2,2,2,4,256]{4,3,0,1,2:T(4,128)(2,1)S(1)}, u32[]{:S(2)}, u32[]{:S(2)}) collective-permute-start(bf16[2,2,2,4,256]{4,3,0,1,2:T(4,128)(2,1)S(1)} %maximum_select_fusion.5), channel_id=1, source_target_pairs={{0,16},{8,24},{16,0},{24,8},{32,48},{40,56},{48,32},{56,40},{64,80... | collective-permute-start | bytes 49160 | tf_op jit(solution)/shard_map/ppermute | solution.py:100
  96.7 12.7 %collective-permute-start.6 = (bf16[4,2,2,4,256]{4,3,0,1,2:T(4,128)(2,1)S(1)}, bf16[4,2,2,4,256]{4,3,0,1,2:T(4,128)(2,1)S(1)}, u32[]{:S(2)}, u32[]{:S(2)}) collective-permute-start(bf16[4,2,2,4,256]{4,3,0,1,2:T(4,128)(2,1)S(1)} %maximum_select_fusion.4), channel_id=1, source_target_pairs={{0,32},{8,40},{16,48},{24,56},{32,0},{40,8},{48,16},{56,24},{64,96... | collective-permute-start | bytes 98312 | tf_op jit(solution)/shard_map/ppermute | solution.py:100
  110.1 15.7 %collective-permute-start.7 = (bf16[8,2,2,4,256]{4,3,0,1,2:T(4,128)(2,1)}, bf16[8,2,2,4,256]{4,3,0,1,2:T(4,128)(2,1)}, u32[]{:S(2)}, u32[]{:S(2)}) collective-permute-start(bf16[8,2,2,4,256]{4,3,0,1,2:T(4,128)(2,1)} %maximum_select_fusion.3), channel_id=1, source_target_pairs={{0,64},{8,72},{16,80},{24,88},{32,96},{40,104},{48,112},{56,120},{... | collective-permute-start | bytes 196616 | tf_op jit(solution)/shard_map/ppermute | solution.py:100
  126.9 5.7 %collective-permute-start.8 = (bf16[16,2,2,4,256]{4,3,0,1,2:T(4,128)(2,1)S(1)}, bf16[16,2,2,4,256]{4,3,0,1,2:T(4,128)(2,1)S(1)}, u32[]{:S(2)}, u32[]{:S(2)}) collective-permute-start(bf16[16,2,2,4,256]{4,3,0,1,2:T(4,128)(2,1)S(1)} %maximum_select_fusion.2), channel_id=1, source_target_pairs={{0,128},{8,136},{16,144},{24,152},{32,160},{40,168},{48,176},{56,1... | collective-permute-start | bytes 393224 | tf_op jit(solution)/shard_map/ppermute | solution.py:100
  132.8 8.8 %collective-permute-start.9 = (bf16[32,2,2,4,256]{4,3,0,1,2:T(4,128)(2,1)S(1)}, bf16[32,2,2,4,256]{4,3,0,1,2:T(4,128)(2,1)S(1)}, u32[]{:S(2)}, u32[]{:S(2)}) collective-permute-start(bf16[32,2,2,4,256]{4,3,0,1,2:T(4,128)(2,1)S(1)} %maximum_select_fusion.1), channel_id=1, source_target_pairs={{0,256},{8,264},{16,272},{24,280},{32,288},{40,296},{48,304},{56,3... | collective-permute-start | bytes 786440 | tf_op jit(solution)/shard_map/ppermute | solution.py:100
  143.8 7.0 %collective-permute-start.10 = (f32[4,2,2,4,256]{4,0,3,1,2:T(4,128)S(1)}, f32[4,2,2,4,256]{4,0,3,1,2:T(4,128)S(1)}, u32[]{:S(2)}, u32[]{:S(2)}) collective-permute-start(f32[4,2,2,4,256]{4,0,3,1,2:T(4,128)S(1)} %slice_select_fusion), channel_id=1, source_target_pairs={{0,4},{1,5},{2,6},{3,7},{4,0},{5,1},{6,2},{7,3},{8,12},{9,13},{10,... | collective-permute-start | bytes 196616 | tf_op jit(solution)/shard_map/ppermute | solution.py:119
  149.1 17.1 %copy-start.17 = (f32[4,4,256]{2,1,0:T(4,128)S(1)}, f32[4,4,256]{2,1,0:T(4,128)}, u32[]{:S(2)}) copy-start(f32[4,4,256]{2,1,0:T(4,128)} %copy-done.16) | copy-start | bytes 49156
  149.5 17.3 %copy-start.7 = (bf16[1,2,128,128]{3,2,0,1:T(8,128)(2,1)S(1)}, bf16[1,2,128,128]{3,2,0,1:T(8,128)(2,1)}, u32[]{:S(2)}) copy-start(bf16[1,2,128,128]{3,2,0,1:T(8,128)(2,1)} %maximum_bitcast_fusion.6) | copy-start | bytes 196612
  150.8 4.7 %collective-permute-start.11 = (f32[2,2,2,4,256]{4,0,3,1,2:T(2,128)S(1)}, f32[2,2,2,4,256]{4,0,3,1,2:T(2,128)S(1)}, u32[]{:S(2)}, u32[]{:S(2)}) collective-permute-start(f32[2,2,2,4,256]{4,0,3,1,2:T(2,128)S(1)} %broadcast_select_fusion), channel_id=1, source_target_pairs={{0,2},{1,3},{2,0},{3,1},{4,6},{5,7},{6,4},{7,5},{8,10},{9,11},{10,... | collective-permute-start | bytes 98312 | tf_op jit(solution)/shard_map/ppermute | solution.py:119
  155.6 10.6 %collective-permute-start.12 = (f32[1,2,2,4,256]{4,0,3,1,2:T(1,128)S(1)}, f32[1,2,2,4,256]{4,0,3,1,2:T(1,128)S(1)}, u32[]{:S(2)}, u32[]{:S(2)}) collective-permute-start(f32[1,2,2,4,256]{4,0,3,1,2:T(1,128)S(1)} %broadcast_select_fusion.1), channel_id=1, source_target_pairs={{0,1},{1,0},{2,3},{3,2},{4,5},{5,4},{6,7},{7,6},{8,9},{9,8},{10,11... | collective-permute-start | bytes 49160 | tf_op jit(solution)/shard_map/ppermute | solution.py:119
  (20 other events, 101.9 us)

commit v4 on v3

--- a/solution.py
+++ b/solution.py
@@ -42,8 +42,8 @@
     return jnp.einsum(form, left, right, preferred_element_type=jnp.float32)
 
 
-def near_field(padded, current, probe, near_list, near_blocks):
-    box_side = current.shape[1]
+def near_forward(padded, near_list, near_blocks):
+    box_side = padded.shape[1] - 2
     one_hot = (near_list[..., None] == jnp.arange(9)).astype(jnp.bfloat16)
     blocks_re = near_blocks[0]
     blocks_im = near_blocks[1]
@@ -64,7 +64,14 @@
     fwd_im = product("rckpq,krcmq->rcmp", blocks_re, picked[1]) + product(
         "rckpq,krcmq->rcmp", blocks_im, picked[0]
     )
-    near_fwd = jnp.stack([fwd_re, fwd_im])
+    return jnp.stack([fwd_re, fwd_im])
+
+
+def near_adjoint_local(probe, near_list, near_blocks):
+    box_side = probe.shape[1]
+    one_hot = (near_list[..., None] == jnp.arange(9)).astype(jnp.bfloat16)
+    blocks_re = near_blocks[0]
+    blocks_im = near_blocks[1]
     back_re = product("rckpq,rcmp->krcmq", blocks_re, probe[0]) + product(
         "rckpq,rcmp->krcmq", blocks_im, probe[1]
     )
@@ -82,13 +89,45 @@
             offset_code // 3 : offset_code // 3 + box_side,
             offset_code % 3 : offset_code % 3 + box_side,
         ].add(placed_all[offset_code])
-    for step_dir, send_row, keep_row in ((1, box_side + 1, 1), (-1, 0, box_side)):
-        arrived = from_behind(placed[:, send_row], "row", step_dir)
-        placed = placed.at[:, keep_row].add(arrived)
-    for step_dir, send_col, keep_col in ((1, box_side + 1, 1), (-1, 0, box_side)):
-        arrived = from_behind(placed[:, 1 : box_side + 1, send_col], "col", step_dir)
-        placed = placed.at[:, 1 : box_side + 1, keep_col].add(arrived)
-    return (near_fwd, placed[:, 1 : box_side + 1, 1 : box_side + 1])
+    return placed
+
+
+def exchange_halo(vectors, placed):
+    box_side = vectors.shape[2]
+    lanes = vectors.shape[-1]
+    cells = vectors.astype(jnp.float32)
+    for axis, dim in (("row", 2), ("col", 3)):
+        count = lax.axis_size(axis)
+        ahead = [(i, i + 1) for i in range(count - 1)]
+        behind = [(i + 1, i) for i in range(count - 1)]
+        flat = cells.reshape(-1, lanes)
+        size = flat.shape[0]
+        if axis == "row":
+            to_next = placed[:, box_side + 1]
+            to_prev = placed[:, 0]
+        else:
+            to_next = placed[:, 1 : box_side + 1, box_side + 1]
+            to_prev = placed[:, 1 : box_side + 1, 0]
+        edge_shape = to_next.shape
+        from_prev = lax.ppermute(
+            jnp.concatenate([flat, to_next.reshape(-1, lanes)]), axis, ahead
+        )
+        from_next = lax.ppermute(
+            jnp.concatenate([flat, to_prev.reshape(-1, lanes)]), axis, behind
+        )
+        if axis == "row":
+            placed = placed.at[:, 1].add(from_prev[size:].reshape(edge_shape))
+            placed = placed.at[:, box_side].add(from_next[size:].reshape(edge_shape))
+        else:
+            placed = placed.at[:, 1 : box_side + 1, 1].add(from_prev[size:].reshape(edge_shape))
+            placed = placed.at[:, 1 : box_side + 1, box_side].add(
+                from_next[size:].reshape(edge_shape)
+            )
+        cells = jnp.concatenate(
+            [from_prev[:size].reshape(cells.shape), cells, from_next[:size].reshape(cells.shape)],
+            axis=dim,
+        )
+    return cells.astype(jnp.bfloat16), placed[:, 1 : box_side + 1, 1 : box_side + 1]
 
 
 def gather_ordered(block, axis):
@@ -235,9 +274,10 @@
     coarse_table,
 ):
     box_side = current.shape[1]
-    vectors = with_halo(jnp.stack([current, probe]), (("row", 2), ("col", 3)), box_side)
+    placed = near_adjoint_local(probe, near_list, near_blocks)
+    vectors, near_adj = exchange_halo(jnp.stack([current, probe]), placed)
     padded = vectors[0][:, box_side - 1 : 2 * box_side + 1, box_side - 1 : 2 * box_side + 1]
-    near_fwd, near_adj = near_field(padded, current, probe, near_list, near_blocks)
+    near_fwd = near_forward(padded, near_list, near_blocks)
     fwd_set = (radiation, reception, leaf_table, coarse_table)
     adj_set = (
         jnp.stack([reception[0].T, -reception[1].T]),

time: 172 us -> 162 us (0.942)
  starting transfers between devices: 76.6 us -> 68.9 us
  waiting for transfers between devices: 13.8 us -> 21.1 us
  other arithmetic: 30.9 us -> 24.2 us
  local copies, waits for them, and re-layouts: 34.2 us -> 32 us
    ppermute x8 -> x4, starting transfers between devices: 26.6 us -> 14.7 us  [the longest x2 10.5 us: exchange_halo(): lax.ppermute(jnp.concatenate([flat, to_next.reshape(-1, lanes)]), axis, a...]
    ppermute x8 -> x4, waiting for transfers between devices: 0.81 us -> 5.67 us  [the longest x2 5.1 us: exchange_halo(): lax.ppermute(jnp.concatenate([flat, to_prev.reshape(-1, lanes)]), axis, b...]
    ppermute x6, starting transfers between devices: 31.7 us -> 36.3 us  [gather_ordered(): other = lax.ppermute(held, axis, [(i, i ^ step) for i in range(count)])]
    scatter-add x12 -> x11, other arithmetic: 6.94 us -> 3.41 us  [the longest x8 3.36 us: near_adjoint_local(): placed = placed.at[:, offset_code // 3:offset_code // 3 + box_side, offse...]
    slice x0 -> x16, local copies, waits for them, and re-layouts: none -> 3.12 us  [the longest x2 1.08 us: exchange_halo(): from_prev[:size].reshape(cells.shape)]
    ppermute x6, waiting for transfers between devices: 10.3 us -> 12.5 us  [gather_ordered(): other = lax.ppermute(held, axis, [(i, i ^ step) for i in range(count)])]
    squeeze x5 -> x1, local copies, waits for them, and re-layouts: 1.97 us -> 0.05 us  [near_forward(): picked[0]]
    unnamed x60 -> x96, local copies, waits for them, and re-layouts: 4.08 us -> 2.66 us
  transfers between devices with their start and end apart: 17 -> 13, of which waited for: 9 -> 10; matrix products, arithmetic and copies ran while one was open for 38% -> 29% of each run, Pallas kernels for 0% -> 0%
where the time goes in v4:
time: 162 us; the launch traced here: 160 us
  starting transfers between devices  68.9 us (43%)
  local copies, waits for them, and re-layouts  32 us (20%)
  other arithmetic  24.2 us (15%)
  waiting for transfers between devices  21.1 us (13%)
  matrix products  12.1 us (7%)
  between operations  1.88 us (1%)
    ppermute x6, starting transfers between devices, gather_ordered(): other = lax.ppermute(held, axis, [(i, i ^ step) for i in range(count)])  36.3 us
    ppermute x3, starting transfers between devices, scatter_sum(): lax.ppermute(send, axis, [(i, i ^ step) for i in range(count)])  17.9 us
    ppermute x6, waiting for transfers between devices, gather_ordered(): other = lax.ppermute(held, axis, [(i, i ^ step) for i in range(count)])  12.5 us
    ppermute x2, starting transfers between devices, exchange_halo(): lax.ppermute(jnp.concatenate([flat, to_next.reshape(-1, lanes)]), axis, a...  10.5 us
    dot_general x17, matrix products, product(): return jnp.einsum(form, left, right, preferred_element_type=jnp.float32)  8.12 us
    another operation x11, local copies, waits for them, and re-layouts, near_forward(): jnp.stack([padded[:, offset_code // 3:offset_code // 3 + box_side, offset...  7.98 us
    ppermute x2, waiting for transfers between devices, exchange_halo(): lax.ppermute(jnp.concatenate([flat, to_prev.reshape(-1, lanes)]), axis, b...  5.1 us
    ppermute x2, starting transfers between devices, exchange_halo(): lax.ppermute(jnp.concatenate([flat, to_prev.reshape(-1, lanes)]), axis, b...  4.23 us
  transfers between devices with their start and end apart: 13, of which 10 were waited for; matrix products, arithmetic and copies ran while one was open for 29% of the time, Pallas kernels for 0%

profile of v4, /device:TPU:1, one launch (start us, length us, event | category | flops | bytes accessed | tf_op | source)
XLA Modules:
  0.0 160.2 jit_solution(1977681702010136342)
XLA Ops:
  0.7 1.6 %fusion.24 = f32[4,4,4,2,128]{4,2,3,1,0:T(4,128)S(1)} fusion(bf16[2,4,4,2,128,128]{5,4,3,2,1,0:T(8,128)(2,1)} %param.39, bf16[2,4,4,4,128]{4,3,2,1,0:T(4,128)(2,1)} %param.37), kind=kOutput, calls=%fused_computation.49 | convolution fusion | flops 4194304 | bytes 1130496 | tf_op jit(solution)/shard_map/rckpq,rcmp->krcmq/dot_general | solution.py:42
  9.4 1.8 %fusion.50 = f32[2,6,6,4,128]{4,3,0,2,1:T(4,128)S(1)} fusion(f32[2,6,6,4,128]{4,3,0,2,1:T(4,128)S(1)} %add_dynamic-update-slice_fusion, s32[]{:T(128)} %bitcast.24, s32[]{:T(128)} %bitcast.25, f32[2,4,4,4,128]{4,3,0,2,1:T(4,128)S(1)} %bitcast.348, pred[]{:T(512)} %and_reduce_fusion), kind=kLoop, calls=%fused_computation.115 | loop fusion | flops 32768 | bytes 196617 | tf_op jit(solution)/shard_map/scatter-add | solution.py:91
  12.1 5.0 %collective-permute-start = (f32[304,128]{1,0:T(8,128)}, f32[304,128]{1,0:T(8,128)}, u32[]{:S(2)}, u32[]{:S(2)}) collective-permute-start(f32[304,128]{1,0:T(8,128)} %pad_maximum_fusion.7), channel_id=1, source_target_pairs={{0,8},{8,16},{16,24},{24,32},{32,40},{40,48},{48,56},{56,64},{64,7... | collective-permute-start | bytes 466952 | tf_op jit(solution)/shard_map/ppermute | solution.py:112
  25.0 2.9 %constant_dynamic-slice_fusion.2 = (bf16[1,64,8,256]{3,0,2,1:T(2,128)(2,1)S(1)}, bf16[1,64,8,256]{3,0,2,1:T(2,128)(2,1)}) fusion(bf16[2,127,15,256]{3,0,2,1:T(2,128)(2,1)} %param.45, s32[]{:T(128)S(6)} %select_n.153, s32[]{:T(128)S(6)} %select_n.154, s32[]{:T(128)S(6)} %add.266), kind=kLoop, calls=%fused_computation.218 | loop fusion | bytes 1048588 | tf_op jit(solution)/shard_map/slice | solution.py:183
  34.3 2.9 %fusion.120 = (f32[2,1,64,8,256]{4,1,3,2,0:T(1,128)}, f32[2,1,64,8,256]{4,1,3,2,0:T(1,128)}) fusion(f32[2,2,64,8,256]{4,1,3,2,0:T(2,128)S(1)} %maximum_convert_fusion), kind=kLoop, calls=%fused_computation.249 | loop fusion | bytes 4194304 | tf_op jit(solution)/shard_map/slice | solution.py:189
  37.4 2.2 %fusion.1 = f32[16,144,2,2,128]{4,1,3,2,0:T(8,128)S(1)} fusion(s32[16,144]{1,0:T(8,128)S(1)} %fusion.82, f32[1,2,225,128]{3,2,1,0:T(8,128)S(1)} %copy-done.14, f32[1,2,225,128]{3,2,1,0:T(8,128)S(1)} %copy-done.15), kind=kOutput, calls=%fused_computation.8 | convolution fusion | flops 3185683200 | bytes 5188608 | tf_op jit(solution)/shard_map/tnp,sxpq->tnsxq/dot_general | solution.py:214
  39.7 2.7 %slice_bitcast_fusion.1 = (f32[16,144,2,128]{3,1,2,0:T(8,128)}, f32[16,144,2,128]{3,1,2,0:T(8,128)}) fusion(f32[16,144,2,2,128]{4,1,3,2,0:T(8,128)S(1)} %fusion.1), kind=kLoop, calls=%fused_computation.5 | loop fusion | bytes 9437184 | tf_op jit(solution)/shard_map/mul | solution.py:220
  49.7 5.4 %collective-permute-start.2 = (f32[800,128]{1,0:T(8,128)S(1)}, f32[800,128]{1,0:T(8,128)S(1)}, u32[]{:S(2)}, u32[]{:S(2)}) collective-permute-start(f32[800,128]{1,0:T(8,128)S(1)} %get-tuple-element.216), channel_id=1, source_target_pairs={{0,1},{1,2},{2,3},{3,4},{4,5},{5,6},{6,7},{8,9},{9,10},{10,11},{11... | collective-permute-start | bytes 1228808 | tf_op jit(solution)/shard_map/ppermute | solution.py:112
  55.1 2.9 %collective-permute-start.3 = (f32[800,128]{1,0:T(8,128)S(1)}, f32[800,128]{1,0:T(8,128)S(1)}, u32[]{:S(2)}, u32[]{:S(2)}) collective-permute-start(f32[800,128]{1,0:T(8,128)S(1)} %get-tuple-element.217), channel_id=1, source_target_pairs={{1,0},{2,1},{3,2},{4,3},{5,4},{6,5},{7,6},{9,8},{10,9},{11,10},{12... | collective-permute-start | bytes 1228808 | tf_op jit(solution)/shard_map/ppermute | solution.py:115
  60.1 4.3 %collective-permute-done.3 = f32[800,128]{1,0:T(8,128)S(1)} collective-permute-done((f32[800,128]{1,0:T(8,128)S(1)}, f32[800,128]{1,0:T(8,128)S(1)}, u32[]{:S(2)}, u32[]{:S(2)}) %collective-permute-start.3) | collective-permute-done | bytes 409632 | tf_op jit(solution)/shard_map/ppermute | solution.py:115
  67.7 3.4 %collective-permute-start.4 = (bf16[1,2,2,4,256]{4,3,0,1,2:T(4,128)(2,1)S(1)}, bf16[1,2,2,4,256]{4,3,0,1,2:T(4,128)(2,1)S(1)}, u32[]{:S(2)}, u32[]{:S(2)}) collective-permute-start(bf16[1,2,2,4,256]{4,3,0,1,2:T(4,128)(2,1)S(1)} %pad_maximum_fusion.12), channel_id=1, source_target_pairs={{0,8},{8,0},{16,24},{24,16},{32,40},{40,32},{48,56},{56,48},{64,72... | collective-permute-start | bytes 24584 | tf_op jit(solution)/shard_map/ppermute | solution.py:139
  71.3 4.1 %subtract_reduce_fusion = (f32[16,2,4,128]{3,2,1,0:T(4,128)}, f32[16,2,4,128]{3,2,1,0:T(4,128)}) fusion(f32[144,2,4,128]{3,0,2,1:T(8,128)S(1)} %copy.715, f32[16,144,2,128]{3,1,2,0:T(8,128)S(1)} %copy-done.3, f32[144,2,4,128]{3,0,2,1:T(8,128)S(1)} %copy.714, f32[16,144,2,128]{3,1,2,0:T(8,128)S(1)} %copy-done.2), kind=kLoop, calls=%fused_computation.1 | loop fusion | flops 18841600 | bytes 6029312 | tf_op jit(solution)/shard_map/reduce_sum | solution.py:220
  76.0 7.1 %collective-permute-start.5 = (bf16[2,2,2,4,256]{4,3,0,1,2:T(4,128)(2,1)}, bf16[2,2,2,4,256]{4,3,0,1,2:T(4,128)(2,1)}, u32[]{:S(2)}, u32[]{:S(2)}) collective-permute-start(bf16[2,2,2,4,256]{4,3,0,1,2:T(4,128)(2,1)} %maximum_select_fusion.5), channel_id=1, source_target_pairs={{0,16},{8,24},{16,0},{24,8},{32,48},{40,56},{48,32},{56,40},{64,80... | collective-permute-start | bytes 49160 | tf_op jit(solution)/shard_map/ppermute | solution.py:139
  88.1 3.1 %stack.184 = bf16[9,2,4,4,4,128]{5,0,4,1,3,2:T(8,128)(2,1)} concatenate(bf16[1,2,4,4,4,128]{5,0,4,1,3,2:T(2,128)(2,1)} %copy.696, bf16[1,2,4,4,4,128]{5,0,4,1,3,2:T(2,128)(2,1)} %copy.697, bf16[1,2,4,4,4,128]{5,0,4,1,3,2:T(2,128)(2,1)} %copy.698, bf16[1,2,4,4,4,128]{5,0,4,1,3,2:T(2,128)(2,1)} %copy.699, bf16[1,2,4,4,4,128]{5,0,4,1,3,2:T(2,128)(2,1)} %copy.700, ...), dimensions={0} | concatenate | bytes 589824 | tf_op jit(solution)/shard_map/stack | solution.py:50
  92.0 8.8 %collective-permute-start.6 = (bf16[4,2,2,4,256]{4,3,0,1,2:T(4,128)(2,1)S(1)}, bf16[4,2,2,4,256]{4,3,0,1,2:T(4,128)(2,1)S(1)}, u32[]{:S(2)}, u32[]{:S(2)}) collective-permute-start(bf16[4,2,2,4,256]{4,3,0,1,2:T(4,128)(2,1)S(1)} %maximum_select_fusion.4), channel_id=1, source_target_pairs={{0,32},{8,40},{16,48},{24,56},{32,0},{40,8},{48,16},{56,24},{64,96... | collective-permute-start | bytes 98312 | tf_op jit(solution)/shard_map/ppermute | solution.py:139
  102.7 9.0 %collective-permute-start.7 = (bf16[8,2,2,4,256]{4,3,0,1,2:T(4,128)(2,1)S(1)}, bf16[8,2,2,4,256]{4,3,0,1,2:T(4,128)(2,1)S(1)}, u32[]{:S(2)}, u32[]{:S(2)}) collective-permute-start(bf16[8,2,2,4,256]{4,3,0,1,2:T(4,128)(2,1)S(1)} %maximum_select_fusion.3), channel_id=1, source_target_pairs={{0,64},{8,72},{16,80},{24,88},{32,96},{40,104},{48,112},{56,120},{... | collective-permute-start | bytes 196616 | tf_op jit(solution)/shard_map/ppermute | solution.py:139
  112.5 6.0 %collective-permute-done.7 = bf16[8,2,2,4,256]{4,3,0,1,2:T(4,128)(2,1)S(1)} collective-permute-done((bf16[8,2,2,4,256]{4,3,0,1,2:T(4,128)(2,1)S(1)}, bf16[8,2,2,4,256]{4,3,0,1,2:T(4,128)(2,1)S(1)}, u32[]{:S(2)}, u32[]{:S(2)}) %collective-permute-start.7) | collective-permute-done | bytes 65568 | tf_op jit(solution)/shard_map/ppermute | solution.py:139
  118.6 3.2 %collective-permute-start.8 = (bf16[16,2,2,4,256]{4,3,0,1,2:T(4,128)(2,1)S(1)}, bf16[16,2,2,4,256]{4,3,0,1,2:T(4,128)(2,1)S(1)}, u32[]{:S(2)}, u32[]{:S(2)}) collective-permute-start(bf16[16,2,2,4,256]{4,3,0,1,2:T(4,128)(2,1)S(1)} %maximum_select_fusion.2), channel_id=1, source_target_pairs={{0,128},{8,136},{16,144},{24,152},{32,160},{40,168},{48,176},{56,1... | collective-permute-start | bytes 393224 | tf_op jit(solution)/shard_map/ppermute | solution.py:139
  121.9 2.5 %collective-permute-done.8 = bf16[16,2,2,4,256]{4,3,0,1,2:T(4,128)(2,1)S(1)} collective-permute-done((bf16[16,2,2,4,256]{4,3,0,1,2:T(4,128)(2,1)S(1)}, bf16[16,2,2,4,256]{4,3,0,1,2:T(4,128)(2,1)S(1)}, u32[]{:S(2)}, u32[]{:S(2)}) %collective-permute-start.8) | collective-permute-done | bytes 131104 | tf_op jit(solution)/shard_map/ppermute | solution.py:139
  124.5 4.7 %collective-permute-start.9 = (bf16[32,2,2,4,256]{4,3,0,1,2:T(4,128)(2,1)S(1)}, bf16[32,2,2,4,256]{4,3,0,1,2:T(4,128)(2,1)S(1)}, u32[]{:S(2)}, u32[]{:S(2)}) collective-permute-start(bf16[32,2,2,4,256]{4,3,0,1,2:T(4,128)(2,1)S(1)} %maximum_select_fusion.1), channel_id=1, source_target_pairs={{0,256},{8,264},{16,272},{24,280},{32,288},{40,296},{48,304},{56,3... | collective-permute-start | bytes 786440 | tf_op jit(solution)/shard_map/ppermute | solution.py:139
  129.7 3.5 %collective-permute-done.9 = bf16[32,2,2,4,256]{4,3,0,1,2:T(4,128)(2,1)S(1)} collective-permute-done((bf16[32,2,2,4,256]{4,3,0,1,2:T(4,128)(2,1)S(1)}, bf16[32,2,2,4,256]{4,3,0,1,2:T(4,128)(2,1)S(1)}, u32[]{:S(2)}, u32[]{:S(2)}) %collective-permute-start.9) | collective-permute-done | bytes 262176 | tf_op jit(solution)/shard_map/ppermute | solution.py:139
  135.3 6.3 %collective-permute-start.10 = (f32[4,2,2,4,256]{4,0,3,1,2:T(4,128)S(1)}, f32[4,2,2,4,256]{4,0,3,1,2:T(4,128)S(1)}, u32[]{:S(2)}, u32[]{:S(2)}) collective-permute-start(f32[4,2,2,4,256]{4,0,3,1,2:T(4,128)S(1)} %slice_select_fusion), channel_id=1, source_target_pairs={{0,4},{1,5},{2,6},{3,7},{4,0},{5,1},{6,2},{7,3},{8,12},{9,13},{10,... | collective-permute-start | bytes 196616 | tf_op jit(solution)/shard_map/ppermute | solution.py:158
  143.3 3.0 %collective-permute-start.11 = (f32[2,2,2,4,256]{4,0,3,1,2:T(2,128)S(1)}, f32[2,2,2,4,256]{4,0,3,1,2:T(2,128)S(1)}, u32[]{:S(2)}, u32[]{:S(2)}) collective-permute-start(f32[2,2,2,4,256]{4,0,3,1,2:T(2,128)S(1)} %broadcast_select_fusion), channel_id=1, source_target_pairs={{0,2},{1,3},{2,0},{3,1},{4,6},{5,7},{6,4},{7,5},{8,10},{9,11},{10,... | collective-permute-start | bytes 98312 | tf_op jit(solution)/shard_map/ppermute | solution.py:158
  148.2 8.6 %collective-permute-start.12 = (f32[1,2,2,4,256]{4,0,3,1,2:T(1,128)S(1)}, f32[1,2,2,4,256]{4,0,3,1,2:T(1,128)S(1)}, u32[]{:S(2)}, u32[]{:S(2)}) collective-permute-start(f32[1,2,2,4,256]{4,0,3,1,2:T(1,128)S(1)} %broadcast_select_fusion.1), channel_id=1, source_target_pairs={{0,1},{1,0},{2,3},{3,2},{4,5},{5,4},{6,7},{7,6},{8,9},{9,8},{10,11... | collective-permute-start | bytes 49160 | tf_op jit(solution)/shard_map/ppermute | solution.py:158
  (241 shorter events, 53.0 us)
Async XLA Ops:
  0.6 66.4 %copy-start = (f32[256,128]{1,0:T(8,128)S(1)}, f32[256,128]{1,0:T(8,128)}, u32[]{:S(2)}) copy-start(f32[256,128]{1,0:T(8,128)} %param.42) | copy-start | bytes 393220
  5.9 14.2 %copy-start.7 = (bf16[2,128,128]{2,1,0:T(8,128)(2,1)S(1)}, bf16[2,128,128]{2,1,0:T(8,128)(2,1)}, u32[]{:S(2)}) copy-start(bf16[2,128,128]{2,1,0:T(8,128)(2,1)} %param.40) | copy-start | bytes 196612
  6.7 14.9 %copy-start.11 = (bf16[2,128,128]{2,1,0:T(8,128)(2,1)S(1)}, bf16[2,128,128]{2,1,0:T(8,128)(2,1)}, u32[]{:S(2)}) copy-start(bf16[2,128,128]{2,1,0:T(8,128)(2,1)} %param.41) | copy-start | bytes 196612
  6.7 16.3 %copy-start.16 = (f32[2,15,15,128]{3,0,2,1:T(2,128)S(1)}, f32[2,15,15,128]{3,0,2,1:T(2,128)}, u32[]{:S(2)}) copy-start(f32[2,15,15,128]{3,0,2,1:T(2,128)} %param.44) | copy-start | bytes 691204
  12.1 30.4 %collective-permute-start = (f32[304,128]{1,0:T(8,128)}, f32[304,128]{1,0:T(8,128)}, u32[]{:S(2)}, u32[]{:S(2)}) collective-permute-start(f32[304,128]{1,0:T(8,128)} %pad_maximum_fusion.7), channel_id=1, source_target_pairs={{0,8},{8,16},{16,24},{24,32},{32,40},{40,48},{48,56},{56,64},{64,7... | collective-permute-start | bytes 466952 | tf_op jit(solution)/shard_map/ppermute | solution.py:112
  43.3 6.0 %collective-permute-start.1 = (f32[304,128]{1,0:T(8,128)S(1)}, f32[304,128]{1,0:T(8,128)S(1)}, u32[]{:S(2)}, u32[]{:S(2)}) collective-permute-start(f32[304,128]{1,0:T(8,128)S(1)} %pad_maximum_fusion.6), channel_id=1, source_target_pairs={{8,0},{16,8},{24,16},{32,24},{40,32},{48,40},{56,48},{64,56},{72,6... | collective-permute-start | bytes 466952 | tf_op jit(solution)/shard_map/ppermute | solution.py:115
  49.7 10.3 %collective-permute-start.2 = (f32[800,128]{1,0:T(8,128)S(1)}, f32[800,128]{1,0:T(8,128)S(1)}, u32[]{:S(2)}, u32[]{:S(2)}) collective-permute-start(f32[800,128]{1,0:T(8,128)S(1)} %get-tuple-element.216), channel_id=1, source_target_pairs={{0,1},{1,2},{2,3},{3,4},{4,5},{5,6},{6,7},{8,9},{9,10},{10,11},{11... | collective-permute-start | bytes 1228808 | tf_op jit(solution)/shard_map/ppermute | solution.py:112
  55.1 9.3 %collective-permute-start.3 = (f32[800,128]{1,0:T(8,128)S(1)}, f32[800,128]{1,0:T(8,128)S(1)}, u32[]{:S(2)}, u32[]{:S(2)}) collective-permute-start(f32[800,128]{1,0:T(8,128)S(1)} %get-tuple-element.217), channel_id=1, source_target_pairs={{1,0},{2,1},{3,2},{4,3},{5,4},{6,5},{7,6},{9,8},{10,9},{11,10},{12... | collective-permute-start | bytes 1228808 | tf_op jit(solution)/shard_map/ppermute | solution.py:115
  67.7 7.8 %collective-permute-start.4 = (bf16[1,2,2,4,256]{4,3,0,1,2:T(4,128)(2,1)S(1)}, bf16[1,2,2,4,256]{4,3,0,1,2:T(4,128)(2,1)S(1)}, u32[]{:S(2)}, u32[]{:S(2)}) collective-permute-start(bf16[1,2,2,4,256]{4,3,0,1,2:T(4,128)(2,1)S(1)} %pad_maximum_fusion.12), channel_id=1, source_target_pairs={{0,8},{8,0},{16,24},{24,16},{32,40},{40,32},{48,56},{56,48},{64,72... | collective-permute-start | bytes 24584 | tf_op jit(solution)/shard_map/ppermute | solution.py:139
  76.0 15.2 %collective-permute-start.5 = (bf16[2,2,2,4,256]{4,3,0,1,2:T(4,128)(2,1)}, bf16[2,2,2,4,256]{4,3,0,1,2:T(4,128)(2,1)}, u32[]{:S(2)}, u32[]{:S(2)}) collective-permute-start(bf16[2,2,2,4,256]{4,3,0,1,2:T(4,128)(2,1)} %maximum_select_fusion.5), channel_id=1, source_target_pairs={{0,16},{8,24},{16,0},{24,8},{32,48},{40,56},{48,32},{56,40},{64,80... | collective-permute-start | bytes 49160 | tf_op jit(solution)/shard_map/ppermute | solution.py:139
  91.2 38.5 %slice-start = ((f32[800,128]{1,0:T(8,128)}), f32[32,128]{1,0:T(8,128)S(1)}, s32[]{:S(2)}) async-start(f32[800,128]{1,0:T(8,128)} %copy-done.29), calls=%async_computation | async-start | bytes 32768 | tf_op jit(solution)/shard_map/slice | solution.py:124
  92.0 10.6 %collective-permute-start.6 = (bf16[4,2,2,4,256]{4,3,0,1,2:T(4,128)(2,1)S(1)}, bf16[4,2,2,4,256]{4,3,0,1,2:T(4,128)(2,1)S(1)}, u32[]{:S(2)}, u32[]{:S(2)}) collective-permute-start(bf16[4,2,2,4,256]{4,3,0,1,2:T(4,128)(2,1)S(1)} %maximum_select_fusion.4), channel_id=1, source_target_pairs={{0,32},{8,40},{16,48},{24,56},{32,0},{40,8},{48,16},{56,24},{64,96... | collective-permute-start | bytes 98312 | tf_op jit(solution)/shard_map/ppermute | solution.py:139
  102.7 15.8 %collective-permute-start.7 = (bf16[8,2,2,4,256]{4,3,0,1,2:T(4,128)(2,1)S(1)}, bf16[8,2,2,4,256]{4,3,0,1,2:T(4,128)(2,1)S(1)}, u32[]{:S(2)}, u32[]{:S(2)}) collective-permute-start(bf16[8,2,2,4,256]{4,3,0,1,2:T(4,128)(2,1)S(1)} %maximum_select_fusion.3), channel_id=1, source_target_pairs={{0,64},{8,72},{16,80},{24,88},{32,96},{40,104},{48,112},{56,120},{... | collective-permute-start | bytes 196616 | tf_op jit(solution)/shard_map/ppermute | solution.py:139
  118.6 5.7 %collective-permute-start.8 = (bf16[16,2,2,4,256]{4,3,0,1,2:T(4,128)(2,1)S(1)}, bf16[16,2,2,4,256]{4,3,0,1,2:T(4,128)(2,1)S(1)}, u32[]{:S(2)}, u32[]{:S(2)}) collective-permute-start(bf16[16,2,2,4,256]{4,3,0,1,2:T(4,128)(2,1)S(1)} %maximum_select_fusion.2), channel_id=1, source_target_pairs={{0,128},{8,136},{16,144},{24,152},{32,160},{40,168},{48,176},{56,1... | collective-permute-start | bytes 393224 | tf_op jit(solution)/shard_map/ppermute | solution.py:139
  124.5 8.6 %collective-permute-start.9 = (bf16[32,2,2,4,256]{4,3,0,1,2:T(4,128)(2,1)S(1)}, bf16[32,2,2,4,256]{4,3,0,1,2:T(4,128)(2,1)S(1)}, u32[]{:S(2)}, u32[]{:S(2)}) collective-permute-start(bf16[32,2,2,4,256]{4,3,0,1,2:T(4,128)(2,1)S(1)} %maximum_select_fusion.1), channel_id=1, source_target_pairs={{0,256},{8,264},{16,272},{24,280},{32,288},{40,296},{48,304},{56,3... | collective-permute-start | bytes 786440 | tf_op jit(solution)/shard_map/ppermute | solution.py:139
  135.2 21.9 %copy-start.19 = (f32[16,2,4,128]{3,2,1,0:T(4,128)S(1)}, f32[16,2,4,128]{3,2,1,0:T(4,128)}, u32[]{:S(2)}) copy-start(f32[16,2,4,128]{3,2,1,0:T(4,128)} %get-tuple-element.182) | copy-start | bytes 196612
  135.3 21.9 %copy-start.18 = (f32[16,2,4,128]{3,2,1,0:T(4,128)S(1)}, f32[16,2,4,128]{3,2,1,0:T(4,128)}, u32[]{:S(2)}) copy-start(f32[16,2,4,128]{3,2,1,0:T(4,128)} %get-tuple-element.183) | copy-start | bytes 196612
  135.3 8.0 %collective-permute-start.10 = (f32[4,2,2,4,256]{4,0,3,1,2:T(4,128)S(1)}, f32[4,2,2,4,256]{4,0,3,1,2:T(4,128)S(1)}, u32[]{:S(2)}, u32[]{:S(2)}) collective-permute-start(f32[4,2,2,4,256]{4,0,3,1,2:T(4,128)S(1)} %slice_select_fusion), channel_id=1, source_target_pairs={{0,4},{1,5},{2,6},{3,7},{4,0},{5,1},{6,2},{7,3},{8,12},{9,13},{10,... | collective-permute-start | bytes 196616 | tf_op jit(solution)/shard_map/ppermute | solution.py:158
  141.6 16.0 %copy-start.21 = (f32[4,4,256]{2,1,0:T(4,128)S(1)}, f32[4,4,256]{2,1,0:T(4,128)}, u32[]{:S(2)}) copy-start(f32[4,4,256]{2,1,0:T(4,128)} %cos.11) | copy-start | bytes 49156
  141.6 16.0 %copy-start.23 = (f32[4,4,256]{2,1,0:T(4,128)S(1)}, f32[4,4,256]{2,1,0:T(4,128)}, u32[]{:S(2)}) copy-start(f32[4,4,256]{2,1,0:T(4,128)} %sin.11) | copy-start | bytes 49156
  142.0 16.2 %copy-start.12 = (bf16[2,128,128]{2,1,0:T(8,128)(2,1)S(1)}, bf16[2,128,128]{2,1,0:T(8,128)(2,1)}, u32[]{:S(2)}) copy-start(bf16[2,128,128]{2,1,0:T(8,128)(2,1)} %param.41) | copy-start | bytes 196612
  142.0 16.2 %copy-start.13 = (bf16[1,2,128,128]{3,2,0,1:T(8,128)(2,1)S(1)}, bf16[1,2,128,128]{3,2,0,1:T(8,128)(2,1)}, u32[]{:S(2)}) copy-start(bf16[1,2,128,128]{3,2,0,1:T(8,128)(2,1)} %maximum_bitcast_fusion.6) | copy-start | bytes 196612
  143.3 4.8 %collective-permute-start.11 = (f32[2,2,2,4,256]{4,0,3,1,2:T(2,128)S(1)}, f32[2,2,2,4,256]{4,0,3,1,2:T(2,128)S(1)}, u32[]{:S(2)}, u32[]{:S(2)}) collective-permute-start(f32[2,2,2,4,256]{4,0,3,1,2:T(2,128)S(1)} %broadcast_select_fusion), channel_id=1, source_target_pairs={{0,2},{1,3},{2,0},{3,1},{4,6},{5,7},{6,4},{7,5},{8,10},{9,11},{10,... | collective-permute-start | bytes 98312 | tf_op jit(solution)/shard_map/ppermute | solution.py:158
  148.2 9.4 %collective-permute-start.12 = (f32[1,2,2,4,256]{4,0,3,1,2:T(1,128)S(1)}, f32[1,2,2,4,256]{4,0,3,1,2:T(1,128)S(1)}, u32[]{:S(2)}, u32[]{:S(2)}) collective-permute-start(f32[1,2,2,4,256]{4,0,3,1,2:T(1,128)S(1)} %broadcast_select_fusion.1), channel_id=1, source_target_pairs={{0,1},{1,0},{2,3},{3,2},{4,5},{5,4},{6,7},{7,6},{8,9},{9,8},{10,11... | collective-permute-start | bytes 49160 | tf_op jit(solution)/shard_map/ppermute | solution.py:158
  (34 other events, 165.1 us)

commit v5 on v4

--- a/solution.py
+++ b/solution.py
@@ -223,18 +223,22 @@
     return jnp.moveaxis(leaf_in, (0, 1), (2, 3))
 
 
-def far_field(vectors, rad_tab, rcv_tab, leaf_tab, coarse_tab, interp, phase):
-    box_side = vectors.shape[2] // 3
+def radiate(vectors, rad_tab):
+    out_re = product("srcmp,sqp->srcmq", vectors[:, 0], rad_tab[:, 0]) - product(
+        "srcmp,sqp->srcmq", vectors[:, 1], rad_tab[:, 1]
+    )
+    out_im = product("srcmp,sqp->srcmq", vectors[:, 0], rad_tab[:, 1]) + product(
+        "srcmp,sqp->srcmq", vectors[:, 1], rad_tab[:, 0]
+    )
+    return jnp.stack([out_re, out_im], 1)
+
+
+def far_field(own, vectors, rad_tab, rcv_tab, leaf_tab, coarse_tab, interp, phase):
+    box_side = own.shape[2]
     span = 3 * box_side
     reach = 2 * box_side - 1
-    out_re = product("srcmp,sqp->srcmq", vectors[:, 0], rad_tab[:, 0]) - product(
-        "srcmp,sqp->srcmq", vectors[:, 1], rad_tab[:, 1]
-    )
-    out_im = product("srcmp,sqp->srcmq", vectors[:, 0], rad_tab[:, 1]) + product(
-        "srcmp,sqp->srcmq", vectors[:, 1], rad_tab[:, 0]
-    )
-    window = jnp.stack([out_re, out_im], 1)
-    leaf_out = window[:, :, box_side : 2 * box_side, box_side : 2 * box_side]
+    leaf_out = radiate(own, rad_tab)
+    window = radiate(vectors, rad_tab)
     leaf_in = leaf_incoming(window, leaf_tab, box_side)
     interpolated = jnp.einsum("kq,sxrcmq->sxrcmk", interp, leaf_out, precision=HIGH)
     angles = phase.reshape(box_side, box_side, -1)
@@ -286,6 +290,7 @@
         None,
     )
     far_both = far_field(
+        jnp.stack([current, probe]),
         vectors,
         jnp.stack([fwd_set[0], adj_set[0]]),
         jnp.stack([fwd_set[1], adj_set[1]]),

time: 162 us -> 163 us (level)
  other arithmetic: 24.2 us -> 31.7 us
  waiting for transfers between devices: 21.1 us -> 15.2 us
  starting transfers between devices: 68.9 us -> 66.2 us
    ppermute x6, waiting for transfers between devices: 12.5 us -> 5.29 us  [gather_ordered(): other = lax.ppermute(held, axis, [(i, i ^ step) for i in range(count)])]
    unnamed x96 -> x82, local copies, waits for them, and re-layouts: 2.66 us -> 8.65 us
    select_n x5, other arithmetic: 1.8 us -> 7.51 us  [gather_ordered(): jnp.where(lower, jnp.concatenate([held, other], 0), jnp.concatenate([othe...]
    another operation x11, local copies, waits for them, and re-layouts: 7.98 us -> 2.94 us  [near_forward(): jnp.stack([padded[:, offset_code // 3:offset_code // 3 + box_side, offset...]
    ppermute x2, waiting for transfers between devices: 0.57 us -> 2.78 us  [exchange_halo(): lax.ppermute(jnp.concatenate([flat, to_next.reshape(-1, lanes)]), axis, a...]
    ppermute x2, starting transfers between devices: 10.5 us -> 8.54 us  [exchange_halo(): lax.ppermute(jnp.concatenate([flat, to_next.reshape(-1, lanes)]), axis, a...]
    dot_general x17 -> x21, matrix products: 8.12 us -> 9.68 us  [product(): return jnp.einsum(form, left, right, preferred_element_type=jnp.float32)]
  transfers between devices with their start and end apart: 13 -> 13, of which waited for: 10 -> 6; matrix products, arithmetic and copies ran while one was open for 29% -> 28% of each run, Pallas kernels for 0% -> 0%
where the time goes in v5:
time: 163 us; the launch traced here: 161 us
  starting transfers between devices  66.2 us (41%)
  local copies, waits for them, and re-layouts  32.6 us (20%)
  other arithmetic  31.7 us (19%)
  waiting for transfers between devices  15.2 us (9%)
  matrix products  13.5 us (8%)
  between operations  1.94 us (1%)
    ppermute x6, starting transfers between devices, gather_ordered(): other = lax.ppermute(held, axis, [(i, i ^ step) for i in range(count)])  36.3 us
    ppermute x3, starting transfers between devices, scatter_sum(): lax.ppermute(send, axis, [(i, i ^ step) for i in range(count)])  18 us
    dot_general x21, matrix products, product(): return jnp.einsum(form, left, right, preferred_element_type=jnp.float32)  9.68 us
    unnamed x82, local copies, waits for them, and re-layouts  8.65 us
    ppermute x2, starting transfers between devices, exchange_halo(): lax.ppermute(jnp.concatenate([flat, to_next.reshape(-1, lanes)]), axis, a...  8.54 us
    select_n x5, other arithmetic, gather_ordered(): jnp.where(lower, jnp.concatenate([held, other], 0), jnp.concatenate([othe...  7.51 us
    ppermute x6, waiting for transfers between devices, gather_ordered(): other = lax.ppermute(held, axis, [(i, i ^ step) for i in range(count)])  5.29 us
    slice x2, local copies, waits for them, and re-layouts, coarse_exchange(): adj = jnp.stack([adj[0], -adj[1]])  4.45 us
  transfers between devices with their start and end apart: 13, of which 6 were waited for; matrix products, arithmetic and copies ran while one was open for 28% of the time, Pallas kernels for 0%

profile of v5, /device:TPU:1, one launch (start us, length us, event | category | flops | bytes accessed | tf_op | source)
XLA Modules:
  0.0 161.3 jit_solution(8773036572387705494)
XLA Ops:
  9.2 1.9 %fusion.51 = f32[2,6,6,4,128]{4,3,0,2,1:T(4,128)S(1)} fusion(f32[2,6,6,4,128]{4,3,0,2,1:T(4,128)S(1)} %add_dynamic-update-slice_fusion, s32[]{:T(128)} %bitcast.24, s32[]{:T(128)} %bitcast.25, f32[2,4,4,4,128]{4,3,0,2,1:T(4,128)S(1)} %bitcast.356, pred[]{:T(512)} %and_reduce_fusion), kind=kLoop, calls=%fused_computation.122 | loop fusion | flops 32768 | bytes 196617 | tf_op jit(solution)/shard_map/scatter-add | solution.py:91
  12.9 5.0 %collective-permute-start = (f32[304,128]{1,0:T(8,128)}, f32[304,128]{1,0:T(8,128)}, u32[]{:S(2)}, u32[]{:S(2)}) collective-permute-start(f32[304,128]{1,0:T(8,128)} %pad_maximum_fusion.6), channel_id=1, source_target_pairs={{0,8},{8,16},{16,24},{24,32},{32,40},{40,48},{48,56},{56,64},{64,7... | collective-permute-start | bytes 466952 | tf_op jit(solution)/shard_map/ppermute | solution.py:112
  21.0 3.1 %collective-permute-start.4 = (bf16[1,2,2,4,256]{4,3,0,1,2:T(4,128)(2,1)}, bf16[1,2,2,4,256]{4,3,0,1,2:T(4,128)(2,1)}, u32[]{:S(2)}, u32[]{:S(2)}) collective-permute-start(bf16[1,2,2,4,256]{4,3,0,1,2:T(4,128)(2,1)} %pad_maximum_fusion.13), channel_id=1, source_target_pairs={{0,8},{8,0},{16,24},{24,16},{32,40},{40,32},{48,56},{56,48},{64,72... | collective-permute-start | bytes 24584 | tf_op jit(solution)/shard_map/ppermute | solution.py:139
  25.9 2.1 %fusion.1 = f32[16,144,2,2,128]{4,1,3,2,0:T(8,128)S(1)} fusion(s32[16,144]{1,0:T(8,128)S(1)} %fusion.93, f32[1,2,225,128]{3,2,1,0:T(8,128)S(1)} %copy.718, f32[1,2,225,128]{3,2,1,0:T(8,128)S(1)} %copy.717), kind=kOutput, calls=%fused_computation.8 | convolution fusion | flops 3185683200 | bytes 5188608 | tf_op jit(solution)/shard_map/tnp,sxpq->tnsxq/dot_general | solution.py:214
  28.0 2.8 %slice_bitcast_fusion.1 = (f32[16,144,2,128]{3,1,2,0:T(8,128)}, f32[16,144,2,128]{3,1,2,0:T(8,128)}) fusion(f32[16,144,2,2,128]{4,1,3,2,0:T(8,128)S(1)} %fusion.1), kind=kLoop, calls=%fused_computation.5 | loop fusion | bytes 9437184 | tf_op jit(solution)/shard_map/mul | solution.py:220
  30.8 2.9 %constant_dynamic-slice_fusion.2 = (bf16[1,64,8,256]{3,0,2,1:T(2,128)(2,1)}, bf16[1,64,8,256]{3,0,2,1:T(2,128)(2,1)S(1)}) fusion(bf16[2,127,15,256]{3,0,2,1:T(2,128)(2,1)} %param.45, s32[]{:T(128)S(6)} %select_n.153, s32[]{:T(128)S(6)} %select_n.154, s32[]{:T(128)S(6)} %add.270), kind=kLoop, calls=%fused_computation.234 | loop fusion | bytes 1048588 | tf_op jit(solution)/shard_map/slice | solution.py:183
  40.1 3.0 %fusion.123 = (f32[2,1,64,8,256]{4,1,3,2,0:T(1,128)}, f32[2,1,64,8,256]{4,1,3,2,0:T(1,128)}) fusion(f32[2,2,64,8,256]{4,1,3,2,0:T(2,128)S(1)} %maximum_convert_fusion), kind=kLoop, calls=%fused_computation.261 | loop fusion | bytes 4194304 | tf_op jit(solution)/shard_map/slice | solution.py:189
  45.3 6.1 %collective-permute-start.5 = (bf16[2,2,2,4,256]{4,3,0,1,2:T(4,128)(2,1)}, bf16[2,2,2,4,256]{4,3,0,1,2:T(4,128)(2,1)}, u32[]{:S(2)}, u32[]{:S(2)}) collective-permute-start(bf16[2,2,2,4,256]{4,3,0,1,2:T(4,128)(2,1)} %maximum_select_fusion.5), channel_id=1, source_target_pairs={{0,16},{8,24},{16,0},{24,8},{32,48},{40,56},{48,32},{56,40},{64,80... | collective-permute-start | bytes 49160 | tf_op jit(solution)/shard_map/ppermute | solution.py:139
  51.4 2.8 %fusion.18 = (f32[2,64,8,256]{3,2,1,0:T(8,128)S(1)}, f32[2,64,8,256]{3,2,1,0:T(8,128)}) fusion(f32[2,1,64,8,256]{4,1,3,2,0:T(1,128)} %get-tuple-element.190, f32[64,8]{1,0:T(8,128)} %copy.727, f32[2,1,64,8,256]{4,1,3,2,0:T(1,128)} %get-tuple-element.191), kind=kLoop, calls=%fused_computation.42 | loop fusion | flops 524288 | bytes 4196352 | tf_op jit(solution)/shard_map/mul | solution.py:189
  55.6 8.9 %collective-permute-start.6 = (bf16[4,2,2,4,256]{4,3,0,1,2:T(4,128)(2,1)}, bf16[4,2,2,4,256]{4,3,0,1,2:T(4,128)(2,1)}, u32[]{:S(2)}, u32[]{:S(2)}) collective-permute-start(bf16[4,2,2,4,256]{4,3,0,1,2:T(4,128)(2,1)} %maximum_select_fusion.4), channel_id=1, source_target_pairs={{0,32},{8,40},{16,48},{24,56},{32,0},{40,8},{48,16},{56,24},{64,96... | collective-permute-start | bytes 98312 | tf_op jit(solution)/shard_map/ppermute | solution.py:139
  69.0 7.8 %collective-permute-start.7 = (bf16[8,2,2,4,256]{4,3,0,1,2:T(4,128)(2,1)}, bf16[8,2,2,4,256]{4,3,0,1,2:T(4,128)(2,1)}, u32[]{:S(2)}, u32[]{:S(2)}) collective-permute-start(bf16[8,2,2,4,256]{4,3,0,1,2:T(4,128)(2,1)} %maximum_select_fusion.3), channel_id=1, source_target_pairs={{0,64},{8,72},{16,80},{24,88},{32,96},{40,104},{48,112},{56,120},{... | collective-permute-start | bytes 196616 | tf_op jit(solution)/shard_map/ppermute | solution.py:139
  79.6 3.4 %collective-permute-done.7 = bf16[8,2,2,4,256]{4,3,0,1,2:T(4,128)(2,1)} collective-permute-done((bf16[8,2,2,4,256]{4,3,0,1,2:T(4,128)(2,1)}, bf16[8,2,2,4,256]{4,3,0,1,2:T(4,128)(2,1)}, u32[]{:S(2)}, u32[]{:S(2)}) %collective-permute-start.7) | collective-permute-done | bytes 65568 | tf_op jit(solution)/shard_map/ppermute | solution.py:139
  84.7 3.0 %collective-permute-start.8 = (bf16[16,2,2,4,256]{4,3,0,1,2:T(4,128)(2,1)}, bf16[16,2,2,4,256]{4,3,0,1,2:T(4,128)(2,1)}, u32[]{:S(2)}, u32[]{:S(2)}) collective-permute-start(bf16[16,2,2,4,256]{4,3,0,1,2:T(4,128)(2,1)} %maximum_select_fusion.2), channel_id=1, source_target_pairs={{0,128},{8,136},{16,144},{24,152},{32,160},{40,168},{48,176},{56,1... | collective-permute-start | bytes 393224 | tf_op jit(solution)/shard_map/ppermute | solution.py:139
  95.4 7.4 %collective-permute-start.9 = (bf16[32,2,2,4,256]{4,3,0,1,2:T(4,128)(2,1)S(1)}, bf16[32,2,2,4,256]{4,3,0,1,2:T(4,128)(2,1)S(1)}, u32[]{:S(2)}, u32[]{:S(2)}) collective-permute-start(bf16[32,2,2,4,256]{4,3,0,1,2:T(4,128)(2,1)S(1)} %maximum_select_fusion.1), channel_id=1, source_target_pairs={{0,256},{8,264},{16,272},{24,280},{32,288},{40,296},{48,304},{56,3... | collective-permute-start | bytes 786440 | tf_op jit(solution)/shard_map/ppermute | solution.py:139
  104.7 1.9 %collective-permute-done.9 = bf16[32,2,2,4,256]{4,3,0,1,2:T(4,128)(2,1)S(1)} collective-permute-done((bf16[32,2,2,4,256]{4,3,0,1,2:T(4,128)(2,1)S(1)}, bf16[32,2,2,4,256]{4,3,0,1,2:T(4,128)(2,1)S(1)}, u32[]{:S(2)}, u32[]{:S(2)}) %collective-permute-start.9) | collective-permute-done | bytes 262176 | tf_op jit(solution)/shard_map/ppermute | solution.py:139
  108.7 4.9 %collective-permute-start.10 = (f32[4,2,2,4,256]{4,0,3,1,2:T(4,128)S(1)}, f32[4,2,2,4,256]{4,0,3,1,2:T(4,128)S(1)}, u32[]{:S(2)}, u32[]{:S(2)}) collective-permute-start(f32[4,2,2,4,256]{4,0,3,1,2:T(4,128)S(1)} %slice_select_fusion), channel_id=1, source_target_pairs={{0,4},{1,5},{2,6},{3,7},{4,0},{5,1},{6,2},{7,3},{8,12},{9,13},{10,... | collective-permute-start | bytes 196616 | tf_op jit(solution)/shard_map/ppermute | solution.py:158
  115.4 3.3 %collective-permute-start.11 = (f32[2,2,2,4,256]{4,0,3,1,2:T(2,128)S(1)}, f32[2,2,2,4,256]{4,0,3,1,2:T(2,128)S(1)}, u32[]{:S(2)}, u32[]{:S(2)}) collective-permute-start(f32[2,2,2,4,256]{4,0,3,1,2:T(2,128)S(1)} %broadcast_select_fusion), channel_id=1, source_target_pairs={{0,2},{1,3},{2,0},{3,1},{4,6},{5,7},{6,4},{7,5},{8,10},{9,11},{10,... | collective-permute-start | bytes 98312 | tf_op jit(solution)/shard_map/ppermute | solution.py:158
  120.1 9.8 %collective-permute-start.12 = (f32[1,2,2,4,256]{4,0,3,1,2:T(1,128)S(1)}, f32[1,2,2,4,256]{4,0,3,1,2:T(1,128)S(1)}, u32[]{:S(2)}, u32[]{:S(2)}) collective-permute-start(f32[1,2,2,4,256]{4,0,3,1,2:T(1,128)S(1)} %broadcast_select_fusion.1), channel_id=1, source_target_pairs={{0,1},{1,0},{2,3},{3,2},{4,5},{5,4},{6,7},{7,6},{8,9},{9,8},{10,11... | collective-permute-start | bytes 49160 | tf_op jit(solution)/shard_map/ppermute | solution.py:158
  130.1 3.5 %collective-permute-start.2 = (f32[800,128]{1,0:T(8,128)S(1)}, f32[800,128]{1,0:T(8,128)S(1)}, u32[]{:S(2)}, u32[]{:S(2)}) collective-permute-start(f32[800,128]{1,0:T(8,128)S(1)} %get-tuple-element.216), channel_id=1, source_target_pairs={{0,1},{1,2},{2,3},{3,4},{4,5},{5,6},{6,7},{8,9},{9,10},{10,11},{11... | collective-permute-start | bytes 1228808 | tf_op jit(solution)/shard_map/ppermute | solution.py:112
  133.6 1.9 %collective-permute-start.3 = (f32[800,128]{1,0:T(8,128)S(1)}, f32[800,128]{1,0:T(8,128)S(1)}, u32[]{:S(2)}, u32[]{:S(2)}) collective-permute-start(f32[800,128]{1,0:T(8,128)S(1)} %get-tuple-element.217), channel_id=1, source_target_pairs={{1,0},{2,1},{3,2},{4,3},{5,4},{6,5},{7,6},{9,8},{10,9},{11,10},{12... | collective-permute-start | bytes 1228808 | tf_op jit(solution)/shard_map/ppermute | solution.py:115
  135.7 2.8 %collective-permute-done.2 = f32[800,128]{1,0:T(8,128)S(1)} collective-permute-done((f32[800,128]{1,0:T(8,128)S(1)}, f32[800,128]{1,0:T(8,128)S(1)}, u32[]{:S(2)}, u32[]{:S(2)}) %collective-permute-start.2) | collective-permute-done | bytes 409632 | tf_op jit(solution)/shard_map/ppermute | solution.py:112
  138.6 4.3 %collective-permute-done.3 = f32[800,128]{1,0:T(8,128)S(1)} collective-permute-done((f32[800,128]{1,0:T(8,128)S(1)}, f32[800,128]{1,0:T(8,128)S(1)}, u32[]{:S(2)}, u32[]{:S(2)}) %collective-permute-start.3) | collective-permute-done | bytes 409632 | tf_op jit(solution)/shard_map/ppermute | solution.py:115
  148.2 3.5 %subtract_reduce_fusion = (f32[16,2,4,128]{3,2,1,0:T(4,128)S(1)}, f32[16,2,4,128]{3,2,1,0:T(4,128)S(1)}) fusion(f32[144,2,4,128]{3,0,2,1:T(8,128)S(1)} %copy.723, f32[16,144,2,128]{3,1,2,0:T(8,128)S(1)} %copy-done.3, f32[144,2,4,128]{3,0,2,1:T(8,128)S(1)} %copy.722, f32[16,144,2,128]{3,1,2,0:T(8,128)S(1)} %copy-done.2), kind=kLoop, calls=%fused_computation.1 | loop fusion | flops 18841600 | bytes 6029312 | tf_op jit(solution)/shard_map/reduce_sum | solution.py:220
  155.1 1.8 %stack.196 = bf16[9,2,4,4,4,128]{5,0,4,1,3,2:T(8,128)(2,1)S(1)} concatenate(bf16[1,2,4,4,4,128]{5,0,4,1,3,2:T(2,128)(2,1)S(1)} %copy.704, bf16[1,2,4,4,4,128]{5,0,4,1,3,2:T(2,128)(2,1)S(1)} %copy.705, bf16[1,2,4,4,4,128]{5,0,4,1,3,2:T(2,128)(2,1)S(1)} %copy.706, bf16[1,2,4,4,4,128]{5,0,4,1,3,2:T(2,128)(2,1)S(1)} %copy.707, bf16[1,2,4,4,4,128]{5,0,4,1,3,2:T(2,128)(2,1)S(1)} %copy.708, ...), dimensions={0} | concatenate | bytes 589824 | tf_op jit(solution)/shard_map/stack | solution.py:50
  (233 shorter events, 61.6 us)
Async XLA Ops:
  0.6 18.6 %copy-start = (f32[256,128]{1,0:T(8,128)S(1)}, f32[256,128]{1,0:T(8,128)}, u32[]{:S(2)}) copy-start(f32[256,128]{1,0:T(8,128)} %param.42) | copy-start | bytes 393220
  4.5 6.9 %copy-start.31 = (bf16[2,4,4,4,128]{4,3,2,1,0:T(4,128)(2,1)S(1)}, bf16[2,4,4,4,128]{4,3,2,1,0:T(4,128)(2,1)}, u32[]{:S(2)}) copy-start(bf16[2,4,4,4,128]{4,3,2,1,0:T(4,128)(2,1)} %param.36) | copy-start | bytes 98308
  5.3 12.6 %copy-start.10 = (bf16[2,128,128]{2,1,0:T(8,128)(2,1)S(1)}, bf16[2,128,128]{2,1,0:T(8,128)(2,1)}, u32[]{:S(2)}) copy-start(bf16[2,128,128]{2,1,0:T(8,128)(2,1)} %param.41) | copy-start | bytes 196612
  5.3 12.9 %copy-start.16 = (bf16[2,128,128]{2,1,0:T(8,128)(2,1)S(1)}, bf16[2,128,128]{2,1,0:T(8,128)(2,1)}, u32[]{:S(2)}) copy-start(bf16[2,128,128]{2,1,0:T(8,128)(2,1)} %param.40) | copy-start | bytes 196612
  7.9 11.1 %copy-start.32 = (f32[16,256]{1,0:T(8,128)S(1)}, f32[16,256]{1,0:T(8,128)}, u32[]{:S(2)}) copy-start(f32[16,256]{1,0:T(8,128)} %param.43) | copy-start | bytes 49156
  11.3 13.9 %copy-start.13 = (f32[2,15,15,128]{3,0,2,1:T(2,128)S(1)}, f32[2,15,15,128]{3,0,2,1:T(2,128)}, u32[]{:S(2)}) copy-start(f32[2,15,15,128]{3,0,2,1:T(2,128)} %param.44) | copy-start | bytes 691204
  12.9 74.9 %collective-permute-start = (f32[304,128]{1,0:T(8,128)}, f32[304,128]{1,0:T(8,128)}, u32[]{:S(2)}, u32[]{:S(2)}) collective-permute-start(f32[304,128]{1,0:T(8,128)} %pad_maximum_fusion.6), channel_id=1, source_target_pairs={{0,8},{8,16},{16,24},{24,32},{32,40},{40,48},{48,56},{56,64},{64,7... | collective-permute-start | bytes 466952 | tf_op jit(solution)/shard_map/ppermute | solution.py:112
  19.2 6.2 %copy-start.19 = (f32[4,4,256]{2,1,0:T(4,128)}, f32[4,4,256]{2,1,0:T(4,128)S(1)}, u32[]{:S(2)}) copy-start(f32[4,4,256]{2,1,0:T(4,128)S(1)} %cos.11) | copy-start | bytes 49156
  19.2 6.2 %copy-start.21 = (f32[4,4,256]{2,1,0:T(4,128)}, f32[4,4,256]{2,1,0:T(4,128)S(1)}, u32[]{:S(2)}) copy-start(f32[4,4,256]{2,1,0:T(4,128)S(1)} %sin.11) | copy-start | bytes 49156
  21.0 22.9 %collective-permute-start.4 = (bf16[1,2,2,4,256]{4,3,0,1,2:T(4,128)(2,1)}, bf16[1,2,2,4,256]{4,3,0,1,2:T(4,128)(2,1)}, u32[]{:S(2)}, u32[]{:S(2)}) collective-permute-start(bf16[1,2,2,4,256]{4,3,0,1,2:T(4,128)(2,1)} %pad_maximum_fusion.13), channel_id=1, source_target_pairs={{0,8},{8,0},{16,24},{24,16},{32,40},{40,32},{48,56},{56,48},{64,72... | collective-permute-start | bytes 24584 | tf_op jit(solution)/shard_map/ppermute | solution.py:139
  45.3 8.9 %collective-permute-start.5 = (bf16[2,2,2,4,256]{4,3,0,1,2:T(4,128)(2,1)}, bf16[2,2,2,4,256]{4,3,0,1,2:T(4,128)(2,1)}, u32[]{:S(2)}, u32[]{:S(2)}) collective-permute-start(bf16[2,2,2,4,256]{4,3,0,1,2:T(4,128)(2,1)} %maximum_select_fusion.5), channel_id=1, source_target_pairs={{0,16},{8,24},{16,0},{24,8},{32,48},{40,56},{48,32},{56,40},{64,80... | collective-permute-start | bytes 49160 | tf_op jit(solution)/shard_map/ppermute | solution.py:139
  55.6 11.8 %collective-permute-start.6 = (bf16[4,2,2,4,256]{4,3,0,1,2:T(4,128)(2,1)}, bf16[4,2,2,4,256]{4,3,0,1,2:T(4,128)(2,1)}, u32[]{:S(2)}, u32[]{:S(2)}) collective-permute-start(bf16[4,2,2,4,256]{4,3,0,1,2:T(4,128)(2,1)} %maximum_select_fusion.4), channel_id=1, source_target_pairs={{0,32},{8,40},{16,48},{24,56},{32,0},{40,8},{48,16},{56,24},{64,96... | collective-permute-start | bytes 98312 | tf_op jit(solution)/shard_map/ppermute | solution.py:139
  69.0 14.0 %collective-permute-start.7 = (bf16[8,2,2,4,256]{4,3,0,1,2:T(4,128)(2,1)}, bf16[8,2,2,4,256]{4,3,0,1,2:T(4,128)(2,1)}, u32[]{:S(2)}, u32[]{:S(2)}) collective-permute-start(bf16[8,2,2,4,256]{4,3,0,1,2:T(4,128)(2,1)} %maximum_select_fusion.3), channel_id=1, source_target_pairs={{0,64},{8,72},{16,80},{24,88},{32,96},{40,104},{48,112},{56,120},{... | collective-permute-start | bytes 196616 | tf_op jit(solution)/shard_map/ppermute | solution.py:139
  84.7 9.3 %collective-permute-start.8 = (bf16[16,2,2,4,256]{4,3,0,1,2:T(4,128)(2,1)}, bf16[16,2,2,4,256]{4,3,0,1,2:T(4,128)(2,1)}, u32[]{:S(2)}, u32[]{:S(2)}) collective-permute-start(bf16[16,2,2,4,256]{4,3,0,1,2:T(4,128)(2,1)} %maximum_select_fusion.2), channel_id=1, source_target_pairs={{0,128},{8,136},{16,144},{24,152},{32,160},{40,168},{48,176},{56,1... | collective-permute-start | bytes 393224 | tf_op jit(solution)/shard_map/ppermute | solution.py:139
  90.1 12.7 %collective-permute-start.1 = (f32[304,128]{1,0:T(8,128)}, f32[304,128]{1,0:T(8,128)}, u32[]{:S(2)}, u32[]{:S(2)}) collective-permute-start(f32[304,128]{1,0:T(8,128)} %pad_maximum_fusion.5), channel_id=1, source_target_pairs={{8,0},{16,8},{24,16},{32,24},{40,32},{48,40},{56,48},{64,56},{72,6... | collective-permute-start | bytes 466952 | tf_op jit(solution)/shard_map/ppermute | solution.py:115
  95.4 11.2 %collective-permute-start.9 = (bf16[32,2,2,4,256]{4,3,0,1,2:T(4,128)(2,1)S(1)}, bf16[32,2,2,4,256]{4,3,0,1,2:T(4,128)(2,1)S(1)}, u32[]{:S(2)}, u32[]{:S(2)}) collective-permute-start(bf16[32,2,2,4,256]{4,3,0,1,2:T(4,128)(2,1)S(1)} %maximum_select_fusion.1), channel_id=1, source_target_pairs={{0,256},{8,264},{16,272},{24,280},{32,288},{40,296},{48,304},{56,3... | collective-permute-start | bytes 786440 | tf_op jit(solution)/shard_map/ppermute | solution.py:139
  108.7 26.9 %copy-start.20 = (f32[4,4,256]{2,1,0:T(4,128)S(1)}, f32[4,4,256]{2,1,0:T(4,128)}, u32[]{:S(2)}) copy-start(f32[4,4,256]{2,1,0:T(4,128)} %copy-done.19) | copy-start | bytes 49156
  108.7 26.9 %copy-start.22 = (f32[4,4,256]{2,1,0:T(4,128)S(1)}, f32[4,4,256]{2,1,0:T(4,128)}, u32[]{:S(2)}) copy-start(f32[4,4,256]{2,1,0:T(4,128)} %copy-done.21) | copy-start | bytes 49156
  108.7 6.6 %collective-permute-start.10 = (f32[4,2,2,4,256]{4,0,3,1,2:T(4,128)S(1)}, f32[4,2,2,4,256]{4,0,3,1,2:T(4,128)S(1)}, u32[]{:S(2)}, u32[]{:S(2)}) collective-permute-start(f32[4,2,2,4,256]{4,0,3,1,2:T(4,128)S(1)} %slice_select_fusion), channel_id=1, source_target_pairs={{0,4},{1,5},{2,6},{3,7},{4,0},{5,1},{6,2},{7,3},{8,12},{9,13},{10,... | collective-permute-start | bytes 196616 | tf_op jit(solution)/shard_map/ppermute | solution.py:158
  115.4 4.7 %collective-permute-start.11 = (f32[2,2,2,4,256]{4,0,3,1,2:T(2,128)S(1)}, f32[2,2,2,4,256]{4,0,3,1,2:T(2,128)S(1)}, u32[]{:S(2)}, u32[]{:S(2)}) collective-permute-start(f32[2,2,2,4,256]{4,0,3,1,2:T(2,128)S(1)} %broadcast_select_fusion), channel_id=1, source_target_pairs={{0,2},{1,3},{2,0},{3,1},{4,6},{5,7},{6,4},{7,5},{8,10},{9,11},{10,... | collective-permute-start | bytes 98312 | tf_op jit(solution)/shard_map/ppermute | solution.py:158
  120.1 15.4 %collective-permute-start.12 = (f32[1,2,2,4,256]{4,0,3,1,2:T(1,128)S(1)}, f32[1,2,2,4,256]{4,0,3,1,2:T(1,128)S(1)}, u32[]{:S(2)}, u32[]{:S(2)}) collective-permute-start(f32[1,2,2,4,256]{4,0,3,1,2:T(1,128)S(1)} %broadcast_select_fusion.1), channel_id=1, source_target_pairs={{0,1},{1,0},{2,3},{3,2},{4,5},{5,4},{6,7},{7,6},{8,9},{9,8},{10,11... | collective-permute-start | bytes 49160 | tf_op jit(solution)/shard_map/ppermute | solution.py:158
  130.1 14.1 %copy-start.6 = (bf16[2,128,128,1,1]{2,1,4,3,0:T(8,128)(2,1)S(1)}, bf16[2,128,128,1,1]{2,1,4,3,0:T(8,128)(2,1)}, u32[]{:S(2)}) copy-start(bf16[2,128,128,1,1]{2,1,4,3,0:T(8,128)(2,1)} %copy-done.5) | copy-start | bytes 196612
  130.1 8.4 %collective-permute-start.2 = (f32[800,128]{1,0:T(8,128)S(1)}, f32[800,128]{1,0:T(8,128)S(1)}, u32[]{:S(2)}, u32[]{:S(2)}) collective-permute-start(f32[800,128]{1,0:T(8,128)S(1)} %get-tuple-element.216), channel_id=1, source_target_pairs={{0,1},{1,2},{2,3},{3,4},{4,5},{5,6},{6,7},{8,9},{9,10},{10,11},{11... | collective-permute-start | bytes 1228808 | tf_op jit(solution)/shard_map/ppermute | solution.py:112
  133.6 9.3 %collective-permute-start.3 = (f32[800,128]{1,0:T(8,128)S(1)}, f32[800,128]{1,0:T(8,128)S(1)}, u32[]{:S(2)}, u32[]{:S(2)}) collective-permute-start(f32[800,128]{1,0:T(8,128)S(1)} %get-tuple-element.217), channel_id=1, source_target_pairs={{1,0},{2,1},{3,2},{4,3},{5,4},{6,5},{7,6},{9,8},{10,9},{11,10},{12... | collective-permute-start | bytes 1228808 | tf_op jit(solution)/shard_map/ppermute | solution.py:115
  (28 other events, 67.5 us)

commit v6 on v5

--- a/solution.py
+++ b/solution.py
@@ -130,34 +130,50 @@
     return cells.astype(jnp.bfloat16), placed[:, 1 : box_side + 1, 1 : box_side + 1]
 
 
+def step_order(count):
+    minor = 16 if count % 16 == 0 else count
+    steps = [1 << b for b in range(count.bit_length() - 1)]
+    low = [k for k in steps if k < minor]
+    high = [k for k in steps if k >= minor]
+    return low[::-1] + high[::-1]
+
+
 def gather_ordered(block, axis):
     count = lax.axis_size(axis)
     index = lax.axis_index(axis)
     held = block[None]
-    step = 1
-    while step < count:
+    steps = step_order(count)
+    for step in steps:
         other = lax.ppermute(held, axis, [(i, i ^ step) for i in range(count)])
         lower = (index & step) == 0
         held = jnp.where(
             lower, jnp.concatenate([held, other], 0), jnp.concatenate([other, held], 0)
         )
-        step *= 2
-    return held
+    bits = len(steps)
+    exps = [step.bit_length() - 1 for step in steps]
+    perm = [bits - 1 - exps.index(e) for e in range(bits - 1, -1, -1)]
+    held = held.reshape((2,) * bits + held.shape[1:])
+    held = jnp.transpose(held, perm + list(range(bits, held.ndim)))
+    return held.reshape((count,) + block.shape)
 
 
 def scatter_sum(parts, axis):
     count = lax.axis_size(axis)
     index = lax.axis_index(axis)
-    held = parts
-    step = count // 2
-    while step >= 1:
-        half = held.shape[0] // 2
+    bits = count.bit_length() - 1
+    held = parts.reshape((2,) * bits + parts.shape[1:])
+    remaining = list(range(bits - 1, -1, -1))
+    for exp in range(bits):
+        step = 1 << exp
+        at = remaining.index(exp)
         upper = (index & step) != 0
-        send = jnp.where(upper, held[:half], held[half:])
-        keep = jnp.where(upper, held[half:], held[:half])
+        lo = lax.index_in_dim(held, 0, at, keepdims=False)
+        hi = lax.index_in_dim(held, 1, at, keepdims=False)
+        send = jnp.where(upper, lo, hi)
+        keep = jnp.where(upper, hi, lo)
         held = keep + lax.ppermute(send, axis, [(i, i ^ step) for i in range(count)])
-        step //= 2
-    return held[0]
+        remaining.pop(at)
+    return held
 
 
 def coarse_exchange(top_b, coarse_tab):

time: 163 us -> 158 us (0.969)
  starting transfers between devices: 66.2 us -> 62.2 us
  waiting for transfers between devices: 15.2 us -> 13.2 us
    ppermute x6, starting transfers between devices: 36.3 us -> 34 us  [gather_ordered(): other = lax.ppermute(held, axis, [(i, i ^ step) for i in range(count)])]
    ppermute x3, starting transfers between devices: 18 us -> 16 us  [scatter_sum(): lax.ppermute(send, axis, [(i, i ^ step) for i in range(count)])]
    unnamed x82 -> x81, local copies, waits for them, and re-layouts: 8.65 us -> 9.48 us
    select_n x5 -> x6, other arithmetic: 7.51 us -> 8.09 us  [gather_ordered(): jnp.where(lower, jnp.concatenate([held, other], 0), jnp.concatenate([othe...]
  transfers between devices with their start and end apart: 13 -> 13, of which waited for: 6 -> 6; matrix products, arithmetic and copies ran while one was open for 28% -> 29% of each run, Pallas kernels for 0% -> 0%
where the time goes in v6:
time: 158 us; the launch traced here: 157 us
  starting transfers between devices  62.2 us (39%)
  local copies, waits for them, and re-layouts  33.6 us (21%)
  other arithmetic  32 us (20%)
  matrix products  13.5 us (9%)
  waiting for transfers between devices  13.2 us (8%)
  between operations  1.94 us (1%)
    ppermute x6, starting transfers between devices, gather_ordered(): other = lax.ppermute(held, axis, [(i, i ^ step) for i in range(count)])  34 us
    ppermute x3, starting transfers between devices, scatter_sum(): lax.ppermute(send, axis, [(i, i ^ step) for i in range(count)])  16 us
    dot_general x21, matrix products, product(): return jnp.einsum(form, left, right, preferred_element_type=jnp.float32)  9.68 us
    unnamed x81, local copies, waits for them, and re-layouts  9.48 us
    ppermute x2, starting transfers between devices, exchange_halo(): lax.ppermute(jnp.concatenate([flat, to_next.reshape(-1, lanes)]), axis, a...  9.05 us
    select_n x6, other arithmetic, gather_ordered(): jnp.where(lower, jnp.concatenate([held, other], 0), jnp.concatenate([othe...  8.09 us
    slice x2, local copies, waits for them, and re-layouts, coarse_exchange(): adj = jnp.stack([adj[0], -adj[1]])  4.45 us
    ppermute x2, waiting for transfers between devices, exchange_halo(): lax.ppermute(jnp.concatenate([flat, to_prev.reshape(-1, lanes)]), axis, b...  4.27 us
  transfers between devices with their start and end apart: 13, of which 6 were waited for; matrix products, arithmetic and copies ran while one was open for 29% of the time, Pallas kernels for 0%

profile of v6, /device:TPU:1, one launch (start us, length us, event | category | flops | bytes accessed | tf_op | source)
XLA Modules:
  0.0 156.5 jit_solution(3114821543637519483)
XLA Ops:
  9.2 1.9 %fusion.50 = f32[2,6,6,4,128]{4,3,0,2,1:T(4,128)S(1)} fusion(f32[2,6,6,4,128]{4,3,0,2,1:T(4,128)S(1)} %add_dynamic-update-slice_fusion, s32[]{:T(128)} %bitcast.24, s32[]{:T(128)} %bitcast.25, f32[2,4,4,4,128]{4,3,0,2,1:T(4,128)S(1)} %bitcast.403, pred[]{:T(512)} %and_reduce_fusion), kind=kLoop, calls=%fused_computation.122 | loop fusion | flops 32768 | bytes 196617 | tf_op jit(solution)/shard_map/scatter-add | solution.py:91
  12.9 5.0 %collective-permute-start = (f32[304,128]{1,0:T(8,128)}, f32[304,128]{1,0:T(8,128)}, u32[]{:S(2)}, u32[]{:S(2)}) collective-permute-start(f32[304,128]{1,0:T(8,128)} %pad_maximum_fusion.6), channel_id=1, source_target_pairs={{0,8},{8,16},{16,24},{24,32},{32,40},{40,48},{48,56},{56,64},{64,7... | collective-permute-start | bytes 466952 | tf_op jit(solution)/shard_map/ppermute | solution.py:112
  21.0 14.1 %collective-permute-start.4 = (bf16[1,2,2,4,256]{4,3,2,1,0:T(4,128)(2,1)}, bf16[1,2,2,4,256]{4,3,2,1,0:T(4,128)(2,1)}, u32[]{:S(2)}, u32[]{:S(2)}) collective-permute-start(bf16[1,2,2,4,256]{4,3,2,1,0:T(4,128)(2,1)} %pad_maximum_fusion.13), channel_id=1, source_target_pairs={{0,64},{8,72},{16,80},{24,88},{32,96},{40,104},{48,112},{56,120},{... | collective-permute-start | bytes 24584 | tf_op jit(solution)/shard_map/ppermute | solution.py:147
  36.9 2.1 %fusion.1 = f32[16,144,2,2,128]{4,1,3,2,0:T(8,128)S(1)} fusion(s32[16,144]{1,0:T(8,128)S(1)} %fusion.96, f32[1,2,225,128]{3,2,1,0:T(8,128)S(1)} %copy.826, f32[1,2,225,128]{3,2,1,0:T(8,128)S(1)} %copy.825), kind=kOutput, calls=%fused_computation.8 | convolution fusion | flops 3185683200 | bytes 5188608 | tf_op jit(solution)/shard_map/tnp,sxpq->tnsxq/dot_general | solution.py:230
  39.0 2.8 %slice_bitcast_fusion.1 = (f32[16,144,2,128]{3,1,2,0:T(8,128)}, f32[16,144,2,128]{3,1,2,0:T(8,128)}) fusion(f32[16,144,2,2,128]{4,1,3,2,0:T(8,128)S(1)} %fusion.1), kind=kLoop, calls=%fused_computation.5 | loop fusion | bytes 9437184 | tf_op jit(solution)/shard_map/mul | solution.py:236
  41.8 2.9 %constant_dynamic-slice_fusion.2 = (bf16[1,64,8,256]{3,0,2,1:T(2,128)(2,1)}, bf16[1,64,8,256]{3,0,2,1:T(2,128)(2,1)S(1)}) fusion(bf16[2,127,15,256]{3,0,2,1:T(2,128)(2,1)} %param.45, s32[]{:T(128)S(6)} %select_n.173, s32[]{:T(128)S(6)} %select_n.174, s32[]{:T(128)S(6)} %add.270), kind=kLoop, calls=%fused_computation.236 | loop fusion | bytes 1048588 | tf_op jit(solution)/shard_map/slice | solution.py:199
  51.1 3.0 %fusion.125 = (f32[2,1,64,8,256]{4,1,3,2,0:T(1,128)}, f32[2,1,64,8,256]{4,1,3,2,0:T(1,128)}) fusion(f32[2,2,64,8,256]{4,1,3,2,0:T(2,128)S(1)} %maximum_convert_fusion), kind=kLoop, calls=%fused_computation.263 | loop fusion | bytes 4194304 | tf_op jit(solution)/shard_map/slice | solution.py:205
  56.3 4.0 %collective-permute-start.5 = (bf16[2,2,2,4,256]{4,3,2,1,0:T(4,128)(2,1)}, bf16[2,2,2,4,256]{4,3,2,1,0:T(4,128)(2,1)}, u32[]{:S(2)}, u32[]{:S(2)}) collective-permute-start(bf16[2,2,2,4,256]{4,3,2,1,0:T(4,128)(2,1)} %maximum_select_fusion.5), channel_id=1, source_target_pairs={{0,32},{8,40},{16,48},{24,56},{32,0},{40,8},{48,16},{56,24},{64,96... | collective-permute-start | bytes 49160 | tf_op jit(solution)/shard_map/ppermute | solution.py:147
  60.4 2.8 %fusion.18 = (f32[2,64,8,256]{3,2,1,0:T(8,128)S(1)}, f32[2,64,8,256]{3,2,1,0:T(8,128)}) fusion(f32[2,1,64,8,256]{4,1,3,2,0:T(1,128)} %get-tuple-element.190, f32[64,8]{1,0:T(8,128)} %copy.835, f32[2,1,64,8,256]{4,1,3,2,0:T(1,128)} %get-tuple-element.191), kind=kLoop, calls=%fused_computation.42 | loop fusion | flops 524288 | bytes 4196352 | tf_op jit(solution)/shard_map/mul | solution.py:205
  63.1 1.9 %collective-permute-done.5 = bf16[2,2,2,4,256]{4,3,2,1,0:T(4,128)(2,1)} collective-permute-done((bf16[2,2,2,4,256]{4,3,2,1,0:T(4,128)(2,1)}, bf16[2,2,2,4,256]{4,3,2,1,0:T(4,128)(2,1)}, u32[]{:S(2)}, u32[]{:S(2)}) %collective-permute-start.5) | collective-permute-done | bytes 16416 | tf_op jit(solution)/shard_map/ppermute | solution.py:147
  66.5 3.1 %collective-permute-start.6 = (bf16[4,2,2,4,256]{4,3,2,1,0:T(4,128)(2,1)}, bf16[4,2,2,4,256]{4,3,2,1,0:T(4,128)(2,1)}, u32[]{:S(2)}, u32[]{:S(2)}) collective-permute-start(bf16[4,2,2,4,256]{4,3,2,1,0:T(4,128)(2,1)} %maximum_select_fusion.4), channel_id=1, source_target_pairs={{0,16},{8,24},{16,0},{24,8},{32,48},{40,56},{48,32},{56,40},{64,80... | collective-permute-start | bytes 98312 | tf_op jit(solution)/shard_map/ppermute | solution.py:147
  74.0 2.7 %collective-permute-start.7 = (bf16[8,2,2,4,256]{4,3,2,1,0:T(4,128)(2,1)}, bf16[8,2,2,4,256]{4,3,2,1,0:T(4,128)(2,1)}, u32[]{:S(2)}, u32[]{:S(2)}) collective-permute-start(bf16[8,2,2,4,256]{4,3,2,1,0:T(4,128)(2,1)} %maximum_select_fusion.3), channel_id=1, source_target_pairs={{0,8},{8,0},{16,24},{24,16},{32,40},{40,32},{48,56},{56,48},{64,72... | collective-permute-start | bytes 196616 | tf_op jit(solution)/shard_map/ppermute | solution.py:147
  81.2 4.8 %collective-permute-start.8 = (bf16[16,2,2,4,256]{4,3,2,1,0:T(4,128)(2,1)}, bf16[16,2,2,4,256]{4,3,2,1,0:T(4,128)(2,1)}, u32[]{:S(2)}, u32[]{:S(2)}) collective-permute-start(bf16[16,2,2,4,256]{4,3,2,1,0:T(4,128)(2,1)} %maximum_select_fusion.2), channel_id=1, source_target_pairs={{0,256},{8,264},{16,272},{24,280},{32,288},{40,296},{48,304},{56,3... | collective-permute-start | bytes 393224 | tf_op jit(solution)/shard_map/ppermute | solution.py:147
  93.4 5.4 %collective-permute-start.9 = (bf16[32,2,2,4,256]{4,3,2,1,0:T(4,128)(2,1)S(1)}, bf16[32,2,2,4,256]{4,3,2,1,0:T(4,128)(2,1)S(1)}, u32[]{:S(2)}, u32[]{:S(2)}) collective-permute-start(bf16[32,2,2,4,256]{4,3,2,1,0:T(4,128)(2,1)S(1)} %maximum_select_fusion.1), channel_id=1, source_target_pairs={{0,128},{8,136},{16,144},{24,152},{32,160},{40,168},{48,176},{56,1... | collective-permute-start | bytes 786440 | tf_op jit(solution)/shard_map/ppermute | solution.py:147
  100.6 2.2 %collective-permute-done.9 = bf16[32,2,2,4,256]{4,3,2,1,0:T(4,128)(2,1)S(1)} collective-permute-done((bf16[32,2,2,4,256]{4,3,2,1,0:T(4,128)(2,1)S(1)}, bf16[32,2,2,4,256]{4,3,2,1,0:T(4,128)(2,1)S(1)}, u32[]{:S(2)}, u32[]{:S(2)}) %collective-permute-start.9) | collective-permute-done | bytes 262176 | tf_op jit(solution)/shard_map/ppermute | solution.py:147
  106.3 7.8 %collective-permute-start.10 = (f32[2,2,2,2,4,256]{5,4,3,2,1,0:T(4,128)S(1)}, f32[2,2,2,2,4,256]{5,4,3,2,1,0:T(4,128)S(1)}, u32[]{:S(2)}, u32[]{:S(2)}) collective-permute-start(f32[2,2,2,2,4,256]{5,4,3,2,1,0:T(4,128)S(1)} %select_bitcast_fusion), channel_id=1, source_target_pairs={{0,1},{1,0},{2,3},{3,2},{4,5},{5,4},{6,7},{7,6},{8,9},{9,8},{10,11... | collective-permute-start | bytes 196616 | tf_op jit(solution)/shard_map/ppermute | solution.py:174
  115.1 3.2 %collective-permute-start.11 = (f32[2,2,2,4,256]{4,3,2,1,0:T(4,128)S(1)}, f32[2,2,2,4,256]{4,3,2,1,0:T(4,128)S(1)}, u32[]{:S(2)}, u32[]{:S(2)}) collective-permute-start(f32[2,2,2,4,256]{4,3,2,1,0:T(4,128)S(1)} %select_bitcast_fusion.1), channel_id=1, source_target_pairs={{0,2},{1,3},{2,0},{3,1},{4,6},{5,7},{6,4},{7,5},{8,10},{9,11},{10,... | collective-permute-start | bytes 98312 | tf_op jit(solution)/shard_map/ppermute | solution.py:174
  119.8 4.9 %collective-permute-start.12 = (f32[2,2,4,256]{3,2,1,0:T(4,128)S(1)}, f32[2,2,4,256]{3,2,1,0:T(4,128)S(1)}, u32[]{:S(2)}, u32[]{:S(2)}) collective-permute-start(f32[2,2,4,256]{3,2,1,0:T(4,128)S(1)} %select_bitcast_fusion.2), channel_id=1, source_target_pairs={{0,4},{1,5},{2,6},{3,7},{4,0},{5,1},{6,2},{7,3},{8,12},{9,13},{10,... | collective-permute-start | bytes 49160 | tf_op jit(solution)/shard_map/ppermute | solution.py:174
  124.9 4.0 %collective-permute-start.2 = (f32[800,128]{1,0:T(8,128)S(1)}, f32[800,128]{1,0:T(8,128)S(1)}, u32[]{:S(2)}, u32[]{:S(2)}) collective-permute-start(f32[800,128]{1,0:T(8,128)S(1)} %get-tuple-element.216), channel_id=1, source_target_pairs={{0,1},{1,2},{2,3},{3,4},{4,5},{5,6},{6,7},{8,9},{9,10},{10,11},{11... | collective-permute-start | bytes 1228808 | tf_op jit(solution)/shard_map/ppermute | solution.py:112
  128.9 1.9 %collective-permute-start.3 = (f32[800,128]{1,0:T(8,128)S(1)}, f32[800,128]{1,0:T(8,128)S(1)}, u32[]{:S(2)}, u32[]{:S(2)}) collective-permute-start(f32[800,128]{1,0:T(8,128)S(1)} %get-tuple-element.217), channel_id=1, source_target_pairs={{1,0},{2,1},{3,2},{4,3},{5,4},{6,5},{7,6},{9,8},{10,9},{11,10},{12... | collective-permute-start | bytes 1228808 | tf_op jit(solution)/shard_map/ppermute | solution.py:115
  131.0 2.8 %collective-permute-done.2 = f32[800,128]{1,0:T(8,128)S(1)} collective-permute-done((f32[800,128]{1,0:T(8,128)S(1)}, f32[800,128]{1,0:T(8,128)S(1)}, u32[]{:S(2)}, u32[]{:S(2)}) %collective-permute-start.2) | collective-permute-done | bytes 409632 | tf_op jit(solution)/shard_map/ppermute | solution.py:112
  133.9 4.3 %collective-permute-done.3 = f32[800,128]{1,0:T(8,128)S(1)} collective-permute-done((f32[800,128]{1,0:T(8,128)S(1)}, f32[800,128]{1,0:T(8,128)S(1)}, u32[]{:S(2)}, u32[]{:S(2)}) %collective-permute-start.3) | collective-permute-done | bytes 409632 | tf_op jit(solution)/shard_map/ppermute | solution.py:115
  143.5 3.5 %subtract_reduce_fusion = (f32[16,2,4,128]{3,2,1,0:T(4,128)S(1)}, f32[16,2,4,128]{3,2,1,0:T(4,128)S(1)}) fusion(f32[144,2,4,128]{3,0,2,1:T(8,128)S(1)} %copy.831, f32[16,144,2,128]{3,1,2,0:T(8,128)S(1)} %copy-done.3, f32[144,2,4,128]{3,0,2,1:T(8,128)S(1)} %copy.830, f32[16,144,2,128]{3,1,2,0:T(8,128)S(1)} %copy-done.2), kind=kLoop, calls=%fused_computation.1 | loop fusion | flops 18841600 | bytes 6029312 | tf_op jit(solution)/shard_map/reduce_sum | solution.py:236
  150.4 1.8 %stack.196 = bf16[9,2,4,4,4,128]{5,0,4,1,3,2:T(8,128)(2,1)S(1)} concatenate(bf16[1,2,4,4,4,128]{5,0,4,1,3,2:T(2,128)(2,1)S(1)} %copy.812, bf16[1,2,4,4,4,128]{5,0,4,1,3,2:T(2,128)(2,1)S(1)} %copy.813, bf16[1,2,4,4,4,128]{5,0,4,1,3,2:T(2,128)(2,1)S(1)} %copy.814, bf16[1,2,4,4,4,128]{5,0,4,1,3,2:T(2,128)(2,1)S(1)} %copy.815, bf16[1,2,4,4,4,128]{5,0,4,1,3,2:T(2,128)(2,1)S(1)} %copy.816, ...), dimensions={0} | concatenate | bytes 589824 | tf_op jit(solution)/shard_map/stack | solution.py:50
  (235 shorter events, 61.8 us)
Async XLA Ops:
  0.6 18.6 %copy-start = (f32[256,128]{1,0:T(8,128)S(1)}, f32[256,128]{1,0:T(8,128)}, u32[]{:S(2)}) copy-start(f32[256,128]{1,0:T(8,128)} %param.42) | copy-start | bytes 393220
  4.5 6.9 %copy-start.31 = (bf16[2,4,4,4,128]{4,3,2,1,0:T(4,128)(2,1)S(1)}, bf16[2,4,4,4,128]{4,3,2,1,0:T(4,128)(2,1)}, u32[]{:S(2)}) copy-start(bf16[2,4,4,4,128]{4,3,2,1,0:T(4,128)(2,1)} %param.36) | copy-start | bytes 98308
  5.3 12.6 %copy-start.10 = (bf16[2,128,128]{2,1,0:T(8,128)(2,1)S(1)}, bf16[2,128,128]{2,1,0:T(8,128)(2,1)}, u32[]{:S(2)}) copy-start(bf16[2,128,128]{2,1,0:T(8,128)(2,1)} %param.41) | copy-start | bytes 196612
  5.3 12.9 %copy-start.16 = (bf16[2,128,128]{2,1,0:T(8,128)(2,1)S(1)}, bf16[2,128,128]{2,1,0:T(8,128)(2,1)}, u32[]{:S(2)}) copy-start(bf16[2,128,128]{2,1,0:T(8,128)(2,1)} %param.40) | copy-start | bytes 196612
  7.9 11.1 %copy-start.32 = (f32[16,256]{1,0:T(8,128)S(1)}, f32[16,256]{1,0:T(8,128)}, u32[]{:S(2)}) copy-start(f32[16,256]{1,0:T(8,128)} %param.43) | copy-start | bytes 49156
  11.3 24.9 %copy-start.13 = (f32[2,15,15,128]{3,0,2,1:T(2,128)S(1)}, f32[2,15,15,128]{3,0,2,1:T(2,128)}, u32[]{:S(2)}) copy-start(f32[2,15,15,128]{3,0,2,1:T(2,128)} %param.44) | copy-start | bytes 691204
  12.9 73.1 %collective-permute-start = (f32[304,128]{1,0:T(8,128)}, f32[304,128]{1,0:T(8,128)}, u32[]{:S(2)}, u32[]{:S(2)}) collective-permute-start(f32[304,128]{1,0:T(8,128)} %pad_maximum_fusion.6), channel_id=1, source_target_pairs={{0,8},{8,16},{16,24},{24,32},{32,40},{40,48},{48,56},{56,64},{64,7... | collective-permute-start | bytes 466952 | tf_op jit(solution)/shard_map/ppermute | solution.py:112
  19.2 17.2 %copy-start.19 = (f32[4,4,256]{2,1,0:T(4,128)}, f32[4,4,256]{2,1,0:T(4,128)S(1)}, u32[]{:S(2)}) copy-start(f32[4,4,256]{2,1,0:T(4,128)S(1)} %cos.11) | copy-start | bytes 49156
  19.2 17.2 %copy-start.21 = (f32[4,4,256]{2,1,0:T(4,128)}, f32[4,4,256]{2,1,0:T(4,128)S(1)}, u32[]{:S(2)}) copy-start(f32[4,4,256]{2,1,0:T(4,128)S(1)} %sin.11) | copy-start | bytes 49156
  21.0 33.9 %collective-permute-start.4 = (bf16[1,2,2,4,256]{4,3,2,1,0:T(4,128)(2,1)}, bf16[1,2,2,4,256]{4,3,2,1,0:T(4,128)(2,1)}, u32[]{:S(2)}, u32[]{:S(2)}) collective-permute-start(bf16[1,2,2,4,256]{4,3,2,1,0:T(4,128)(2,1)} %pad_maximum_fusion.13), channel_id=1, source_target_pairs={{0,64},{8,72},{16,80},{24,88},{32,96},{40,104},{48,112},{56,120},{... | collective-permute-start | bytes 24584 | tf_op jit(solution)/shard_map/ppermute | solution.py:147
  56.3 8.7 %collective-permute-start.5 = (bf16[2,2,2,4,256]{4,3,2,1,0:T(4,128)(2,1)}, bf16[2,2,2,4,256]{4,3,2,1,0:T(4,128)(2,1)}, u32[]{:S(2)}, u32[]{:S(2)}) collective-permute-start(bf16[2,2,2,4,256]{4,3,2,1,0:T(4,128)(2,1)} %maximum_select_fusion.5), channel_id=1, source_target_pairs={{0,32},{8,40},{16,48},{24,56},{32,0},{40,8},{48,16},{56,24},{64,96... | collective-permute-start | bytes 49160 | tf_op jit(solution)/shard_map/ppermute | solution.py:147
  66.5 6.0 %collective-permute-start.6 = (bf16[4,2,2,4,256]{4,3,2,1,0:T(4,128)(2,1)}, bf16[4,2,2,4,256]{4,3,2,1,0:T(4,128)(2,1)}, u32[]{:S(2)}, u32[]{:S(2)}) collective-permute-start(bf16[4,2,2,4,256]{4,3,2,1,0:T(4,128)(2,1)} %maximum_select_fusion.4), channel_id=1, source_target_pairs={{0,16},{8,24},{16,0},{24,8},{32,48},{40,56},{48,32},{56,40},{64,80... | collective-permute-start | bytes 98312 | tf_op jit(solution)/shard_map/ppermute | solution.py:147
  74.0 5.5 %collective-permute-start.7 = (bf16[8,2,2,4,256]{4,3,2,1,0:T(4,128)(2,1)}, bf16[8,2,2,4,256]{4,3,2,1,0:T(4,128)(2,1)}, u32[]{:S(2)}, u32[]{:S(2)}) collective-permute-start(bf16[8,2,2,4,256]{4,3,2,1,0:T(4,128)(2,1)} %maximum_select_fusion.3), channel_id=1, source_target_pairs={{0,8},{8,0},{16,24},{24,16},{32,40},{40,32},{48,56},{56,48},{64,72... | collective-permute-start | bytes 196616 | tf_op jit(solution)/shard_map/ppermute | solution.py:147
  81.2 10.8 %collective-permute-start.8 = (bf16[16,2,2,4,256]{4,3,2,1,0:T(4,128)(2,1)}, bf16[16,2,2,4,256]{4,3,2,1,0:T(4,128)(2,1)}, u32[]{:S(2)}, u32[]{:S(2)}) collective-permute-start(bf16[16,2,2,4,256]{4,3,2,1,0:T(4,128)(2,1)} %maximum_select_fusion.2), channel_id=1, source_target_pairs={{0,256},{8,264},{16,272},{24,280},{32,288},{40,296},{48,304},{56,3... | collective-permute-start | bytes 393224 | tf_op jit(solution)/shard_map/ppermute | solution.py:147
  88.3 10.5 %collective-permute-start.1 = (f32[304,128]{1,0:T(8,128)}, f32[304,128]{1,0:T(8,128)}, u32[]{:S(2)}, u32[]{:S(2)}) collective-permute-start(f32[304,128]{1,0:T(8,128)} %pad_maximum_fusion.5), channel_id=1, source_target_pairs={{8,0},{16,8},{24,16},{32,24},{40,32},{48,40},{56,48},{64,56},{72,6... | collective-permute-start | bytes 466952 | tf_op jit(solution)/shard_map/ppermute | solution.py:115
  93.4 9.4 %collective-permute-start.9 = (bf16[32,2,2,4,256]{4,3,2,1,0:T(4,128)(2,1)S(1)}, bf16[32,2,2,4,256]{4,3,2,1,0:T(4,128)(2,1)S(1)}, u32[]{:S(2)}, u32[]{:S(2)}) collective-permute-start(bf16[32,2,2,4,256]{4,3,2,1,0:T(4,128)(2,1)S(1)} %maximum_select_fusion.1), channel_id=1, source_target_pairs={{0,128},{8,136},{16,144},{24,152},{32,160},{40,168},{48,176},{56,1... | collective-permute-start | bytes 786440 | tf_op jit(solution)/shard_map/ppermute | solution.py:147
  106.3 24.6 %copy-start.20 = (f32[4,4,256]{2,1,0:T(4,128)S(1)}, f32[4,4,256]{2,1,0:T(4,128)}, u32[]{:S(2)}) copy-start(f32[4,4,256]{2,1,0:T(4,128)} %copy-done.19) | copy-start | bytes 49156
  106.3 24.6 %copy-start.22 = (f32[4,4,256]{2,1,0:T(4,128)S(1)}, f32[4,4,256]{2,1,0:T(4,128)}, u32[]{:S(2)}) copy-start(f32[4,4,256]{2,1,0:T(4,128)} %copy-done.21) | copy-start | bytes 49156
  106.3 8.7 %collective-permute-start.10 = (f32[2,2,2,2,4,256]{5,4,3,2,1,0:T(4,128)S(1)}, f32[2,2,2,2,4,256]{5,4,3,2,1,0:T(4,128)S(1)}, u32[]{:S(2)}, u32[]{:S(2)}) collective-permute-start(f32[2,2,2,2,4,256]{5,4,3,2,1,0:T(4,128)S(1)} %select_bitcast_fusion), channel_id=1, source_target_pairs={{0,1},{1,0},{2,3},{3,2},{4,5},{5,4},{6,7},{7,6},{8,9},{9,8},{10,11... | collective-permute-start | bytes 196616 | tf_op jit(solution)/shard_map/ppermute | solution.py:174
  115.1 4.7 %collective-permute-start.11 = (f32[2,2,2,4,256]{4,3,2,1,0:T(4,128)S(1)}, f32[2,2,2,4,256]{4,3,2,1,0:T(4,128)S(1)}, u32[]{:S(2)}, u32[]{:S(2)}) collective-permute-start(f32[2,2,2,4,256]{4,3,2,1,0:T(4,128)S(1)} %select_bitcast_fusion.1), channel_id=1, source_target_pairs={{0,2},{1,3},{2,0},{3,1},{4,6},{5,7},{6,4},{7,5},{8,10},{9,11},{10,... | collective-permute-start | bytes 98312 | tf_op jit(solution)/shard_map/ppermute | solution.py:174
  119.8 11.0 %collective-permute-start.12 = (f32[2,2,4,256]{3,2,1,0:T(4,128)S(1)}, f32[2,2,4,256]{3,2,1,0:T(4,128)S(1)}, u32[]{:S(2)}, u32[]{:S(2)}) collective-permute-start(f32[2,2,4,256]{3,2,1,0:T(4,128)S(1)} %select_bitcast_fusion.2), channel_id=1, source_target_pairs={{0,4},{1,5},{2,6},{3,7},{4,0},{5,1},{6,2},{7,3},{8,12},{9,13},{10,... | collective-permute-start | bytes 49160 | tf_op jit(solution)/shard_map/ppermute | solution.py:174
  124.9 14.6 %copy-start.6 = (bf16[2,128,128,1,1]{2,1,4,3,0:T(8,128)(2,1)S(1)}, bf16[2,128,128,1,1]{2,1,4,3,0:T(8,128)(2,1)}, u32[]{:S(2)}) copy-start(bf16[2,128,128,1,1]{2,1,4,3,0:T(8,128)(2,1)} %copy-done.5) | copy-start | bytes 196612
  124.9 8.9 %collective-permute-start.2 = (f32[800,128]{1,0:T(8,128)S(1)}, f32[800,128]{1,0:T(8,128)S(1)}, u32[]{:S(2)}, u32[]{:S(2)}) collective-permute-start(f32[800,128]{1,0:T(8,128)S(1)} %get-tuple-element.216), channel_id=1, source_target_pairs={{0,1},{1,2},{2,3},{3,4},{4,5},{5,6},{6,7},{8,9},{9,10},{10,11},{11... | collective-permute-start | bytes 1228808 | tf_op jit(solution)/shard_map/ppermute | solution.py:112
  128.9 9.3 %collective-permute-start.3 = (f32[800,128]{1,0:T(8,128)S(1)}, f32[800,128]{1,0:T(8,128)S(1)}, u32[]{:S(2)}, u32[]{:S(2)}) collective-permute-start(f32[800,128]{1,0:T(8,128)S(1)} %get-tuple-element.217), channel_id=1, source_target_pairs={{1,0},{2,1},{3,2},{4,3},{5,4},{6,5},{7,6},{9,8},{10,9},{11,10},{12... | collective-permute-start | bytes 1228808 | tf_op jit(solution)/shard_map/ppermute | solution.py:115
  (28 other events, 65.1 us)

commit v7 on v6

--- a/solution.py
+++ b/solution.py
@@ -4,33 +4,6 @@
 from jax.sharding import PartitionSpec as P
 
 HIGH = lax.Precision.HIGHEST
-
-
-def with_halo(cells, sides, width):
-    for axis, dim in sides:
-        count = lax.axis_size(axis)
-        ends = count - 1
-        head = lax.slice_in_dim(cells, 0, width, axis=dim)
-        tail = lax.slice_in_dim(cells, cells.shape[dim] - width, cells.shape[dim], axis=dim)
-        cells = jnp.concatenate(
-            [
-                lax.ppermute(tail, axis, [(i, (i + 1) % count) for i in range(ends)]),
-                cells,
-                lax.ppermute(head, axis, [((i + 1) % count, i) for i in range(ends)]),
-            ],
-            axis=dim,
-        )
-    return cells
-
-
-def from_behind(block, axis, distance):
-    devices = range(lax.axis_size(axis))
-    route = [(i - distance, i) for i in devices if i - distance in devices]
-    return lax.ppermute(block, axis, route)
-
-
-def complex_mul(left_re, left_im, right_re, right_im):
-    return (left_re * right_re - left_im * right_im, left_re * right_im + left_im * right_re)
 
 
 def conj_flip(table, axes):
@@ -109,12 +82,8 @@
             to_next = placed[:, 1 : box_side + 1, box_side + 1]
             to_prev = placed[:, 1 : box_side + 1, 0]
         edge_shape = to_next.shape
-        from_prev = lax.ppermute(
-            jnp.concatenate([flat, to_next.reshape(-1, lanes)]), axis, ahead
-        )
-        from_next = lax.ppermute(
-            jnp.concatenate([flat, to_prev.reshape(-1, lanes)]), axis, behind
-        )
+        from_prev = lax.ppermute(jnp.concatenate([flat, to_next.reshape(-1, lanes)]), axis, ahead)
+        from_next = lax.ppermute(jnp.concatenate([flat, to_prev.reshape(-1, lanes)]), axis, behind)
         if axis == "row":
             placed = placed.at[:, 1].add(from_prev[size:].reshape(edge_shape))
             placed = placed.at[:, box_side].add(from_next[size:].reshape(edge_shape))
@@ -136,25 +105,6 @@
     low = [k for k in steps if k < minor]
     high = [k for k in steps if k >= minor]
     return low[::-1] + high[::-1]
-
-
-def gather_ordered(block, axis):
-    count = lax.axis_size(axis)
-    index = lax.axis_index(axis)
-    held = block[None]
-    steps = step_order(count)
-    for step in steps:
-        other = lax.ppermute(held, axis, [(i, i ^ step) for i in range(count)])
-        lower = (index & step) == 0
-        held = jnp.where(
-            lower, jnp.concatenate([held, other], 0), jnp.concatenate([other, held], 0)
-        )
-    bits = len(steps)
-    exps = [step.bit_length() - 1 for step in steps]
-    perm = [bits - 1 - exps.index(e) for e in range(bits - 1, -1, -1)]
-    held = held.reshape((2,) * bits + held.shape[1:])
-    held = jnp.transpose(held, perm + list(range(bits, held.ndim)))
-    return held.reshape((count,) + block.shape)
 
 
 def scatter_sum(parts, axis):
@@ -176,12 +126,35 @@
     return held
 
 
+def gather_halves(block, axis):
+    count = lax.axis_size(axis)
+    index = lax.axis_index(axis)
+    held = block[None]
+    steps = step_order(count)
+    for step in steps[:-1]:
+        other = lax.ppermute(held, axis, [(i, i ^ step) for i in range(count)])
+        lower = (index & step) == 0
+        held = jnp.where(
+            lower, jnp.concatenate([held, other], 0), jnp.concatenate([other, held], 0)
+        )
+    bits = len(steps) - 1
+    exps = [step.bit_length() - 1 for step in steps[:-1]]
+    order = sorted(exps, reverse=True)
+    perm = [bits - 1 - exps.index(e) for e in order]
+    held = held.reshape((2,) * bits + held.shape[1:])
+    held = jnp.transpose(held, perm + list(range(bits, held.ndim)))
+    held = held.reshape((count // 2,) + block.shape)
+    last = steps[-1]
+    other = lax.ppermute(held, axis, [(i, i ^ last) for i in range(count)])
+    return held, other, last
+
+
 def coarse_exchange(top_b, coarse_tab):
     row_count = lax.axis_size("row")
     col_count = lax.axis_size("col")
     row_idx = lax.axis_index("row")
     col_idx = lax.axis_index("col")
-    sources = gather_ordered(top_b, "row").astype(jnp.float32)
+    mine, theirs, last = gather_halves(top_b, "row")
     zero = jnp.zeros((), jnp.int32)
     fwd_tab = coarse_tab[0]
     fwd = lax.dynamic_slice(
@@ -204,12 +177,24 @@
     weight = distant.astype(jnp.float32)[None, :, :, None]
     coef_re = coeff[:, 0] * weight
     coef_im = coeff[:, 1] * weight
-    val_re = jnp.moveaxis(sources[:, :, 0], 0, 1)[:, :, None]
-    val_im = jnp.moveaxis(sources[:, :, 1], 0, 1)[:, :, None]
-    c_re = coef_re[:, :, :, None]
-    c_im = coef_im[:, :, :, None]
-    got_re = (c_re * val_re - c_im * val_im).sum(1)
-    got_im = (c_re * val_im + c_im * val_re).sum(1)
+    own_bit = (row_idx // last) % 2
+
+    def half(coef, bit):
+        shape = coef.shape
+        coef = coef.reshape((shape[0], row_count // (2 * last), 2, last) + shape[2:])
+        coef = lax.dynamic_index_in_dim(coef, bit, 2, keepdims=False)
+        return coef.reshape((shape[0], row_count // 2) + shape[2:])[:, :, :, None]
+
+    def partial(sources, c_re, c_im):
+        sources = sources.astype(jnp.float32)
+        val_re = jnp.moveaxis(sources[:, :, 0], 0, 1)[:, :, None]
+        val_im = jnp.moveaxis(sources[:, :, 1], 0, 1)[:, :, None]
+        return (c_re * val_re - c_im * val_im).sum(1), (c_re * val_im + c_im * val_re).sum(1)
+
+    near_re, near_im = partial(mine, half(coef_re, own_bit), half(coef_im, own_bit))
+    far_re, far_im = partial(theirs, half(coef_re, 1 - own_bit), half(coef_im, 1 - own_bit))
+    got_re = near_re + far_re
+    got_im = near_im + far_im
     parts = jnp.moveaxis(jnp.stack([got_re, got_im], 1), 2, 0)
     return scatter_sum(parts, "col")
 
@@ -251,8 +236,6 @@
 
 def far_field(own, vectors, rad_tab, rcv_tab, leaf_tab, coarse_tab, interp, phase):
     box_side = own.shape[2]
-    span = 3 * box_side
-    reach = 2 * box_side - 1
     leaf_out = radiate(own, rad_tab)
     window = radiate(vectors, rad_tab)
     leaf_in = leaf_incoming(window, leaf_tab, box_side)
@@ -281,7 +264,7 @@
     return jnp.stack([res_re, res_im], 1)
 
 
-def per_device(
+def per_device_body(
     current,
     probe,
     near_list,
@@ -334,7 +317,7 @@
         P(),
     )
     return jax.shard_map(
-        per_device,
+        per_device_body,
         mesh=mesh,
         in_specs=placed,
         out_specs=(P(None, "row", "col", None, None), P(None, "row", "col", None, None)),

time: 158 us -> 155 us (0.981)
  other arithmetic: 32 us -> 26.9 us
  waiting for transfers between devices: 13.2 us -> 16.6 us
  local copies, waits for them, and re-layouts: 33.6 us -> 31.5 us
    select_n x6 -> x5, other arithmetic: 8.09 us -> 4.21 us  [gather_halves(): jnp.where(lower, jnp.concatenate([held, other], 0), jnp.concatenate([othe...]
    dynamic_slice x0 -> x2, local copies, waits for them, and re-layouts: none -> 3.47 us  [half(): coef = lax.dynamic_index_in_dim(coef, bit, 2, keepdims=False)]
    ppermute x6, waiting for transfers between devices: 4.1 us -> 7.43 us  [the longest x5 4.63 us: gather_halves(): other = lax.ppermute(held, axis, [(i, i ^ step) for i in range(count)])]
    unnamed x81 -> x83, local copies, waits for them, and re-layouts: 9.48 us -> 8.71 us
  transfers between devices with their start and end apart: 13 -> 13, of which waited for: 6 -> 8; matrix products, arithmetic and copies ran while one was open for 29% -> 27% of each run, Pallas kernels for 0% -> 0%
where the time goes in v7:
time: 155 us; the launch traced here: 153 us
  starting transfers between devices  62.8 us (41%)
  local copies, waits for them, and re-layouts  31.5 us (20%)
  other arithmetic  26.9 us (17%)
  waiting for transfers between devices  16.6 us (11%)
  matrix products  13.5 us (9%)
  between operations  2.06 us (1%)
    ppermute x5, starting transfers between devices, gather_halves(): other = lax.ppermute(held, axis, [(i, i ^ step) for i in range(count)])  28.6 us
    ppermute x3, starting transfers between devices, scatter_sum(): lax.ppermute(send, axis, [(i, i ^ step) for i in range(count)])  16 us
    dot_general x21, matrix products, product(): return jnp.einsum(form, left, right, preferred_element_type=jnp.float32)  9.67 us
    ppermute x2, starting transfers between devices, exchange_halo(): lax.ppermute(jnp.concatenate([flat, to_next.reshape(-1, lanes)]), axis, a...  9.05 us
    unnamed x83, local copies, waits for them, and re-layouts  8.71 us
    ppermute x1, starting transfers between devices, gather_halves(): other = lax.ppermute(held, axis, [(i, i ^ last) for i in range(count)])  5.75 us
    ppermute x5, waiting for transfers between devices, gather_halves(): other = lax.ppermute(held, axis, [(i, i ^ step) for i in range(count)])  4.63 us
    slice x2, local copies, waits for them, and re-layouts, coarse_exchange(): adj = jnp.stack([adj[0], -adj[1]])  4.44 us
  transfers between devices with their start and end apart: 13, of which 8 were waited for; matrix products, arithmetic and copies ran while one was open for 27% of the time, Pallas kernels for 0%

profile of v7, /device:TPU:1, one launch (start us, length us, event | category | flops | bytes accessed | tf_op | source)
XLA Modules:
  0.0 153.3 jit_solution(17958233575944405698)
XLA Ops:
  9.2 2.0 %fusion.49 = f32[2,6,6,4,128]{4,3,0,2,1:T(4,128)S(1)} fusion(f32[2,6,6,4,128]{4,3,0,2,1:T(4,128)S(1)} %add_dynamic-update-slice_fusion, s32[]{:T(128)} %bitcast.24, s32[]{:T(128)} %bitcast.25, f32[2,4,4,4,128]{4,3,0,2,1:T(4,128)S(1)} %bitcast.419, pred[]{:T(512)} %and_reduce_fusion), kind=kLoop, calls=%fused_computation.123 | loop fusion | flops 32768 | bytes 196617 | tf_op jit(solution)/shard_map/scatter-add | solution.py:64
  12.9 5.0 %collective-permute-start = (f32[304,128]{1,0:T(8,128)}, f32[304,128]{1,0:T(8,128)}, u32[]{:S(2)}, u32[]{:S(2)}) collective-permute-start(f32[304,128]{1,0:T(8,128)} %pad_maximum_fusion.6), channel_id=1, source_target_pairs={{0,8},{8,16},{16,24},{24,32},{32,40},{40,48},{48,56},{56,64},{64,7... | collective-permute-start | bytes 466952 | tf_op jit(solution)/shard_map/ppermute | solution.py:85
  20.5 14.1 %collective-permute-start.4 = (bf16[1,2,2,4,256]{4,3,2,1,0:T(4,128)(2,1)}, bf16[1,2,2,4,256]{4,3,2,1,0:T(4,128)(2,1)}, u32[]{:S(2)}, u32[]{:S(2)}) collective-permute-start(bf16[1,2,2,4,256]{4,3,2,1,0:T(4,128)(2,1)} %pad_maximum_fusion.13), channel_id=1, source_target_pairs={{0,64},{8,72},{16,80},{24,88},{32,96},{40,104},{48,112},{56,120},{... | collective-permute-start | bytes 24584 | tf_op jit(solution)/shard_map/ppermute | solution.py:135
  37.0 2.1 %fusion.1 = f32[16,144,2,2,128]{4,1,3,2,0:T(8,128)S(1)} fusion(s32[16,144]{1,0:T(8,128)S(1)} %fusion.95, f32[1,2,225,128]{3,2,1,0:T(8,128)S(1)} %copy.752, f32[1,2,225,128]{3,2,1,0:T(8,128)S(1)} %copy.751), kind=kOutput, calls=%fused_computation.6 | convolution fusion | flops 3185683200 | bytes 5188608 | tf_op jit(solution)/shard_map/tnp,sxpq->tnsxq/dot_general | solution.py:215
  39.1 2.8 %slice_bitcast_fusion.1 = (f32[16,144,2,128]{3,1,2,0:T(8,128)}, f32[16,144,2,128]{3,1,2,0:T(8,128)}) fusion(f32[16,144,2,2,128]{4,1,3,2,0:T(8,128)S(1)} %fusion.1), kind=kLoop, calls=%fused_computation.3 | loop fusion | bytes 9437184 | tf_op jit(solution)/shard_map/mul | solution.py:221
  41.9 2.9 %constant_dynamic-slice_fusion.6 = (bf16[1,64,8,256]{3,0,2,1:T(2,128)(2,1)}, bf16[1,64,8,256]{3,0,2,1:T(2,128)(2,1)S(1)}) fusion(bf16[2,127,15,256]{3,0,2,1:T(2,128)(2,1)} %param.45, s32[]{:T(128)S(6)} %select_n.186, s32[]{:T(128)S(6)} %select_n.187, s32[]{:T(128)S(6)} %add.324), kind=kLoop, calls=%fused_computation.244 | loop fusion | bytes 1048588 | tf_op jit(solution)/shard_map/slice | solution.py:172
  56.2 2.8 %broadcast_multiply_fusion.1 = (f32[2,2,2,16,8,256]{5,4,3,2,1,0:T(8,128)}, f32[2,2,2,16,8,256]{5,4,3,2,1,0:T(8,128)}) fusion(f32[2,2,2,16,8,256]{5,4,3,2,1,0:T(8,128)S(1)} %bitcast.390, f32[2,2,16,8]{3,2,1,0:T(8,128)S(1)} %or_convert_fusion, f32[2,2,2,16,8,256]{5,4,3,2,1,0:T(8,128)} %bitcast.391), kind=kLoop, calls=%fused_computation.66 | loop fusion | flops 524288 | bytes 4196352 | tf_op jit(solution)/shard_map/mul | solution.py:178
  61.0 4.0 %collective-permute-start.5 = (bf16[2,2,2,4,256]{4,3,2,1,0:T(4,128)(2,1)}, bf16[2,2,2,4,256]{4,3,2,1,0:T(4,128)(2,1)}, u32[]{:S(2)}, u32[]{:S(2)}) collective-permute-start(bf16[2,2,2,4,256]{4,3,2,1,0:T(4,128)(2,1)} %maximum_select_fusion.4), channel_id=1, source_target_pairs={{0,32},{8,40},{16,48},{24,56},{32,0},{40,8},{48,16},{56,24},{64,96... | collective-permute-start | bytes 49160 | tf_op jit(solution)/shard_map/ppermute | solution.py:135
  65.0 2.4 %constant_dynamic-slice_fusion.1 = (f32[2,2,1,16,8,256]{5,4,3,2,1,0:T(8,128)}, f32[2,2,1,16,8,256]{5,4,3,2,1,0:T(8,128)}) fusion(f32[2,2,2,16,8,256]{5,4,3,2,1,0:T(8,128)} %get-tuple-element.244, s32[]{:T(128)S(6)} %select_n.202, s32[]{:T(128)S(6)} %select_n.190), kind=kLoop, calls=%fused_computation.239 | loop fusion | bytes 2097160 | tf_op jit(solution)/shard_map/jit(dynamic_index_in_dim)/dynamic_slice | solution.py:185
  67.4 2.3 %collective-permute-done.5 = bf16[2,2,2,4,256]{4,3,2,1,0:T(4,128)(2,1)} collective-permute-done((bf16[2,2,2,4,256]{4,3,2,1,0:T(4,128)(2,1)}, bf16[2,2,2,4,256]{4,3,2,1,0:T(4,128)(2,1)}, u32[]{:S(2)}, u32[]{:S(2)}) %collective-permute-start.5) | collective-permute-done | bytes 16416 | tf_op jit(solution)/shard_map/ppermute | solution.py:135
  71.1 3.1 %collective-permute-start.6 = (bf16[4,2,2,4,256]{4,3,2,1,0:T(4,128)(2,1)}, bf16[4,2,2,4,256]{4,3,2,1,0:T(4,128)(2,1)}, u32[]{:S(2)}, u32[]{:S(2)}) collective-permute-start(bf16[4,2,2,4,256]{4,3,2,1,0:T(4,128)(2,1)} %maximum_select_fusion.3), channel_id=1, source_target_pairs={{0,16},{8,24},{16,0},{24,8},{32,48},{40,56},{48,32},{56,40},{64,80... | collective-permute-start | bytes 98312 | tf_op jit(solution)/shard_map/ppermute | solution.py:135
  77.9 2.6 %collective-permute-start.7 = (bf16[8,2,2,4,256]{4,3,2,1,0:T(4,128)(2,1)S(1)}, bf16[8,2,2,4,256]{4,3,2,1,0:T(4,128)(2,1)S(1)}, u32[]{:S(2)}, u32[]{:S(2)}) collective-permute-start(bf16[8,2,2,4,256]{4,3,2,1,0:T(4,128)(2,1)S(1)} %maximum_select_fusion.2), channel_id=1, source_target_pairs={{0,8},{8,0},{16,24},{24,16},{32,40},{40,32},{48,56},{56,48},{64,72... | collective-permute-start | bytes 196616 | tf_op jit(solution)/shard_map/ppermute | solution.py:135
  83.1 4.7 %collective-permute-start.8 = (bf16[16,2,2,4,256]{4,3,2,1,0:T(4,128)(2,1)S(1)}, bf16[16,2,2,4,256]{4,3,2,1,0:T(4,128)(2,1)S(1)}, u32[]{:S(2)}, u32[]{:S(2)}) collective-permute-start(bf16[16,2,2,4,256]{4,3,2,1,0:T(4,128)(2,1)S(1)} %maximum_select_fusion.1), channel_id=1, source_target_pairs={{0,256},{8,264},{16,272},{24,280},{32,288},{40,296},{48,304},{56,3... | collective-permute-start | bytes 393224 | tf_op jit(solution)/shard_map/ppermute | solution.py:135
  92.6 5.7 %collective-permute-start.9 = (bf16[32,2,2,4,256]{4,3,2,1,0:T(4,128)(2,1)S(1)}, bf16[32,2,2,4,256]{4,3,2,1,0:T(4,128)(2,1)S(1)}, u32[]{:S(2)}, u32[]{:S(2)}) collective-permute-start(bf16[32,2,2,4,256]{4,3,2,1,0:T(4,128)(2,1)S(1)} %bitcast.401), channel_id=1, source_target_pairs={{0,128},{8,136},{16,144},{24,152},{32,160},{40,168},{48,176},{56,1... | collective-permute-start | bytes 786440 | tf_op jit(solution)/shard_map/ppermute | solution.py:148
  99.3 2.8 %collective-permute-done.9 = bf16[32,2,2,4,256]{4,3,2,1,0:T(4,128)(2,1)S(1)} collective-permute-done((bf16[32,2,2,4,256]{4,3,2,1,0:T(4,128)(2,1)S(1)}, bf16[32,2,2,4,256]{4,3,2,1,0:T(4,128)(2,1)S(1)}, u32[]{:S(2)}, u32[]{:S(2)}) %collective-permute-start.9) | collective-permute-done | bytes 262176 | tf_op jit(solution)/shard_map/ppermute | solution.py:148
  103.1 7.9 %collective-permute-start.10 = (f32[2,2,2,2,4,256]{5,4,3,2,1,0:T(4,128)S(1)}, f32[2,2,2,2,4,256]{5,4,3,2,1,0:T(4,128)S(1)}, u32[]{:S(2)}, u32[]{:S(2)}) collective-permute-start(f32[2,2,2,2,4,256]{5,4,3,2,1,0:T(4,128)S(1)} %select_bitcast_fusion), channel_id=1, source_target_pairs={{0,1},{1,0},{2,3},{3,2},{4,5},{5,4},{6,7},{7,6},{8,9},{9,8},{10,11... | collective-permute-start | bytes 196616 | tf_op jit(solution)/shard_map/ppermute | solution.py:124
  111.9 3.2 %collective-permute-start.11 = (f32[2,2,2,4,256]{4,3,2,1,0:T(4,128)S(1)}, f32[2,2,2,4,256]{4,3,2,1,0:T(4,128)S(1)}, u32[]{:S(2)}, u32[]{:S(2)}) collective-permute-start(f32[2,2,2,4,256]{4,3,2,1,0:T(4,128)S(1)} %select_bitcast_fusion.1), channel_id=1, source_target_pairs={{0,2},{1,3},{2,0},{3,1},{4,6},{5,7},{6,4},{7,5},{8,10},{9,11},{10,... | collective-permute-start | bytes 98312 | tf_op jit(solution)/shard_map/ppermute | solution.py:124
  116.6 4.9 %collective-permute-start.12 = (f32[2,2,4,256]{3,2,1,0:T(4,128)S(1)}, f32[2,2,4,256]{3,2,1,0:T(4,128)S(1)}, u32[]{:S(2)}, u32[]{:S(2)}) collective-permute-start(f32[2,2,4,256]{3,2,1,0:T(4,128)S(1)} %select_bitcast_fusion.2), channel_id=1, source_target_pairs={{0,4},{1,5},{2,6},{3,7},{4,0},{5,1},{6,2},{7,3},{8,12},{9,13},{10,... | collective-permute-start | bytes 49160 | tf_op jit(solution)/shard_map/ppermute | solution.py:124
  121.7 4.0 %collective-permute-start.2 = (f32[800,128]{1,0:T(8,128)S(1)}, f32[800,128]{1,0:T(8,128)S(1)}, u32[]{:S(2)}, u32[]{:S(2)}) collective-permute-start(f32[800,128]{1,0:T(8,128)S(1)} %get-tuple-element.222), channel_id=1, source_target_pairs={{0,1},{1,2},{2,3},{3,4},{4,5},{5,6},{6,7},{8,9},{9,10},{10,11},{11... | collective-permute-start | bytes 1228808 | tf_op jit(solution)/shard_map/ppermute | solution.py:85
  125.7 1.9 %collective-permute-start.3 = (f32[800,128]{1,0:T(8,128)S(1)}, f32[800,128]{1,0:T(8,128)S(1)}, u32[]{:S(2)}, u32[]{:S(2)}) collective-permute-start(f32[800,128]{1,0:T(8,128)S(1)} %get-tuple-element.223), channel_id=1, source_target_pairs={{1,0},{2,1},{3,2},{4,3},{5,4},{6,5},{7,6},{9,8},{10,9},{11,10},{12... | collective-permute-start | bytes 1228808 | tf_op jit(solution)/shard_map/ppermute | solution.py:86
  127.8 2.8 %collective-permute-done.2 = f32[800,128]{1,0:T(8,128)S(1)} collective-permute-done((f32[800,128]{1,0:T(8,128)S(1)}, f32[800,128]{1,0:T(8,128)S(1)}, u32[]{:S(2)}, u32[]{:S(2)}) %collective-permute-start.2) | collective-permute-done | bytes 409632 | tf_op jit(solution)/shard_map/ppermute | solution.py:85
  130.7 4.3 %collective-permute-done.3 = f32[800,128]{1,0:T(8,128)S(1)} collective-permute-done((f32[800,128]{1,0:T(8,128)S(1)}, f32[800,128]{1,0:T(8,128)S(1)}, u32[]{:S(2)}, u32[]{:S(2)}) %collective-permute-start.3) | collective-permute-done | bytes 409632 | tf_op jit(solution)/shard_map/ppermute | solution.py:86
  140.3 3.5 %subtract_reduce_fusion = (f32[16,2,4,128]{3,2,1,0:T(4,128)S(1)}, f32[16,2,4,128]{3,2,1,0:T(4,128)S(1)}) fusion(f32[144,2,4,128]{3,0,2,1:T(8,128)S(1)} %copy.757, f32[16,144,2,128]{3,1,2,0:T(8,128)S(1)} %copy-done.3, f32[144,2,4,128]{3,0,2,1:T(8,128)S(1)} %copy.756, f32[16,144,2,128]{3,1,2,0:T(8,128)S(1)} %copy-done.2), kind=kLoop, calls=%fused_computation.1 | loop fusion | flops 18841600 | bytes 6029312 | tf_op jit(solution)/shard_map/reduce_sum | solution.py:221
  147.2 1.8 %stack.192 = bf16[9,2,4,4,4,128]{5,0,4,1,3,2:T(8,128)(2,1)S(1)} concatenate(bf16[1,2,4,4,4,128]{5,0,4,1,3,2:T(2,128)(2,1)S(1)} %copy.738, bf16[1,2,4,4,4,128]{5,0,4,1,3,2:T(2,128)(2,1)S(1)} %copy.739, bf16[1,2,4,4,4,128]{5,0,4,1,3,2:T(2,128)(2,1)S(1)} %copy.740, bf16[1,2,4,4,4,128]{5,0,4,1,3,2:T(2,128)(2,1)S(1)} %copy.741, bf16[1,2,4,4,4,128]{5,0,4,1,3,2:T(2,128)(2,1)S(1)} %copy.742, ...), dimensions={0} | concatenate | bytes 589824 | tf_op jit(solution)/shard_map/stack | solution.py:23
  (242 shorter events, 57.7 us)
Async XLA Ops:
  0.6 18.6 %copy-start = (f32[256,128]{1,0:T(8,128)S(1)}, f32[256,128]{1,0:T(8,128)}, u32[]{:S(2)}) copy-start(f32[256,128]{1,0:T(8,128)} %param.42) | copy-start | bytes 393220
  11.3 24.9 %copy-start.16 = (f32[2,15,15,128]{3,0,2,1:T(2,128)S(1)}, f32[2,15,15,128]{3,0,2,1:T(2,128)}, u32[]{:S(2)}) copy-start(f32[2,15,15,128]{3,0,2,1:T(2,128)} %param.44) | copy-start | bytes 691204
  12.9 74.9 %collective-permute-start = (f32[304,128]{1,0:T(8,128)}, f32[304,128]{1,0:T(8,128)}, u32[]{:S(2)}, u32[]{:S(2)}) collective-permute-start(f32[304,128]{1,0:T(8,128)} %pad_maximum_fusion.6), channel_id=1, source_target_pairs={{0,8},{8,16},{16,24},{24,32},{32,40},{40,48},{48,56},{56,64},{64,7... | collective-permute-start | bytes 466952 | tf_op jit(solution)/shard_map/ppermute | solution.py:85
  19.2 17.2 %copy-start.22 = (f32[4,4,256]{2,1,0:T(4,128)}, f32[4,4,256]{2,1,0:T(4,128)S(1)}, u32[]{:S(2)}) copy-start(f32[4,4,256]{2,1,0:T(4,128)S(1)} %cos.11) | copy-start | bytes 49156
  19.2 17.2 %copy-start.24 = (f32[4,4,256]{2,1,0:T(4,128)}, f32[4,4,256]{2,1,0:T(4,128)S(1)}, u32[]{:S(2)}) copy-start(f32[4,4,256]{2,1,0:T(4,128)S(1)} %sin.11) | copy-start | bytes 49156
  19.8 16.6 %copy-start.30 = (bf16[2,4,256]{2,1,0:T(4,128)(2,1)}, bf16[2,4,256]{2,1,0:T(4,128)(2,1)S(1)}, u32[]{:S(2)}) copy-start(bf16[2,4,256]{2,1,0:T(4,128)(2,1)S(1)} %get-tuple-element.186) | copy-start | bytes 12292
  19.9 16.6 %copy-start.31 = (bf16[2,4,256]{2,1,0:T(4,128)(2,1)}, bf16[2,4,256]{2,1,0:T(4,128)(2,1)S(1)}, u32[]{:S(2)}) copy-start(bf16[2,4,256]{2,1,0:T(4,128)(2,1)S(1)} %get-tuple-element.187) | copy-start | bytes 12292
  20.5 39.1 %collective-permute-start.4 = (bf16[1,2,2,4,256]{4,3,2,1,0:T(4,128)(2,1)}, bf16[1,2,2,4,256]{4,3,2,1,0:T(4,128)(2,1)}, u32[]{:S(2)}, u32[]{:S(2)}) collective-permute-start(bf16[1,2,2,4,256]{4,3,2,1,0:T(4,128)(2,1)} %pad_maximum_fusion.13), channel_id=1, source_target_pairs={{0,64},{8,72},{16,80},{24,88},{32,96},{40,104},{48,112},{56,120},{... | collective-permute-start | bytes 24584 | tf_op jit(solution)/shard_map/ppermute | solution.py:135
  59.0 15.3 %copy-start.4 = (f32[2,2,2,16,8,256]{5,4,3,2,1,0:T(8,128)S(1)}, f32[2,2,2,16,8,256]{5,4,3,2,1,0:T(8,128)}, u32[]{:S(2)}) copy-start(f32[2,2,2,16,8,256]{5,4,3,2,1,0:T(8,128)} %get-tuple-element.245) | copy-start | bytes 3145732
  61.0 8.7 %collective-permute-start.5 = (bf16[2,2,2,4,256]{4,3,2,1,0:T(4,128)(2,1)}, bf16[2,2,2,4,256]{4,3,2,1,0:T(4,128)(2,1)}, u32[]{:S(2)}, u32[]{:S(2)}) collective-permute-start(bf16[2,2,2,4,256]{4,3,2,1,0:T(4,128)(2,1)} %maximum_select_fusion.4), channel_id=1, source_target_pairs={{0,32},{8,40},{16,48},{24,56},{32,0},{40,8},{48,16},{56,24},{64,96... | collective-permute-start | bytes 49160 | tf_op jit(solution)/shard_map/ppermute | solution.py:135
  71.1 5.9 %collective-permute-start.6 = (bf16[4,2,2,4,256]{4,3,2,1,0:T(4,128)(2,1)}, bf16[4,2,2,4,256]{4,3,2,1,0:T(4,128)(2,1)}, u32[]{:S(2)}, u32[]{:S(2)}) collective-permute-start(bf16[4,2,2,4,256]{4,3,2,1,0:T(4,128)(2,1)} %maximum_select_fusion.3), channel_id=1, source_target_pairs={{0,16},{8,24},{16,0},{24,8},{32,48},{40,56},{48,32},{56,40},{64,80... | collective-permute-start | bytes 98312 | tf_op jit(solution)/shard_map/ppermute | solution.py:135
  77.9 5.0 %collective-permute-start.7 = (bf16[8,2,2,4,256]{4,3,2,1,0:T(4,128)(2,1)S(1)}, bf16[8,2,2,4,256]{4,3,2,1,0:T(4,128)(2,1)S(1)}, u32[]{:S(2)}, u32[]{:S(2)}) collective-permute-start(bf16[8,2,2,4,256]{4,3,2,1,0:T(4,128)(2,1)S(1)} %maximum_select_fusion.2), channel_id=1, source_target_pairs={{0,8},{8,0},{16,24},{24,16},{32,40},{40,32},{48,56},{56,48},{64,72... | collective-permute-start | bytes 196616 | tf_op jit(solution)/shard_map/ppermute | solution.py:135
  81.4 17.0 %copy-start.7 = (f32[2,2,1,16,8,256]{5,4,3,2,1,0:T(8,128)S(1)}, f32[2,2,1,16,8,256]{5,4,3,2,1,0:T(8,128)}, u32[]{:S(2)}) copy-start(f32[2,2,1,16,8,256]{5,4,3,2,1,0:T(8,128)} %get-tuple-element.206) | copy-start | bytes 1572868
  81.4 17.0 %copy-start.8 = (f32[2,2,1,16,8,256]{5,4,3,2,1,0:T(8,128)S(1)}, f32[2,2,1,16,8,256]{5,4,3,2,1,0:T(8,128)}, u32[]{:S(2)}) copy-start(f32[2,2,1,16,8,256]{5,4,3,2,1,0:T(8,128)} %get-tuple-element.208) | copy-start | bytes 1572868
  83.1 8.9 %collective-permute-start.8 = (bf16[16,2,2,4,256]{4,3,2,1,0:T(4,128)(2,1)S(1)}, bf16[16,2,2,4,256]{4,3,2,1,0:T(4,128)(2,1)S(1)}, u32[]{:S(2)}, u32[]{:S(2)}) collective-permute-start(bf16[16,2,2,4,256]{4,3,2,1,0:T(4,128)(2,1)S(1)} %maximum_select_fusion.1), channel_id=1, source_target_pairs={{0,256},{8,264},{16,272},{24,280},{32,288},{40,296},{48,304},{56,3... | collective-permute-start | bytes 393224 | tf_op jit(solution)/shard_map/ppermute | solution.py:135
  89.5 9.6 %collective-permute-start.1 = (f32[304,128]{1,0:T(8,128)S(1)}, f32[304,128]{1,0:T(8,128)S(1)}, u32[]{:S(2)}, u32[]{:S(2)}) collective-permute-start(f32[304,128]{1,0:T(8,128)S(1)} %pad_maximum_fusion.5), channel_id=1, source_target_pairs={{8,0},{16,8},{24,16},{32,24},{40,32},{48,40},{56,48},{64,56},{72,6... | collective-permute-start | bytes 466952 | tf_op jit(solution)/shard_map/ppermute | solution.py:86
  92.6 9.5 %collective-permute-start.9 = (bf16[32,2,2,4,256]{4,3,2,1,0:T(4,128)(2,1)S(1)}, bf16[32,2,2,4,256]{4,3,2,1,0:T(4,128)(2,1)S(1)}, u32[]{:S(2)}, u32[]{:S(2)}) collective-permute-start(bf16[32,2,2,4,256]{4,3,2,1,0:T(4,128)(2,1)S(1)} %bitcast.401), channel_id=1, source_target_pairs={{0,128},{8,136},{16,144},{24,152},{32,160},{40,168},{48,176},{56,1... | collective-permute-start | bytes 786440 | tf_op jit(solution)/shard_map/ppermute | solution.py:148
  103.1 24.6 %copy-start.23 = (f32[4,4,256]{2,1,0:T(4,128)S(1)}, f32[4,4,256]{2,1,0:T(4,128)}, u32[]{:S(2)}) copy-start(f32[4,4,256]{2,1,0:T(4,128)} %copy-done.22) | copy-start | bytes 49156
  103.1 24.6 %copy-start.25 = (f32[4,4,256]{2,1,0:T(4,128)S(1)}, f32[4,4,256]{2,1,0:T(4,128)}, u32[]{:S(2)}) copy-start(f32[4,4,256]{2,1,0:T(4,128)} %copy-done.24) | copy-start | bytes 49156
  103.1 8.7 %collective-permute-start.10 = (f32[2,2,2,2,4,256]{5,4,3,2,1,0:T(4,128)S(1)}, f32[2,2,2,2,4,256]{5,4,3,2,1,0:T(4,128)S(1)}, u32[]{:S(2)}, u32[]{:S(2)}) collective-permute-start(f32[2,2,2,2,4,256]{5,4,3,2,1,0:T(4,128)S(1)} %select_bitcast_fusion), channel_id=1, source_target_pairs={{0,1},{1,0},{2,3},{3,2},{4,5},{5,4},{6,7},{7,6},{8,9},{9,8},{10,11... | collective-permute-start | bytes 196616 | tf_op jit(solution)/shard_map/ppermute | solution.py:124
  111.9 4.7 %collective-permute-start.11 = (f32[2,2,2,4,256]{4,3,2,1,0:T(4,128)S(1)}, f32[2,2,2,4,256]{4,3,2,1,0:T(4,128)S(1)}, u32[]{:S(2)}, u32[]{:S(2)}) collective-permute-start(f32[2,2,2,4,256]{4,3,2,1,0:T(4,128)S(1)} %select_bitcast_fusion.1), channel_id=1, source_target_pairs={{0,2},{1,3},{2,0},{3,1},{4,6},{5,7},{6,4},{7,5},{8,10},{9,11},{10,... | collective-permute-start | bytes 98312 | tf_op jit(solution)/shard_map/ppermute | solution.py:124
  116.6 11.0 %collective-permute-start.12 = (f32[2,2,4,256]{3,2,1,0:T(4,128)S(1)}, f32[2,2,4,256]{3,2,1,0:T(4,128)S(1)}, u32[]{:S(2)}, u32[]{:S(2)}) collective-permute-start(f32[2,2,4,256]{3,2,1,0:T(4,128)S(1)} %select_bitcast_fusion.2), channel_id=1, source_target_pairs={{0,4},{1,5},{2,6},{3,7},{4,0},{5,1},{6,2},{7,3},{8,12},{9,13},{10,... | collective-permute-start | bytes 49160 | tf_op jit(solution)/shard_map/ppermute | solution.py:124
  121.7 8.9 %collective-permute-start.2 = (f32[800,128]{1,0:T(8,128)S(1)}, f32[800,128]{1,0:T(8,128)S(1)}, u32[]{:S(2)}, u32[]{:S(2)}) collective-permute-start(f32[800,128]{1,0:T(8,128)S(1)} %get-tuple-element.222), channel_id=1, source_target_pairs={{0,1},{1,2},{2,3},{3,4},{4,5},{5,6},{6,7},{8,9},{9,10},{10,11},{11... | collective-permute-start | bytes 1228808 | tf_op jit(solution)/shard_map/ppermute | solution.py:85
  125.7 9.3 %collective-permute-start.3 = (f32[800,128]{1,0:T(8,128)S(1)}, f32[800,128]{1,0:T(8,128)S(1)}, u32[]{:S(2)}, u32[]{:S(2)}) collective-permute-start(f32[800,128]{1,0:T(8,128)S(1)} %get-tuple-element.223), channel_id=1, source_target_pairs={{1,0},{2,1},{3,2},{4,3},{5,4},{6,5},{7,6},{9,8},{10,9},{11,10},{12... | collective-permute-start | bytes 1228808 | tf_op jit(solution)/shard_map/ppermute | solution.py:86
  (28 other events, 115.5 us)

commit v8 on v6

--- a/solution.py
+++ b/solution.py
@@ -4,33 +4,6 @@
 from jax.sharding import PartitionSpec as P
 
 HIGH = lax.Precision.HIGHEST
-
-
-def with_halo(cells, sides, width):
-    for axis, dim in sides:
-        count = lax.axis_size(axis)
-        ends = count - 1
-        head = lax.slice_in_dim(cells, 0, width, axis=dim)
-        tail = lax.slice_in_dim(cells, cells.shape[dim] - width, cells.shape[dim], axis=dim)
-        cells = jnp.concatenate(
-            [
-                lax.ppermute(tail, axis, [(i, (i + 1) % count) for i in range(ends)]),
-                cells,
-                lax.ppermute(head, axis, [((i + 1) % count, i) for i in range(ends)]),
-            ],
-            axis=dim,
-        )
-    return cells
-
-
-def from_behind(block, axis, distance):
-    devices = range(lax.axis_size(axis))
-    route = [(i - distance, i) for i in devices if i - distance in devices]
-    return lax.ppermute(block, axis, route)
-
-
-def complex_mul(left_re, left_im, right_re, right_im):
-    return (left_re * right_re - left_im * right_im, left_re * right_im + left_im * right_re)
 
 
 def conj_flip(table, axes):
@@ -109,12 +82,8 @@
             to_next = placed[:, 1 : box_side + 1, box_side + 1]
             to_prev = placed[:, 1 : box_side + 1, 0]
         edge_shape = to_next.shape
-        from_prev = lax.ppermute(
-            jnp.concatenate([flat, to_next.reshape(-1, lanes)]), axis, ahead
-        )
-        from_next = lax.ppermute(
-            jnp.concatenate([flat, to_prev.reshape(-1, lanes)]), axis, behind
-        )
+        from_prev = lax.ppermute(jnp.concatenate([flat, to_next.reshape(-1, lanes)]), axis, ahead)
+        from_next = lax.ppermute(jnp.concatenate([flat, to_prev.reshape(-1, lanes)]), axis, behind)
         if axis == "row":
             placed = placed.at[:, 1].add(from_prev[size:].reshape(edge_shape))
             placed = placed.at[:, box_side].add(from_next[size:].reshape(edge_shape))
@@ -163,7 +132,7 @@
     bits = count.bit_length() - 1
     held = parts.reshape((2,) * bits + parts.shape[1:])
     remaining = list(range(bits - 1, -1, -1))
-    for exp in range(bits):
+    for exp in range(bits - 1, -1, -1):
         step = 1 << exp
         at = remaining.index(exp)
         upper = (index & step) != 0
@@ -251,8 +220,6 @@
 
 def far_field(own, vectors, rad_tab, rcv_tab, leaf_tab, coarse_tab, interp, phase):
     box_side = own.shape[2]
-    span = 3 * box_side
-    reach = 2 * box_side - 1
     leaf_out = radiate(own, rad_tab)
     window = radiate(vectors, rad_tab)
     leaf_in = leaf_incoming(window, leaf_tab, box_side)
@@ -281,7 +248,7 @@
     return jnp.stack([res_re, res_im], 1)
 
 
-def per_device(
+def per_device_body(
     current,
     probe,
     near_list,
@@ -334,7 +301,7 @@
         P(),
     )
     return jax.shard_map(
-        per_device,
+        per_device_body,
         mesh=mesh,
         in_specs=placed,
         out_specs=(P(None, "row", "col", None, None), P(None, "row", "col", None, None)),

time: 158 us -> 160 us (1.013)
    ppermute x3, starting transfers between devices: 16 us -> 18.2 us  [scatter_sum(): lax.ppermute(send, axis, [(i, i ^ step) for i in range(count)])]
  transfers between devices with their start and end apart: 13 -> 13, of which waited for: 6 -> 6; matrix products, arithmetic and copies ran while one was open for 29% -> 28% of each run, Pallas kernels for 0% -> 0%
where the time goes in v8:
time: 160 us; the launch traced here: 159 us
  starting transfers between devices  63.6 us (40%)
  local copies, waits for them, and re-layouts  33.5 us (21%)
  other arithmetic  32 us (20%)
  waiting for transfers between devices  14.2 us (9%)
  matrix products  13.5 us (8%)
  between operations  1.95 us (1%)
    ppermute x6, starting transfers between devices, gather_ordered(): other = lax.ppermute(held, axis, [(i, i ^ step) for i in range(count)])  34 us
    ppermute x3, starting transfers between devices, scatter_sum(): lax.ppermute(send, axis, [(i, i ^ step) for i in range(count)])  18.2 us
    dot_general x21, matrix products, product(): return jnp.einsum(form, left, right, preferred_element_type=jnp.float32)  9.68 us
    unnamed x81, local copies, waits for them, and re-layouts  9.51 us
    ppermute x2, starting transfers between devices, exchange_halo(): lax.ppermute(jnp.concatenate([flat, to_next.reshape(-1, lanes)]), axis, a...  8.27 us
    select_n x6, other arithmetic, gather_ordered(): jnp.where(lower, jnp.concatenate([held, other], 0), jnp.concatenate([othe...  8.11 us
    slice x2, local copies, waits for them, and re-layouts, coarse_exchange(): adj = jnp.stack([adj[0], -adj[1]])  4.44 us
    ppermute x2, waiting for transfers between devices, exchange_halo(): lax.ppermute(jnp.concatenate([flat, to_prev.reshape(-1, lanes)]), axis, b...  4.27 us
  transfers between devices with their start and end apart: 13, of which 6 were waited for; matrix products, arithmetic and copies ran while one was open for 28% of the time, Pallas kernels for 0%

profile of v8, /device:TPU:1, one launch (start us, length us, event | category | flops | bytes accessed | tf_op | source)
XLA Modules:
  0.0 158.8 jit_solution(2302085613864093837)
XLA Ops:
  9.2 1.9 %fusion.50 = f32[2,6,6,4,128]{4,3,0,2,1:T(4,128)S(1)} fusion(f32[2,6,6,4,128]{4,3,0,2,1:T(4,128)S(1)} %add_dynamic-update-slice_fusion, s32[]{:T(128)} %bitcast.24, s32[]{:T(128)} %bitcast.25, f32[2,4,4,4,128]{4,3,0,2,1:T(4,128)S(1)} %bitcast.370, pred[]{:T(512)} %and_reduce_fusion), kind=kLoop, calls=%fused_computation.122 | loop fusion | flops 32768 | bytes 196617 | tf_op jit(solution)/shard_map/scatter-add | solution.py:64
  12.8 5.0 %collective-permute-start = (f32[304,128]{1,0:T(8,128)}, f32[304,128]{1,0:T(8,128)}, u32[]{:S(2)}, u32[]{:S(2)}) collective-permute-start(f32[304,128]{1,0:T(8,128)} %pad_maximum_fusion.6), channel_id=1, source_target_pairs={{0,8},{8,16},{16,24},{24,32},{32,40},{40,48},{48,56},{56,64},{64,7... | collective-permute-start | bytes 466952 | tf_op jit(solution)/shard_map/ppermute | solution.py:85
  20.9 14.1 %collective-permute-start.4 = (bf16[1,2,2,4,256]{4,3,2,1,0:T(4,128)(2,1)}, bf16[1,2,2,4,256]{4,3,2,1,0:T(4,128)(2,1)}, u32[]{:S(2)}, u32[]{:S(2)}) collective-permute-start(bf16[1,2,2,4,256]{4,3,2,1,0:T(4,128)(2,1)} %pad_maximum_fusion.13), channel_id=1, source_target_pairs={{0,64},{8,72},{16,80},{24,88},{32,96},{40,104},{48,112},{56,120},{... | collective-permute-start | bytes 24584 | tf_op jit(solution)/shard_map/ppermute | solution.py:116
  36.8 2.1 %fusion.1 = f32[16,144,2,2,128]{4,1,3,2,0:T(8,128)S(1)} fusion(s32[16,144]{1,0:T(8,128)S(1)} %fusion.92, f32[1,2,225,128]{3,2,1,0:T(8,128)S(1)} %copy.747, f32[1,2,225,128]{3,2,1,0:T(8,128)S(1)} %copy.746), kind=kOutput, calls=%fused_computation.8 | convolution fusion | flops 3185683200 | bytes 5188608 | tf_op jit(solution)/shard_map/tnp,sxpq->tnsxq/dot_general | solution.py:199
  38.9 2.8 %slice_bitcast_fusion.1 = (f32[16,144,2,128]{3,1,2,0:T(8,128)}, f32[16,144,2,128]{3,1,2,0:T(8,128)}) fusion(f32[16,144,2,2,128]{4,1,3,2,0:T(8,128)S(1)} %fusion.1), kind=kLoop, calls=%fused_computation.5 | loop fusion | bytes 9437184 | tf_op jit(solution)/shard_map/mul | solution.py:205
  41.7 2.9 %constant_dynamic-slice_fusion.2 = (bf16[1,64,8,256]{3,0,2,1:T(2,128)(2,1)}, bf16[1,64,8,256]{3,0,2,1:T(2,128)(2,1)S(1)}) fusion(bf16[2,127,15,256]{3,0,2,1:T(2,128)(2,1)} %param.45, s32[]{:T(128)S(6)} %select_n.173, s32[]{:T(128)S(6)} %select_n.174, s32[]{:T(128)S(6)} %add.270), kind=kLoop, calls=%fused_computation.232 | loop fusion | bytes 1048588 | tf_op jit(solution)/shard_map/slice | solution.py:168
  51.0 3.0 %fusion.121 = (f32[2,1,64,8,256]{4,1,3,2,0:T(1,128)}, f32[2,1,64,8,256]{4,1,3,2,0:T(1,128)}) fusion(f32[2,2,64,8,256]{4,1,3,2,0:T(2,128)S(1)} %maximum_convert_fusion), kind=kLoop, calls=%fused_computation.259 | loop fusion | bytes 4194304 | tf_op jit(solution)/shard_map/slice | solution.py:174
  56.2 4.0 %collective-permute-start.5 = (bf16[2,2,2,4,256]{4,3,2,1,0:T(4,128)(2,1)}, bf16[2,2,2,4,256]{4,3,2,1,0:T(4,128)(2,1)}, u32[]{:S(2)}, u32[]{:S(2)}) collective-permute-start(bf16[2,2,2,4,256]{4,3,2,1,0:T(4,128)(2,1)} %maximum_select_fusion.5), channel_id=1, source_target_pairs={{0,32},{8,40},{16,48},{24,56},{32,0},{40,8},{48,16},{56,24},{64,96... | collective-permute-start | bytes 49160 | tf_op jit(solution)/shard_map/ppermute | solution.py:116
  60.2 2.8 %fusion.18 = (f32[2,64,8,256]{3,2,1,0:T(8,128)S(1)}, f32[2,64,8,256]{3,2,1,0:T(8,128)}) fusion(f32[2,1,64,8,256]{4,1,3,2,0:T(1,128)} %get-tuple-element.190, f32[64,8]{1,0:T(8,128)} %copy.756, f32[2,1,64,8,256]{4,1,3,2,0:T(1,128)} %get-tuple-element.191), kind=kLoop, calls=%fused_computation.42 | loop fusion | flops 524288 | bytes 4196352 | tf_op jit(solution)/shard_map/mul | solution.py:174
  63.0 1.9 %collective-permute-done.5 = bf16[2,2,2,4,256]{4,3,2,1,0:T(4,128)(2,1)} collective-permute-done((bf16[2,2,2,4,256]{4,3,2,1,0:T(4,128)(2,1)}, bf16[2,2,2,4,256]{4,3,2,1,0:T(4,128)(2,1)}, u32[]{:S(2)}, u32[]{:S(2)}) %collective-permute-start.5) | collective-permute-done | bytes 16416 | tf_op jit(solution)/shard_map/ppermute | solution.py:116
  66.3 3.1 %collective-permute-start.6 = (bf16[4,2,2,4,256]{4,3,2,1,0:T(4,128)(2,1)}, bf16[4,2,2,4,256]{4,3,2,1,0:T(4,128)(2,1)}, u32[]{:S(2)}, u32[]{:S(2)}) collective-permute-start(bf16[4,2,2,4,256]{4,3,2,1,0:T(4,128)(2,1)} %maximum_select_fusion.4), channel_id=1, source_target_pairs={{0,16},{8,24},{16,0},{24,8},{32,48},{40,56},{48,32},{56,40},{64,80... | collective-permute-start | bytes 98312 | tf_op jit(solution)/shard_map/ppermute | solution.py:116
  73.9 2.7 %collective-permute-start.7 = (bf16[8,2,2,4,256]{4,3,2,1,0:T(4,128)(2,1)}, bf16[8,2,2,4,256]{4,3,2,1,0:T(4,128)(2,1)}, u32[]{:S(2)}, u32[]{:S(2)}) collective-permute-start(bf16[8,2,2,4,256]{4,3,2,1,0:T(4,128)(2,1)} %maximum_select_fusion.3), channel_id=1, source_target_pairs={{0,8},{8,0},{16,24},{24,16},{32,40},{40,32},{48,56},{56,48},{64,72... | collective-permute-start | bytes 196616 | tf_op jit(solution)/shard_map/ppermute | solution.py:116
  81.1 4.8 %collective-permute-start.8 = (bf16[16,2,2,4,256]{4,3,2,1,0:T(4,128)(2,1)}, bf16[16,2,2,4,256]{4,3,2,1,0:T(4,128)(2,1)}, u32[]{:S(2)}, u32[]{:S(2)}) collective-permute-start(bf16[16,2,2,4,256]{4,3,2,1,0:T(4,128)(2,1)} %maximum_select_fusion.2), channel_id=1, source_target_pairs={{0,256},{8,264},{16,272},{24,280},{32,288},{40,296},{48,304},{56,3... | collective-permute-start | bytes 393224 | tf_op jit(solution)/shard_map/ppermute | solution.py:116
  93.3 5.4 %collective-permute-start.9 = (bf16[32,2,2,4,256]{4,3,2,1,0:T(4,128)(2,1)S(1)}, bf16[32,2,2,4,256]{4,3,2,1,0:T(4,128)(2,1)S(1)}, u32[]{:S(2)}, u32[]{:S(2)}) collective-permute-start(bf16[32,2,2,4,256]{4,3,2,1,0:T(4,128)(2,1)S(1)} %maximum_select_fusion.1), channel_id=1, source_target_pairs={{0,128},{8,136},{16,144},{24,152},{32,160},{40,168},{48,176},{56,1... | collective-permute-start | bytes 786440 | tf_op jit(solution)/shard_map/ppermute | solution.py:116
  100.5 2.2 %collective-permute-done.9 = bf16[32,2,2,4,256]{4,3,2,1,0:T(4,128)(2,1)S(1)} collective-permute-done((bf16[32,2,2,4,256]{4,3,2,1,0:T(4,128)(2,1)S(1)}, bf16[32,2,2,4,256]{4,3,2,1,0:T(4,128)(2,1)S(1)}, u32[]{:S(2)}, u32[]{:S(2)}) %collective-permute-start.9) | collective-permute-done | bytes 262176 | tf_op jit(solution)/shard_map/ppermute | solution.py:116
  106.2 4.8 %collective-permute-start.10 = (f32[2,2,2,2,4,256]{5,4,2,3,1,0:T(4,128)S(1)}, f32[2,2,2,2,4,256]{5,4,2,3,1,0:T(4,128)S(1)}, u32[]{:S(2)}, u32[]{:S(2)}) collective-permute-start(f32[2,2,2,2,4,256]{5,4,2,3,1,0:T(4,128)S(1)} %bitcast.387), channel_id=1, source_target_pairs={{0,4},{1,5},{2,6},{3,7},{4,0},{5,1},{6,2},{7,3},{8,12},{9,13},{10,... | collective-permute-start | bytes 196616 | tf_op jit(solution)/shard_map/ppermute | solution.py:143
  112.9 3.2 %collective-permute-start.11 = (f32[2,2,2,4,256]{4,3,1,2,0:T(4,128)S(1)}, f32[2,2,2,4,256]{4,3,1,2,0:T(4,128)S(1)}, u32[]{:S(2)}, u32[]{:S(2)}) collective-permute-start(f32[2,2,2,4,256]{4,3,1,2,0:T(4,128)S(1)} %select_bitcast_fusion), channel_id=1, source_target_pairs={{0,2},{1,3},{2,0},{3,1},{4,6},{5,7},{6,4},{7,5},{8,10},{9,11},{10,... | collective-permute-start | bytes 98312 | tf_op jit(solution)/shard_map/ppermute | solution.py:143
  117.6 10.1 %collective-permute-start.12 = (f32[2,2,4,256]{3,2,0,1:T(4,128)S(1)}, f32[2,2,4,256]{3,2,0,1:T(4,128)S(1)}, u32[]{:S(2)}, u32[]{:S(2)}) collective-permute-start(f32[2,2,4,256]{3,2,0,1:T(4,128)S(1)} %select_bitcast_fusion.1), channel_id=1, source_target_pairs={{0,1},{1,0},{2,3},{3,2},{4,5},{5,4},{6,7},{7,6},{8,9},{9,8},{10,11... | collective-permute-start | bytes 49160 | tf_op jit(solution)/shard_map/ppermute | solution.py:143
  127.9 3.2 %collective-permute-start.2 = (f32[800,128]{1,0:T(8,128)S(1)}, f32[800,128]{1,0:T(8,128)S(1)}, u32[]{:S(2)}, u32[]{:S(2)}) collective-permute-start(f32[800,128]{1,0:T(8,128)S(1)} %get-tuple-element.216), channel_id=1, source_target_pairs={{0,1},{1,2},{2,3},{3,4},{4,5},{5,6},{6,7},{8,9},{9,10},{10,11},{11... | collective-permute-start | bytes 1228808 | tf_op jit(solution)/shard_map/ppermute | solution.py:85
  131.2 1.9 %collective-permute-start.3 = (f32[800,128]{1,0:T(8,128)S(1)}, f32[800,128]{1,0:T(8,128)S(1)}, u32[]{:S(2)}, u32[]{:S(2)}) collective-permute-start(f32[800,128]{1,0:T(8,128)S(1)} %get-tuple-element.217), channel_id=1, source_target_pairs={{1,0},{2,1},{3,2},{4,3},{5,4},{6,5},{7,6},{9,8},{10,9},{11,10},{12... | collective-permute-start | bytes 1228808 | tf_op jit(solution)/shard_map/ppermute | solution.py:86
  133.2 2.8 %collective-permute-done.2 = f32[800,128]{1,0:T(8,128)S(1)} collective-permute-done((f32[800,128]{1,0:T(8,128)S(1)}, f32[800,128]{1,0:T(8,128)S(1)}, u32[]{:S(2)}, u32[]{:S(2)}) %collective-permute-start.2) | collective-permute-done | bytes 409632 | tf_op jit(solution)/shard_map/ppermute | solution.py:85
  136.2 4.3 %collective-permute-done.3 = f32[800,128]{1,0:T(8,128)S(1)} collective-permute-done((f32[800,128]{1,0:T(8,128)S(1)}, f32[800,128]{1,0:T(8,128)S(1)}, u32[]{:S(2)}, u32[]{:S(2)}) %collective-permute-start.3) | collective-permute-done | bytes 409632 | tf_op jit(solution)/shard_map/ppermute | solution.py:86
  145.8 3.5 %subtract_reduce_fusion = (f32[16,2,4,128]{3,2,1,0:T(4,128)S(1)}, f32[16,2,4,128]{3,2,1,0:T(4,128)S(1)}) fusion(f32[144,2,4,128]{3,0,2,1:T(8,128)S(1)} %copy.752, f32[16,144,2,128]{3,1,2,0:T(8,128)S(1)} %copy-done.3, f32[144,2,4,128]{3,0,2,1:T(8,128)S(1)} %copy.751, f32[16,144,2,128]{3,1,2,0:T(8,128)S(1)} %copy-done.2), kind=kLoop, calls=%fused_computation.1 | loop fusion | flops 18841600 | bytes 6029312 | tf_op jit(solution)/shard_map/reduce_sum | solution.py:205
  152.7 1.8 %stack.196 = bf16[9,2,4,4,4,128]{5,0,4,1,3,2:T(8,128)(2,1)S(1)} concatenate(bf16[1,2,4,4,4,128]{5,0,4,1,3,2:T(2,128)(2,1)S(1)} %copy.733, bf16[1,2,4,4,4,128]{5,0,4,1,3,2:T(2,128)(2,1)S(1)} %copy.734, bf16[1,2,4,4,4,128]{5,0,4,1,3,2:T(2,128)(2,1)S(1)} %copy.735, bf16[1,2,4,4,4,128]{5,0,4,1,3,2:T(2,128)(2,1)S(1)} %copy.736, bf16[1,2,4,4,4,128]{5,0,4,1,3,2:T(2,128)(2,1)S(1)} %copy.737, ...), dimensions={0} | concatenate | bytes 589824 | tf_op jit(solution)/shard_map/stack | solution.py:23
  (236 shorter events, 62.7 us)
Async XLA Ops:
  0.6 18.5 %copy-start = (f32[256,128]{1,0:T(8,128)S(1)}, f32[256,128]{1,0:T(8,128)}, u32[]{:S(2)}) copy-start(f32[256,128]{1,0:T(8,128)} %param.42) | copy-start | bytes 393220
  4.5 6.8 %copy-start.31 = (bf16[2,4,4,4,128]{4,3,2,1,0:T(4,128)(2,1)S(1)}, bf16[2,4,4,4,128]{4,3,2,1,0:T(4,128)(2,1)}, u32[]{:S(2)}) copy-start(bf16[2,4,4,4,128]{4,3,2,1,0:T(4,128)(2,1)} %param.36) | copy-start | bytes 98308
  5.3 12.5 %copy-start.10 = (bf16[2,128,128]{2,1,0:T(8,128)(2,1)S(1)}, bf16[2,128,128]{2,1,0:T(8,128)(2,1)}, u32[]{:S(2)}) copy-start(bf16[2,128,128]{2,1,0:T(8,128)(2,1)} %param.41) | copy-start | bytes 196612
  5.3 12.8 %copy-start.16 = (bf16[2,128,128]{2,1,0:T(8,128)(2,1)S(1)}, bf16[2,128,128]{2,1,0:T(8,128)(2,1)}, u32[]{:S(2)}) copy-start(bf16[2,128,128]{2,1,0:T(8,128)(2,1)} %param.40) | copy-start | bytes 196612
  7.9 11.1 %copy-start.32 = (f32[16,256]{1,0:T(8,128)S(1)}, f32[16,256]{1,0:T(8,128)}, u32[]{:S(2)}) copy-start(f32[16,256]{1,0:T(8,128)} %param.43) | copy-start | bytes 49156
  11.2 24.9 %copy-start.13 = (f32[2,15,15,128]{3,0,2,1:T(2,128)S(1)}, f32[2,15,15,128]{3,0,2,1:T(2,128)}, u32[]{:S(2)}) copy-start(f32[2,15,15,128]{3,0,2,1:T(2,128)} %param.44) | copy-start | bytes 691204
  12.8 73.1 %collective-permute-start = (f32[304,128]{1,0:T(8,128)}, f32[304,128]{1,0:T(8,128)}, u32[]{:S(2)}, u32[]{:S(2)}) collective-permute-start(f32[304,128]{1,0:T(8,128)} %pad_maximum_fusion.6), channel_id=1, source_target_pairs={{0,8},{8,16},{16,24},{24,32},{32,40},{40,48},{48,56},{56,64},{64,7... | collective-permute-start | bytes 466952 | tf_op jit(solution)/shard_map/ppermute | solution.py:85
  19.1 17.2 %copy-start.19 = (f32[4,4,256]{2,1,0:T(4,128)}, f32[4,4,256]{2,1,0:T(4,128)S(1)}, u32[]{:S(2)}) copy-start(f32[4,4,256]{2,1,0:T(4,128)S(1)} %cos.11) | copy-start | bytes 49156
  19.1 17.2 %copy-start.21 = (f32[4,4,256]{2,1,0:T(4,128)}, f32[4,4,256]{2,1,0:T(4,128)S(1)}, u32[]{:S(2)}) copy-start(f32[4,4,256]{2,1,0:T(4,128)S(1)} %sin.11) | copy-start | bytes 49156
  20.9 33.9 %collective-permute-start.4 = (bf16[1,2,2,4,256]{4,3,2,1,0:T(4,128)(2,1)}, bf16[1,2,2,4,256]{4,3,2,1,0:T(4,128)(2,1)}, u32[]{:S(2)}, u32[]{:S(2)}) collective-permute-start(bf16[1,2,2,4,256]{4,3,2,1,0:T(4,128)(2,1)} %pad_maximum_fusion.13), channel_id=1, source_target_pairs={{0,64},{8,72},{16,80},{24,88},{32,96},{40,104},{48,112},{56,120},{... | collective-permute-start | bytes 24584 | tf_op jit(solution)/shard_map/ppermute | solution.py:116
  56.2 8.7 %collective-permute-start.5 = (bf16[2,2,2,4,256]{4,3,2,1,0:T(4,128)(2,1)}, bf16[2,2,2,4,256]{4,3,2,1,0:T(4,128)(2,1)}, u32[]{:S(2)}, u32[]{:S(2)}) collective-permute-start(bf16[2,2,2,4,256]{4,3,2,1,0:T(4,128)(2,1)} %maximum_select_fusion.5), channel_id=1, source_target_pairs={{0,32},{8,40},{16,48},{24,56},{32,0},{40,8},{48,16},{56,24},{64,96... | collective-permute-start | bytes 49160 | tf_op jit(solution)/shard_map/ppermute | solution.py:116
  66.3 6.0 %collective-permute-start.6 = (bf16[4,2,2,4,256]{4,3,2,1,0:T(4,128)(2,1)}, bf16[4,2,2,4,256]{4,3,2,1,0:T(4,128)(2,1)}, u32[]{:S(2)}, u32[]{:S(2)}) collective-permute-start(bf16[4,2,2,4,256]{4,3,2,1,0:T(4,128)(2,1)} %maximum_select_fusion.4), channel_id=1, source_target_pairs={{0,16},{8,24},{16,0},{24,8},{32,48},{40,56},{48,32},{56,40},{64,80... | collective-permute-start | bytes 98312 | tf_op jit(solution)/shard_map/ppermute | solution.py:116
  73.9 5.5 %collective-permute-start.7 = (bf16[8,2,2,4,256]{4,3,2,1,0:T(4,128)(2,1)}, bf16[8,2,2,4,256]{4,3,2,1,0:T(4,128)(2,1)}, u32[]{:S(2)}, u32[]{:S(2)}) collective-permute-start(bf16[8,2,2,4,256]{4,3,2,1,0:T(4,128)(2,1)} %maximum_select_fusion.3), channel_id=1, source_target_pairs={{0,8},{8,0},{16,24},{24,16},{32,40},{40,32},{48,56},{56,48},{64,72... | collective-permute-start | bytes 196616 | tf_op jit(solution)/shard_map/ppermute | solution.py:116
  81.1 10.8 %collective-permute-start.8 = (bf16[16,2,2,4,256]{4,3,2,1,0:T(4,128)(2,1)}, bf16[16,2,2,4,256]{4,3,2,1,0:T(4,128)(2,1)}, u32[]{:S(2)}, u32[]{:S(2)}) collective-permute-start(bf16[16,2,2,4,256]{4,3,2,1,0:T(4,128)(2,1)} %maximum_select_fusion.2), channel_id=1, source_target_pairs={{0,256},{8,264},{16,272},{24,280},{32,288},{40,296},{48,304},{56,3... | collective-permute-start | bytes 393224 | tf_op jit(solution)/shard_map/ppermute | solution.py:116
  88.3 10.5 %collective-permute-start.1 = (f32[304,128]{1,0:T(8,128)}, f32[304,128]{1,0:T(8,128)}, u32[]{:S(2)}, u32[]{:S(2)}) collective-permute-start(f32[304,128]{1,0:T(8,128)} %pad_maximum_fusion.5), channel_id=1, source_target_pairs={{8,0},{16,8},{24,16},{32,24},{40,32},{48,40},{56,48},{64,56},{72,6... | collective-permute-start | bytes 466952 | tf_op jit(solution)/shard_map/ppermute | solution.py:86
  93.3 9.4 %collective-permute-start.9 = (bf16[32,2,2,4,256]{4,3,2,1,0:T(4,128)(2,1)S(1)}, bf16[32,2,2,4,256]{4,3,2,1,0:T(4,128)(2,1)S(1)}, u32[]{:S(2)}, u32[]{:S(2)}) collective-permute-start(bf16[32,2,2,4,256]{4,3,2,1,0:T(4,128)(2,1)S(1)} %maximum_select_fusion.1), channel_id=1, source_target_pairs={{0,128},{8,136},{16,144},{24,152},{32,160},{40,168},{48,176},{56,1... | collective-permute-start | bytes 786440 | tf_op jit(solution)/shard_map/ppermute | solution.py:116
  106.2 26.9 %copy-start.20 = (f32[4,4,256]{2,1,0:T(4,128)S(1)}, f32[4,4,256]{2,1,0:T(4,128)}, u32[]{:S(2)}) copy-start(f32[4,4,256]{2,1,0:T(4,128)} %copy-done.19) | copy-start | bytes 49156
  106.2 26.9 %copy-start.22 = (f32[4,4,256]{2,1,0:T(4,128)S(1)}, f32[4,4,256]{2,1,0:T(4,128)}, u32[]{:S(2)}) copy-start(f32[4,4,256]{2,1,0:T(4,128)} %copy-done.21) | copy-start | bytes 49156
  106.2 6.6 %collective-permute-start.10 = (f32[2,2,2,2,4,256]{5,4,2,3,1,0:T(4,128)S(1)}, f32[2,2,2,2,4,256]{5,4,2,3,1,0:T(4,128)S(1)}, u32[]{:S(2)}, u32[]{:S(2)}) collective-permute-start(f32[2,2,2,2,4,256]{5,4,2,3,1,0:T(4,128)S(1)} %bitcast.387), channel_id=1, source_target_pairs={{0,4},{1,5},{2,6},{3,7},{4,0},{5,1},{6,2},{7,3},{8,12},{9,13},{10,... | collective-permute-start | bytes 196616 | tf_op jit(solution)/shard_map/ppermute | solution.py:143
  112.9 4.7 %collective-permute-start.11 = (f32[2,2,2,4,256]{4,3,1,2,0:T(4,128)S(1)}, f32[2,2,2,4,256]{4,3,1,2,0:T(4,128)S(1)}, u32[]{:S(2)}, u32[]{:S(2)}) collective-permute-start(f32[2,2,2,4,256]{4,3,1,2,0:T(4,128)S(1)} %select_bitcast_fusion), channel_id=1, source_target_pairs={{0,2},{1,3},{2,0},{3,1},{4,6},{5,7},{6,4},{7,5},{8,10},{9,11},{10,... | collective-permute-start | bytes 98312 | tf_op jit(solution)/shard_map/ppermute | solution.py:143
  117.6 15.5 %collective-permute-start.12 = (f32[2,2,4,256]{3,2,0,1:T(4,128)S(1)}, f32[2,2,4,256]{3,2,0,1:T(4,128)S(1)}, u32[]{:S(2)}, u32[]{:S(2)}) collective-permute-start(f32[2,2,4,256]{3,2,0,1:T(4,128)S(1)} %select_bitcast_fusion.1), channel_id=1, source_target_pairs={{0,1},{1,0},{2,3},{3,2},{4,5},{5,4},{6,7},{7,6},{8,9},{9,8},{10,11... | collective-permute-start | bytes 49160 | tf_op jit(solution)/shard_map/ppermute | solution.py:143
  127.9 13.8 %copy-start.6 = (bf16[2,128,128,1,1]{2,1,4,3,0:T(8,128)(2,1)S(1)}, bf16[2,128,128,1,1]{2,1,4,3,0:T(8,128)(2,1)}, u32[]{:S(2)}) copy-start(bf16[2,128,128,1,1]{2,1,4,3,0:T(8,128)(2,1)} %copy-done.5) | copy-start | bytes 196612
  127.9 8.1 %collective-permute-start.2 = (f32[800,128]{1,0:T(8,128)S(1)}, f32[800,128]{1,0:T(8,128)S(1)}, u32[]{:S(2)}, u32[]{:S(2)}) collective-permute-start(f32[800,128]{1,0:T(8,128)S(1)} %get-tuple-element.216), channel_id=1, source_target_pairs={{0,1},{1,2},{2,3},{3,4},{4,5},{5,6},{6,7},{8,9},{9,10},{10,11},{11... | collective-permute-start | bytes 1228808 | tf_op jit(solution)/shard_map/ppermute | solution.py:85
  131.2 9.3 %collective-permute-start.3 = (f32[800,128]{1,0:T(8,128)S(1)}, f32[800,128]{1,0:T(8,128)S(1)}, u32[]{:S(2)}, u32[]{:S(2)}) collective-permute-start(f32[800,128]{1,0:T(8,128)S(1)} %get-tuple-element.217), channel_id=1, source_target_pairs={{1,0},{2,1},{3,2},{4,3},{5,4},{6,5},{7,6},{9,8},{10,9},{11,10},{12... | collective-permute-start | bytes 1228808 | tf_op jit(solution)/shard_map/ppermute | solution.py:86
  (28 other events, 65.0 us)
